TPU v7x, 512 devices: a whole 4x8x8 slice. The times are simulated.
512 devices in a mesh: tm: 64 (over z, x, y_hi), chan: 8 (over y_lo, core).
Axes of the slice: x: 4, y: 8 (y_hi: 2, y_lo: 4; y = y_hi * 4 + y_lo), z: 8, core: 2. Of those that a mesh axis runs over, the one named last changes fastest.
Arguments:
- field: float32 [2, 2, 64, 65536], P(None, None, 'chan', 'tm'), may hold values from -15.5 to 15.5
- noise: float32 [1, 2, 2, 64, 65536], P(None, None, None, 'chan', 'tm'), may hold values from -1.25 to 1.25
- assign: int32 [64], P('chan'), may hold values from 0 to 63, each once
Outputs:
- received: float32 [2, 2, 64, 65536], P(None, None, 'chan', 'tm')
- recovered: float32 [2, 2, 64, 65536], P(None, None, 'chan', 'tm')
All inputs are finite; a program needn't handle non-finite values.
Results may differ from a plain program's by a relative error of at most 0.0003.
Values sent between devices are 32-bit elements; how exact they have to be, the bound alone decides.
No kernel may reach another device: no remote copies, remote signals or barrier semaphores. Data moves between devices by JAX's collectives and lax.ppermute only.
A program may use at most 64 MiB of HBM per device.

v0:
```python
import jax
import jax.numpy as jnp
from jax import lax
from jax.sharding import Mesh, PartitionSpec as P

OPTICAL_CHANNELS = 64
FILTER_HALF_TAPS = 128
STEPS = 2
FIBER_SECTIONS = 1


ATT = 0.955
GAMMA = 0.004
WALK = 0.5
SPREAD = 0.4
CHIRP = 0.25
EPS = 1e-06


def padded(array, sides, width):
    for axis, dim in sides:
        count, length = (lax.axis_size(axis), array.shape[dim])
        up = [(i, (i + 1) % count) for i in range(count)]
        down = [(j, i) for i, j in up]
        last = lax.slice_in_dim(array, length - width, length, axis=dim)
        leading = lax.slice_in_dim(array, 0, width, axis=dim)
        before = lax.ppermute(last, axis, up)
        after = lax.ppermute(leading, axis, down)
        array = jnp.concatenate([before, array, after], axis=dim)
    return array


def tap_tables(channel_ids, sign, reach, channels):
    rows = jnp.arange(3 * reach, dtype=jnp.int32)[:, None]
    cols = jnp.arange(reach, dtype=jnp.int32)[None, :]
    lag = cols - rows + reach
    interior_part = (jnp.abs(lag) <= reach).astype(jnp.float32)
    centre = (
        WALK * reach * (2.0 * channel_ids.astype(jnp.float32) - (channels - 1)) / (channels - 1)
    )
    centre = centre[:, None, None]
    width = SPREAD * reach
    offset = sign * lag.astype(jnp.float32)[None] - centre
    symbol_profile = jnp.exp(-jnp.square(offset / width))
    turn = jnp.square(offset) / (2.0 * CHIRP * reach)
    taps = jnp.arange(-reach, reach + 1, dtype=jnp.int32).astype(jnp.float32)
    scale = jnp.sqrt(
        jnp.sum(jnp.exp(-2.0 * jnp.square((taps[None, :] - centre[:, :, 0]) / width)), axis=1)
    )
    scale = scale[:, None, None]
    mat_re = interior_part * symbol_profile * jnp.cos(turn) / scale
    mat_im = sign * interior_part * symbol_profile * jnp.sin(turn) / scale
    return (mat_re, mat_im)


def merged_table(mat_re, mat_im):
    top = jnp.concatenate([mat_re, mat_im], axis=2)
    bottom = jnp.concatenate([-mat_im, mat_re], axis=2)
    return jnp.concatenate([top, bottom], axis=1)


def disperse(ext, table, reach):
    pols, parts, chans, segment_length = ext.shape
    blocks = segment_length // reach - 2
    rows = ext.reshape(pols, parts, chans, blocks + 2, reach)
    window = jnp.concatenate(
        [rows[:, :, :, 0:blocks], rows[:, :, :, 1 : blocks + 1], rows[:, :, :, 2 : blocks + 2]],
        axis=4,
    )
    stacked = jnp.moveaxis(window, 1, 3).reshape(pols, chans, blocks, parts * 3 * reach)
    out = jnp.einsum("pcjq,cqn->pcjn", stacked, table, precision=lax.Precision.HIGHEST)
    out = jnp.moveaxis(out.reshape(pols, chans, blocks, parts, reach), 3, 1)
    return out.reshape(pols, parts, chans, blocks * reach)


def rotate(ext, sign, own, total):
    angle = sign * GAMMA * (2.0 * total[None, :] - own)
    cosine = jnp.cos(angle)
    sine = jnp.sin(angle)
    real = ext[:, 0]
    imag = ext[:, 1]
    return jnp.stack([real * cosine - imag * sine, real * sine + imag * cosine], axis=1)


TM = ("z", "x", "yh")
CHAN = ("ylo", "core")


def psum_tm(value):
    for axis in ("yh", "x", "z"):
        value = lax.psum(value, axis)
    return value


def psum_chan(value):
    for axis in ("core", "ylo"):
        value = lax.psum(value, axis)
    return value


def on_device(field, noise, assign):
    forward, backward = lax.optimization_barrier(
        (
            merged_table(*tap_tables(assign, 1.0, FILTER_HALF_TAPS, OPTICAL_CHANNELS)),
            merged_table(*tap_tables(assign, -1.0, FILTER_HALF_TAPS, OPTICAL_CHANNELS)),
        )
    )
    total_len = lax.axis_size(TM) * field.shape[3]
    depth = 1
    counts = [min(depth, STEPS - start) for start in range(0, STEPS, depth)]

    def widen(current, count):
        return padded(current, ((TM, 3),), count * FILTER_HALF_TAPS)

    def nonlinear(ext, sign):
        own = jnp.sum(jnp.square(ext), axis=(0, 1))
        total = psum_chan(jnp.sum(own, axis=0))
        return rotate(ext, sign, own, total)

    def channel_power(current):
        summed = psum_tm(jnp.sum(jnp.square(current), axis=(0, 1, 3)))
        return summed / total_len

    current = field
    forward_current = current
    for count in counts:
        ext = widen(forward_current, count)
        ext = disperse(ext, forward, FILTER_HALF_TAPS) * ATT
        ext = nonlinear(ext, 1.0)
        forward_current = ext
    current = forward_current
    last_noise = noise[FIBER_SECTIONS - 1]
    gain = lax.rsqrt(channel_power(current) + EPS)
    received = current * gain[None, None, :, None] + last_noise
    arrival = channel_power(received)
    current = received
    rescale = jnp.sqrt(ATT ** (2 * STEPS) / (arrival + EPS))
    current = current * rescale[None, None, :, None]
    backward_current = current
    for count in counts:
        ext = widen(backward_current, count)
        ext = nonlinear(ext, -1.0) / ATT
        ext = disperse(ext, backward, FILTER_HALF_TAPS)
        backward_current = ext
    current = backward_current
    return (received, current)


def solution(mesh):
    tm, chan = mesh.shape["tm"], mesh.shape["chan"]
    fine = Mesh(mesh.devices.reshape(tm // 16, 8, 2, chan // 2, 2), TM + CHAN)
    placed = (P(None, None, CHAN, TM), P(None, None, None, CHAN, TM), P(CHAN))
    return jax.shard_map(
        on_device,
        mesh=fine,
        in_specs=placed,
        out_specs=(P(None, None, CHAN, TM), P(None, None, CHAN, TM)),
        check_vma=False,
    )
```

profile of v0, /device:TPU:1, one launch (start us, length us, event | category | flops | bytes accessed | tf_op | source)
XLA Modules:
  0.0 230.6 jit_solution(6730102665136638164)
XLA Ops:
  1.4 8.3 %collective-permute-start = (f32[2,2,8,128]{3,2,1,0:T(8,128)S(1)}, f32[2,2,8,128]{3,2,1,0:T(8,128)S(1)}, u32[]{:S(2)}, u32[]{:S(2)}) collective-permute-start(f32[2,2,8,128]{3,2,1,0:T(8,128)S(1)} %get-tuple-element.53), channel_id=1, source_target_pairs={{0,8},{8,16},{16,24},{24,32},{32,40},{40,48},{48,56},{56,64},{64,7... | collective-permute-start | bytes 49160 | tf_op jit(solution)/shard_map/ppermute | solution.py:27
  9.6 12.6 %collective-permute-start.1 = (f32[2,2,8,128]{3,2,1,0:T(8,128)S(1)}, f32[2,2,8,128]{3,2,1,0:T(8,128)S(1)}, u32[]{:S(2)}, u32[]{:S(2)}) collective-permute-start(f32[2,2,8,128]{3,2,1,0:T(8,128)S(1)} %get-tuple-element.54), channel_id=1, source_target_pairs={{8,0},{16,8},{24,16},{32,24},{40,32},{48,40},{56,48},{64,56},{72,6... | collective-permute-start | bytes 49160 | tf_op jit(solution)/shard_map/ppermute | solution.py:28
  23.3 12.3 %fusion.27 = (f32[8,384,128]{2,1,0:T(8,128)S(1)}, f32[8,384,128]{2,1,0:T(8,128)S(1)}, f32[8,384,128]{2,1,0:T(8,128)S(1)}, f32[8,384,128]{2,1,0:T(8,128)S(1)}, f3...) fusion(f32[384,128]{1,0:T(8,128)S(1)} %fusion.50, f32[384,128]{1,0:T(8,128)S(1)} %broadcast_multiply_fusion, ...), kind=kLoop, calls=%fused_computation.33 | loop fusion | flops 9830400 | bytes 10223680 | tf_op jit(solution)/shard_map/div | solution.py:52
  45.5 7.2 %psum.99 = f32[1024]{0:T(1024)S(1)} all-reduce(f32[1024]{0:T(1024)S(1)} %psum.98), channel_id=1, replica_groups=mesh['z'=4,'x'=8,'yh'=2,'ylo'=4,'core'=2] {'ylo'}, use_global_device_ids=true, to_apply=%region_4.0 | all-reduce | flops 1024 | bytes 8192 | tf_op jit(solution)/shard_map/psum | solution.py:97
  54.9 11.7 %collective-permute-start.3 = (f32[2,2,8,128]{3,2,1,0:T(8,128)S(1)}, f32[2,2,8,128]{3,2,1,0:T(8,128)S(1)}, u32[]{:S(2)}, u32[]{:S(2)}) collective-permute-start(f32[2,2,8,128]{3,2,1,0:T(8,128)S(1)} %get-tuple-element.52), channel_id=1, source_target_pairs={{8,0},{16,8},{24,16},{32,24},{40,32},{48,40},{56,48},{64,56},{72,6... | collective-permute-start | bytes 49160 | tf_op jit(solution)/shard_map/ppermute | solution.py:28
  67.5 5.5 %fusion.49 = (f32[8,256]{1,0:T(8,128)S(1)}, f32[8,8,256]{2,1,0:T(8,128)S(1)}, f32[8,256,2,8]{1,3,2,0:T(8,128)S(1)}) fusion(f32[2,8,8,768]{3,2,0,1:T(8,128)S(1)} %bitcast.130, f32[8,768,256]{2,1,0:T(8,128)} %copy-done), kind=kOutput, calls=%fused_computation.73 | convolution fusion | flops 302102528 | bytes 6889472 | tf_op jit(solution)/shard_map/pcjq,cqn->pcjn/dot_general | solution.py:71
  73.0 5.6 %psum.100 = f32[1024]{0:T(1024)S(1)} all-reduce(f32[1024]{0:T(1024)S(1)} %bitcast.143), channel_id=1, replica_groups=mesh['z'=4,'x'=8,'yh'=2,'ylo'=4,'core'=2] {'core'}, use_global_device_ids=true, to_apply=%region_9.0 | all-reduce | flops 1024 | bytes 8192 | tf_op jit(solution)/shard_map/psum | solution.py:97
  78.6 7.4 %psum.101 = f32[1024]{0:T(1024)S(1)} all-reduce(f32[1024]{0:T(1024)S(1)} %psum.100), channel_id=1, replica_groups=mesh['z'=4,'x'=8,'yh'=2,'ylo'=4,'core'=2] {'ylo'}, use_global_device_ids=true, to_apply=%region_10.0 | all-reduce | flops 1024 | bytes 8192 | tf_op jit(solution)/shard_map/psum | solution.py:97
  86.5 7.7 %psum.102 = f32[8]{0:T(128)S(1)} all-reduce(f32[8]{0:T(128)S(1)} %multiply_reduce_fusion.5), channel_id=1, replica_groups=mesh['z'=4,'x'=8,'yh'=2,'ylo'=4,'core'=2] {'yh'}, use_global_device_ids=true, to_apply=%region_14.0 | all-reduce | flops 8 | bytes 64 | tf_op jit(solution)/shard_map/psum | solution.py:91
  94.1 12.5 %psum.103 = f32[8]{0:T(128)S(1)} all-reduce(f32[8]{0:T(128)S(1)} %psum.102), channel_id=1, replica_groups=mesh['z'=4,'x'=8,'yh'=2,'ylo'=4,'core'=2] {'x'}, use_global_device_ids=true, to_apply=%region_15.0 | all-reduce | flops 8 | bytes 64 | tf_op jit(solution)/shard_map/psum | solution.py:91
  106.7 14.0 %psum.104 = f32[8]{0:T(128)S(1)} all-reduce(f32[8]{0:T(128)S(1)} %psum.103), channel_id=1, replica_groups=mesh['z'=4,'x'=8,'yh'=2,'ylo'=4,'core'=2] {'z'}, use_global_device_ids=true, to_apply=%region_16.0 | all-reduce | flops 8 | bytes 64 | tf_op jit(solution)/shard_map/psum | solution.py:91
  120.9 7.8 %psum.105 = f32[8]{0:T(128)S(1)} all-reduce(f32[8]{0:T(128)S(1)} %get-tuple-element.14), channel_id=1, replica_groups=mesh['z'=4,'x'=8,'yh'=2,'ylo'=4,'core'=2] {'yh'}, use_global_device_ids=true, to_apply=%region_18.0 | all-reduce | flops 8 | bytes 64 | tf_op jit(solution)/shard_map/psum | solution.py:91
  128.7 12.5 %psum.106 = f32[8]{0:T(128)S(1)} all-reduce(f32[8]{0:T(128)S(1)} %psum.105), channel_id=1, replica_groups=mesh['z'=4,'x'=8,'yh'=2,'ylo'=4,'core'=2] {'x'}, use_global_device_ids=true, to_apply=%region_19.0 | all-reduce | flops 8 | bytes 64 | tf_op jit(solution)/shard_map/psum | solution.py:91
  141.2 7.1 %psum.107 = f32[8]{0:T(128)S(1)} all-reduce(f32[8]{0:T(128)S(1)} %psum.106), channel_id=1, replica_groups=mesh['z'=4,'x'=8,'yh'=2,'ylo'=4,'core'=2] {'z'}, use_global_device_ids=true, to_apply=%region_20.0 | all-reduce | flops 8 | bytes 64 | tf_op jit(solution)/shard_map/psum | solution.py:91
  148.4 7.3 %collective-permute-start.4 = (f32[2,2,8,128]{3,2,1,0:T(8,128)S(1)}, f32[2,2,8,128]{3,2,1,0:T(8,128)S(1)}, u32[]{:S(2)}, u32[]{:S(2)}) collective-permute-start(f32[2,2,8,128]{3,2,1,0:T(8,128)S(1)} %get-tuple-element.49), channel_id=1, source_target_pairs={{0,8},{8,16},{16,24},{24,32},{32,40},{40,48},{48,56},{56,64},{64,7... | collective-permute-start | bytes 49160 | tf_op jit(solution)/shard_map/ppermute | solution.py:27
  155.7 6.1 %collective-permute-start.5 = (f32[2,2,8,128]{3,2,1,0:T(8,128)S(1)}, f32[2,2,8,128]{3,2,1,0:T(8,128)S(1)}, u32[]{:S(2)}, u32[]{:S(2)}) collective-permute-start(f32[2,2,8,128]{3,2,1,0:T(8,128)S(1)} %get-tuple-element.50), channel_id=1, source_target_pairs={{8,0},{16,8},{24,16},{32,24},{40,32},{48,40},{56,48},{64,56},{72,6... | collective-permute-start | bytes 49160 | tf_op jit(solution)/shard_map/ppermute | solution.py:28
  164.1 18.6 %psum.108 = f32[1280]{0:T(1024)S(1)} all-reduce(f32[1280]{0:T(1024)S(1)} %get-tuple-element.8), channel_id=1, replica_groups=mesh['z'=4,'x'=8,'yh'=2,'ylo'=4,'core'=2] {'core'}, use_global_device_ids=true, to_apply=%region_22.0 | all-reduce | flops 1280 | bytes 10240 | tf_op jit(solution)/shard_map/psum | solution.py:97
  182.8 8.6 %psum.109 = f32[1280]{0:T(1024)S(1)} all-reduce(f32[1280]{0:T(1024)S(1)} %psum.108), channel_id=1, replica_groups=mesh['z'=4,'x'=8,'yh'=2,'ylo'=4,'core'=2] {'ylo'}, use_global_device_ids=true, to_apply=%region_23.0 | all-reduce | flops 1280 | bytes 10240 | tf_op jit(solution)/shard_map/psum | solution.py:97
  191.8 5.4 %fusion.37 = f32[2,2,8,8,128]{4,3,1,0,2:T(8,128)S(1)} fusion(f32[2,8,8,768]{3,2,0,1:T(8,128)S(1)} %bitcast.131, f32[8,768,256]{2,1,0:T(8,128)} %get-tuple-element.5), kind=kOutput, calls=%fused_computation.39 | convolution fusion | flops 301989888 | bytes 6815744 | tf_op jit(solution)/shard_map/pcjq,cqn->pcjn/dot_general | solution.py:71
  197.3 3.9 %collective-permute-start.6 = (f32[2,2,8,128]{3,2,0,1:T(8,128)S(1)}, f32[2,2,8,128]{3,2,0,1:T(8,128)S(1)}, u32[]{:S(2)}, u32[]{:S(2)}) collective-permute-start(f32[2,2,8,128]{3,2,0,1:T(8,128)S(1)} %get-tuple-element.47), channel_id=1, source_target_pairs={{0,8},{8,16},{16,24},{24,32},{32,40},{40,48},{48,56},{56,64},{64,7... | collective-permute-start | bytes 49160 | tf_op jit(solution)/shard_map/ppermute | solution.py:27
  201.3 9.5 %collective-permute-start.7 = (f32[2,2,8,128]{3,2,0,1:T(8,128)S(1)}, f32[2,2,8,128]{3,2,0,1:T(8,128)S(1)}, u32[]{:S(2)}, u32[]{:S(2)}) collective-permute-start(f32[2,2,8,128]{3,2,0,1:T(8,128)S(1)} %get-tuple-element.48), channel_id=1, source_target_pairs={{8,0},{16,8},{24,16},{32,24},{40,32},{48,40},{56,48},{64,56},{72,6... | collective-permute-start | bytes 49160 | tf_op jit(solution)/shard_map/ppermute | solution.py:28
  211.6 5.7 %psum.110 = f32[1280]{0:T(1024)S(1)} all-reduce(f32[1280]{0:T(1024)S(1)} %get-tuple-element.6), channel_id=1, replica_groups=mesh['z'=4,'x'=8,'yh'=2,'ylo'=4,'core'=2] {'core'}, use_global_device_ids=true, to_apply=%region_26.27 | all-reduce | flops 1280 | bytes 10240 | tf_op jit(solution)/shard_map/psum | solution.py:97
  217.3 6.8 %psum.111 = f32[1280]{0:T(1024)S(1)} all-reduce(f32[1280]{0:T(1024)S(1)} %psum.110), channel_id=1, replica_groups=mesh['z'=4,'x'=8,'yh'=2,'ylo'=4,'core'=2] {'ylo'}, use_global_device_ids=true, to_apply=%region_27.28 | all-reduce | flops 1280 | bytes 10240 | tf_op jit(solution)/shard_map/psum | solution.py:97
  224.4 5.4 %fusion.40 = f32[2,2,8,8,128]{4,3,1,0,2:T(8,128)S(1)} fusion(f32[2,8,8,768]{3,2,0,1:T(8,128)S(1)} %bitcast.132, f32[8,768,256]{2,1,0:T(8,128)} %get-tuple-element.5), kind=kOutput, calls=%fused_computation.40 | convolution fusion | flops 301989888 | bytes 6815744 | tf_op jit(solution)/shard_map/pcjq,cqn->pcjn/dot_general | solution.py:71
  (77 shorter events, 20.0 us)
Async XLA Ops:
  1.4 37.4 %collective-permute-start = (f32[2,2,8,128]{3,2,1,0:T(8,128)S(1)}, f32[2,2,8,128]{3,2,1,0:T(8,128)S(1)}, u32[]{:S(2)}, u32[]{:S(2)}) collective-permute-start(f32[2,2,8,128]{3,2,1,0:T(8,128)S(1)} %get-tuple-element.53), channel_id=1, source_target_pairs={{0,8},{8,16},{16,24},{24,32},{32,40},{40,48},{48,56},{56,64},{64,7... | collective-permute-start | bytes 49160 | tf_op jit(solution)/shard_map/ppermute | solution.py:27
  9.6 29.1 %collective-permute-start.1 = (f32[2,2,8,128]{3,2,1,0:T(8,128)S(1)}, f32[2,2,8,128]{3,2,1,0:T(8,128)S(1)}, u32[]{:S(2)}, u32[]{:S(2)}) collective-permute-start(f32[2,2,8,128]{3,2,1,0:T(8,128)S(1)} %get-tuple-element.54), channel_id=1, source_target_pairs={{8,0},{16,8},{24,16},{32,24},{40,32},{48,40},{56,48},{64,56},{72,6... | collective-permute-start | bytes 49160 | tf_op jit(solution)/shard_map/ppermute | solution.py:28
  35.6 3.1 %copy-start.2 = (f32[2,2,8,1024]{3,2,1,0:T(8,128)S(1)}, f32[2,2,8,1024]{3,2,1,0:T(8,128)}, u32[]{:S(2)}) copy-start(f32[2,2,8,1024]{3,2,1,0:T(8,128)} %param.3) | copy-start | bytes 393220
  38.7 3.6 %copy-start = (f32[8,768,256]{2,1,0:T(8,128)}, f32[8,768,256]{2,1,0:T(8,128)S(1)}, u32[]{:S(2)}) copy-start(f32[8,768,256]{2,1,0:T(8,128)S(1)} %get-tuple-element.4) | copy-start | bytes 18874372
  53.0 13.6 %collective-permute-start.2 = (f32[2,2,8,128]{3,2,1,0:T(8,128)S(1)}, f32[2,2,8,128]{3,2,1,0:T(8,128)S(1)}, u32[]{:S(2)}, u32[]{:S(2)}) collective-permute-start(f32[2,2,8,128]{3,2,1,0:T(8,128)S(1)} %get-tuple-element.51), channel_id=1, source_target_pairs={{0,8},{8,16},{16,24},{24,32},{32,40},{40,48},{48,56},{56,64},{64,7... | collective-permute-start | bytes 49160 | tf_op jit(solution)/shard_map/ppermute | solution.py:27
  54.9 12.3 %collective-permute-start.3 = (f32[2,2,8,128]{3,2,1,0:T(8,128)S(1)}, f32[2,2,8,128]{3,2,1,0:T(8,128)S(1)}, u32[]{:S(2)}, u32[]{:S(2)}) collective-permute-start(f32[2,2,8,128]{3,2,1,0:T(8,128)S(1)} %get-tuple-element.52), channel_id=1, source_target_pairs={{8,0},{16,8},{24,16},{32,24},{40,32},{48,40},{56,48},{64,56},{72,6... | collective-permute-start | bytes 49160 | tf_op jit(solution)/shard_map/ppermute | solution.py:28
  67.4 53.3 %copy-start.3 = (f32[1,2,2,8,1024]{4,3,2,1,0:T(8,128)S(1)}, f32[1,2,2,8,1024]{4,3,2,1,0:T(8,128)}, u32[]{:S(2)}) copy-start(f32[1,2,2,8,1024]{4,3,2,1,0:T(8,128)} %param.4) | copy-start | bytes 393220
  120.9 70.8 %copy-start.1 = (f32[2,2,8,1024]{3,2,1,0:T(8,128)}, f32[2,2,8,1024]{3,2,1,0:T(8,128)S(1)}, u32[]{:S(2)}) copy-start(f32[2,2,8,1024]{3,2,1,0:T(8,128)S(1)} %get-tuple-element.15) | copy-start | bytes 393220
  148.4 13.4 %collective-permute-start.4 = (f32[2,2,8,128]{3,2,1,0:T(8,128)S(1)}, f32[2,2,8,128]{3,2,1,0:T(8,128)S(1)}, u32[]{:S(2)}, u32[]{:S(2)}) collective-permute-start(f32[2,2,8,128]{3,2,1,0:T(8,128)S(1)} %get-tuple-element.49), channel_id=1, source_target_pairs={{0,8},{8,16},{16,24},{24,32},{32,40},{40,48},{48,56},{56,64},{64,7... | collective-permute-start | bytes 49160 | tf_op jit(solution)/shard_map/ppermute | solution.py:27
  155.7 8.4 %collective-permute-start.5 = (f32[2,2,8,128]{3,2,1,0:T(8,128)S(1)}, f32[2,2,8,128]{3,2,1,0:T(8,128)S(1)}, u32[]{:S(2)}, u32[]{:S(2)}) collective-permute-start(f32[2,2,8,128]{3,2,1,0:T(8,128)S(1)} %get-tuple-element.50), channel_id=1, source_target_pairs={{8,0},{16,8},{24,16},{32,24},{40,32},{48,40},{56,48},{64,56},{72,6... | collective-permute-start | bytes 49160 | tf_op jit(solution)/shard_map/ppermute | solution.py:28
  197.3 13.4 %collective-permute-start.6 = (f32[2,2,8,128]{3,2,0,1:T(8,128)S(1)}, f32[2,2,8,128]{3,2,0,1:T(8,128)S(1)}, u32[]{:S(2)}, u32[]{:S(2)}) collective-permute-start(f32[2,2,8,128]{3,2,0,1:T(8,128)S(1)} %get-tuple-element.47), channel_id=1, source_target_pairs={{0,8},{8,16},{16,24},{24,32},{32,40},{40,48},{48,56},{56,64},{64,7... | collective-permute-start | bytes 49160 | tf_op jit(solution)/shard_map/ppermute | solution.py:27
  201.3 10.3 %collective-permute-start.7 = (f32[2,2,8,128]{3,2,0,1:T(8,128)S(1)}, f32[2,2,8,128]{3,2,0,1:T(8,128)S(1)}, u32[]{:S(2)}, u32[]{:S(2)}) collective-permute-start(f32[2,2,8,128]{3,2,0,1:T(8,128)S(1)} %get-tuple-element.48), channel_id=1, source_target_pairs={{8,0},{16,8},{24,16},{32,24},{40,32},{48,40},{56,48},{64,56},{72,6... | collective-permute-start | bytes 49160 | tf_op jit(solution)/shard_map/ppermute | solution.py:28
where the time goes:
time: 233 us; the launch traced here: 231 us
  blocking collectives  125 us (54%)
  starting transfers between devices  61.3 us (26%)
  matrix products  19.8 us (8%)
  other arithmetic  17.9 us (8%)
  waiting for transfers between devices  3.79 us (2%)
    psum x8, blocking collectives, psum_chan(): value = lax.psum(value, axis)  63 us
    psum x6, blocking collectives, psum_tm(): value = lax.psum(value, axis)  61.6 us
    ppermute x4, starting transfers between devices, padded(): after = lax.ppermute(leading, axis, down)  39.8 us
    ppermute x4, starting transfers between devices, padded(): before = lax.ppermute(last, axis, up)  21.4 us
    dot_general x4, matrix products, disperse(): jnp.einsum('pcjq,cqn->pcjn', stacked, table, precision=lax.Precision.HIGH...  19.8 us
    div x1, other arithmetic, tap_tables(): mat_im = sign * interior_part * symbol_profile * jnp.sin(turn) / scale  12.3 us
  transfers between devices with their start and end apart: 8, of which 3 were waited for; matrix products, arithmetic and copies ran while one was open for 7% of the time, Pallas kernels for 0%

commit v1 on v0

--- a/solution.py
+++ b/solution.py
@@ -15,19 +15,6 @@
 SPREAD = 0.4
 CHIRP = 0.25
 EPS = 1e-06
-
-
-def padded(array, sides, width):
-    for axis, dim in sides:
-        count, length = (lax.axis_size(axis), array.shape[dim])
-        up = [(i, (i + 1) % count) for i in range(count)]
-        down = [(j, i) for i, j in up]
-        last = lax.slice_in_dim(array, length - width, length, axis=dim)
-        leading = lax.slice_in_dim(array, 0, width, axis=dim)
-        before = lax.ppermute(last, axis, up)
-        after = lax.ppermute(leading, axis, down)
-        array = jnp.concatenate([before, array, after], axis=dim)
-    return array
 
 
 def tap_tables(channel_ids, sign, reach, channels):
@@ -106,11 +93,9 @@
         )
     )
     total_len = lax.axis_size(TM) * field.shape[3]
-    depth = 1
-    counts = [min(depth, STEPS - start) for start in range(0, STEPS, depth)]
-
-    def widen(current, count):
-        return padded(current, ((TM, 3),), count * FILTER_HALF_TAPS)
+    reach = FILTER_HALF_TAPS
+    field_width = 2 * STEPS * reach
+    noise_width = STEPS * reach
 
     def nonlinear(ext, sign):
         own = jnp.sum(jnp.square(ext), axis=(0, 1))
@@ -121,28 +106,32 @@
         summed = psum_tm(jnp.sum(jnp.square(current), axis=(0, 1, 3)))
         return summed / total_len
 
-    current = field
-    forward_current = current
-    for count in counts:
-        ext = widen(forward_current, count)
-        ext = disperse(ext, forward, FILTER_HALF_TAPS) * ATT
-        ext = nonlinear(ext, 1.0)
-        forward_current = ext
-    current = forward_current
     last_noise = noise[FIBER_SECTIONS - 1]
-    gain = lax.rsqrt(channel_power(current) + EPS)
-    received = current * gain[None, None, :, None] + last_noise
+    count, length = lax.axis_size(TM), field.shape[3]
+    up = [(i, (i + 1) % count) for i in range(count)]
+    down = [(j, i) for i, j in up]
+    trailing = jnp.concatenate(
+        [field[..., length - field_width :], last_noise[..., length - noise_width :]], axis=3
+    )
+    leading = jnp.concatenate([field[..., :field_width], last_noise[..., :noise_width]], axis=3)
+    before = lax.ppermute(trailing, TM, up)
+    after = lax.ppermute(leading, TM, down)
+    current = jnp.concatenate([before[..., :field_width], field, after[..., :field_width]], axis=3)
+    noise_ext = jnp.concatenate([before[..., field_width:], last_noise, after[..., field_width:]], axis=3)
+
+    for step in range(STEPS):
+        current = disperse(current, forward, reach) * ATT
+        current = nonlinear(current, 1.0)
+    centre = slice(noise_width, noise_width + length)
+    gain = lax.rsqrt(channel_power(current[..., centre]) + EPS)
+    current = current * gain[None, None, :, None] + noise_ext
+    received = current[..., centre]
     arrival = channel_power(received)
-    current = received
     rescale = jnp.sqrt(ATT ** (2 * STEPS) / (arrival + EPS))
     current = current * rescale[None, None, :, None]
-    backward_current = current
-    for count in counts:
-        ext = widen(backward_current, count)
-        ext = nonlinear(ext, -1.0) / ATT
-        ext = disperse(ext, backward, FILTER_HALF_TAPS)
-        backward_current = ext
-    current = backward_current
+    for step in range(STEPS):
+        current = nonlinear(current, -1.0) / ATT
+        current = disperse(current, backward, reach)
     return (received, current)
 
 

time: 233 us -> 194 us (0.83)
  starting transfers between devices: 61.3 us -> 20.9 us
  blocking collectives: 125 us -> 121 us
  matrix products: 19.8 us -> 23.6 us
  waiting for transfers between devices: 3.79 us -> 0.01 us
  other arithmetic: 17.9 us -> 21.5 us
  local copies, waits for them, and re-layouts: 2.19 us -> 4.81 us
    ppermute x8 -> x2, starting transfers between devices: 61.3 us -> 20.9 us  [the longest x1 12.6 us: on_device(): after = lax.ppermute(leading, TM, down)]
    dot_general x4, matrix products: 19.8 us -> 23.6 us  [disperse(): jnp.einsum('pcjq,cqn->pcjn', stacked, table, precision=lax.Precision.HIGH...]
    ppermute x8 -> x2, waiting for transfers between devices: 3.79 us -> 0.01 us  [the longest x1 0.01 us: on_device(): before = lax.ppermute(trailing, TM, up)]
    psum x8, blocking collectives: 63 us -> 60.4 us  [psum_chan(): value = lax.psum(value, axis)]
  transfers between devices with their start and end apart: 8 -> 2, of which waited for: 3 -> 0; matrix products, arithmetic and copies ran while one was open for 7% -> 9% of each run, Pallas kernels for 0% -> 0%
where the time goes in v1:
time: 194 us; the launch traced here: 193 us
  blocking collectives  121 us (62%)
  matrix products  23.6 us (12%)
  other arithmetic  21.5 us (11%)
  starting transfers between devices  20.9 us (11%)
  local copies, waits for them, and re-layouts  4.81 us (2%)
    psum x8, blocking collectives, psum_chan(): value = lax.psum(value, axis)  60.4 us
    psum x6, blocking collectives, psum_tm(): value = lax.psum(value, axis)  60.3 us
    dot_general x4, matrix products, disperse(): jnp.einsum('pcjq,cqn->pcjn', stacked, table, precision=lax.Precision.HIGH...  23.6 us
    ppermute x1, starting transfers between devices, on_device(): after = lax.ppermute(leading, TM, down)  12.6 us
    div x1, other arithmetic, tap_tables(): mat_im = sign * interior_part * symbol_profile * jnp.sin(turn) / scale  12.3 us
    ppermute x1, starting transfers between devices, on_device(): before = lax.ppermute(trailing, TM, up)  8.27 us
    concatenate x1, other arithmetic, merged_table(): return jnp.concatenate([top, bottom], axis=1)  5.14 us
  transfers between devices with their start and end apart: 2, of which 0 were waited for; matrix products, arithmetic and copies ran while one was open for 9% of the time, Pallas kernels for 0%

profile of v1, /device:TPU:1, one launch (start us, length us, event | category | flops | bytes accessed | tf_op | source)
XLA Modules:
  0.0 192.6 jit_solution(15109144350219172534)
XLA Ops:
  0.6 0.8 fusion.81
  1.4 0.9 fusion.80
  2.3 8.3 %collective-permute-start = (f32[2,2,8,768]{3,2,1,0:T(8,128)S(1)}, f32[2,2,8,768]{3,2,1,0:T(8,128)S(1)}, u32[]{:S(2)}, u32[]{:S(2)}) collective-permute-start(f32[2,2,8,768]{3,2,1,0:T(8,128)S(1)} %pad_maximum_fusion.2), channel_id=1, source_target_pairs={{0,8},{8,16},{16,24},{24,32},{32,40},{40,48},{48,56},{56,64},{64,7... | collective-permute-start | bytes 294920 | tf_op jit(solution)/shard_map/ppermute | solution.py:117
  10.6 12.6 %collective-permute-start.1 = (f32[2,2,8,768]{3,2,1,0:T(8,128)S(1)}, f32[2,2,8,768]{3,2,1,0:T(8,128)S(1)}, u32[]{:S(2)}, u32[]{:S(2)}) collective-permute-start(f32[2,2,8,768]{3,2,1,0:T(8,128)S(1)} %pad_maximum_fusion.3), channel_id=1, source_target_pairs={{8,0},{16,8},{24,16},{32,24},{40,32},{48,40},{56,48},{64,56},{72,6... | collective-permute-start | bytes 294920 | tf_op jit(solution)/shard_map/ppermute | solution.py:118
  23.6 12.3 %fusion.27 = (f32[8,384,128]{2,1,0:T(8,128)S(1)}, f32[8,384,128]{2,1,0:T(8,128)S(1)}, f32[8,384,128]{2,1,0:T(8,128)S(1)}, f32[8,384,128]{2,1,0:T(8,128)S(1)}, f3...) fusion(f32[384,128]{1,0:T(8,128)S(1)} %fusion.64, f32[384,128]{1,0:T(8,128)S(1)} %broadcast_multiply_fusion.1, ...), kind=kLoop, calls=%fused_computation.33 | loop fusion | flops 9830400 | bytes 10223680 | tf_op jit(solution)/shard_map/div | solution.py:39
  36.0 5.1 %maximum_maximum_fusion = (f32[8,768,256]{2,1,0:T(8,128)}, f32[8,768,256]{2,1,0:T(8,128)}) fusion(f32[8,384,128]{2,1,0:T(8,128)S(1)} %get-tuple-element.37, f32[8,384,128]{2,1,0:T(8,128)S(1)} %get-tuple-element.38, f32[8,384,128]{2,1,0:T(8,128)S(1)} %get-tuple-element.39, f32[8,384,128]{2,1,0:T(8,128)S(1)} %get-tuple-element.36, ...), kind=kLoop, calls=%fused_computation | loop fusion | flops 9437184 | bytes 22020096 | tf_op jit(solution)/shard_map/concatenate | solution.py:46
  42.5 6.1 %multiply_reduce_fusion.3 = (f32[14,256]{1,0:T(8,128)S(1)}, f32[8,14,256]{2,1,0:T(8,128)S(1)}, f32[2,8,14,256]{3,2,0,1:T(8,128)S(1)}) fusion(f32[2,8,14,768]{3,1,2,0:T(8,128)S(1)} %reshape.291, f32[8,768,256]{2,1,0:T(8,128)} %get-tuple-element.4), kind=kOutput, calls=%fused_computation.56 | convolution fusion | flops 528679424 | bytes 7337984 | tf_op jit(solution)/shard_map/pcjq,cqn->pcjn/dot_general | solution.py:58
  48.7 3.1 %psum.98 = f32[1792]{0:T(1024)S(1)} all-reduce(f32[1792]{0:T(1024)S(1)} %bitcast.144), channel_id=1, replica_groups=mesh['z'=4,'x'=8,'yh'=2,'ylo'=4,'core'=2] {'core'}, use_global_device_ids=true, to_apply=%region_3.0 | all-reduce | flops 1792 | bytes 14336 | tf_op jit(solution)/shard_map/psum | solution.py:84
  51.8 7.6 %psum.99 = f32[1792]{0:T(1024)S(1)} all-reduce(f32[1792]{0:T(1024)S(1)} %psum.98), channel_id=1, replica_groups=mesh['z'=4,'x'=8,'yh'=2,'ylo'=4,'core'=2] {'ylo'}, use_global_device_ids=true, to_apply=%region_4.0 | all-reduce | flops 1792 | bytes 14336 | tf_op jit(solution)/shard_map/psum | solution.py:84
  60.9 6.1 %multiply_reduce_fusion.1 = (f32[12,256]{1,0:T(8,128)S(1)}, f32[8,12,256]{2,1,0:T(8,128)S(1)}, f32[2,8,12,256]{3,2,0,1:T(8,128)S(1)}) fusion(f32[2,8,12,768]{3,1,2,0:T(8,128)S(1)} %reshape.292, f32[8,768,256]{2,1,0:T(8,128)} %get-tuple-element.4), kind=kOutput, calls=%fused_computation.54 | convolution fusion | flops 453153792 | bytes 7188480 | tf_op jit(solution)/shard_map/pcjq,cqn->pcjn/dot_general | solution.py:58
  67.1 4.5 %psum.100 = f32[1536]{0:T(1024)S(1)} all-reduce(f32[1536]{0:T(1024)S(1)} %bitcast.145), channel_id=1, replica_groups=mesh['z'=4,'x'=8,'yh'=2,'ylo'=4,'core'=2] {'core'}, use_global_device_ids=true, to_apply=%region_9.0 | all-reduce | flops 1536 | bytes 12288 | tf_op jit(solution)/shard_map/psum | solution.py:84
  71.6 7.6 %psum.101 = f32[1536]{0:T(1024)S(1)} all-reduce(f32[1536]{0:T(1024)S(1)} %psum.100), channel_id=1, replica_groups=mesh['z'=4,'x'=8,'yh'=2,'ylo'=4,'core'=2] {'ylo'}, use_global_device_ids=true, to_apply=%region_10.0 | all-reduce | flops 1536 | bytes 12288 | tf_op jit(solution)/shard_map/psum | solution.py:84
  79.7 7.7 %psum.102 = f32[8]{0:T(128)S(1)} all-reduce(f32[8]{0:T(128)S(1)} %fusion.61), channel_id=1, replica_groups=mesh['z'=4,'x'=8,'yh'=2,'ylo'=4,'core'=2] {'yh'}, use_global_device_ids=true, to_apply=%region_14.0 | all-reduce | flops 8 | bytes 64 | tf_op jit(solution)/shard_map/psum | solution.py:78
  87.4 12.5 %psum.103 = f32[8]{0:T(128)S(1)} all-reduce(f32[8]{0:T(128)S(1)} %psum.102), channel_id=1, replica_groups=mesh['z'=4,'x'=8,'yh'=2,'ylo'=4,'core'=2] {'x'}, use_global_device_ids=true, to_apply=%region_15.0 | all-reduce | flops 8 | bytes 64 | tf_op jit(solution)/shard_map/psum | solution.py:78
  99.9 11.2 %psum.104 = f32[8]{0:T(128)S(1)} all-reduce(f32[8]{0:T(128)S(1)} %psum.103), channel_id=1, replica_groups=mesh['z'=4,'x'=8,'yh'=2,'ylo'=4,'core'=2] {'z'}, use_global_device_ids=true, to_apply=%region_16.0 | all-reduce | flops 8 | bytes 64 | tf_op jit(solution)/shard_map/psum | solution.py:78
  112.0 7.7 %psum.105 = f32[8]{0:T(128)S(1)} all-reduce(f32[8]{0:T(128)S(1)} %get-tuple-element.16), channel_id=1, replica_groups=mesh['z'=4,'x'=8,'yh'=2,'ylo'=4,'core'=2] {'yh'}, use_global_device_ids=true, to_apply=%region_18.0 | all-reduce | flops 8 | bytes 64 | tf_op jit(solution)/shard_map/psum | solution.py:78
  119.7 13.0 %psum.106 = f32[8]{0:T(128)S(1)} all-reduce(f32[8]{0:T(128)S(1)} %psum.105), channel_id=1, replica_groups=mesh['z'=4,'x'=8,'yh'=2,'ylo'=4,'core'=2] {'x'}, use_global_device_ids=true, to_apply=%region_19.0 | all-reduce | flops 8 | bytes 64 | tf_op jit(solution)/shard_map/psum | solution.py:78
  132.7 8.2 %psum.107 = f32[8]{0:T(128)S(1)} all-reduce(f32[8]{0:T(128)S(1)} %psum.106), channel_id=1, replica_groups=mesh['z'=4,'x'=8,'yh'=2,'ylo'=4,'core'=2] {'z'}, use_global_device_ids=true, to_apply=%region_20.0 | all-reduce | flops 8 | bytes 64 | tf_op jit(solution)/shard_map/psum | solution.py:78
  141.0 17.8 %psum.108 = f32[1536]{0:T(1024)S(1)} all-reduce(f32[1536]{0:T(1024)S(1)} %get-tuple-element.10), channel_id=1, replica_groups=mesh['z'=4,'x'=8,'yh'=2,'ylo'=4,'core'=2] {'core'}, use_global_device_ids=true, to_apply=%region_22.0 | all-reduce | flops 1536 | bytes 12288 | tf_op jit(solution)/shard_map/psum | solution.py:84
  158.8 8.5 %psum.109 = f32[1536]{0:T(1024)S(1)} all-reduce(f32[1536]{0:T(1024)S(1)} %psum.108), channel_id=1, replica_groups=mesh['z'=4,'x'=8,'yh'=2,'ylo'=4,'core'=2] {'ylo'}, use_global_device_ids=true, to_apply=%region_23.0 | all-reduce | flops 1536 | bytes 12288 | tf_op jit(solution)/shard_map/psum | solution.py:84
  168.6 6.0 %fusion.43 = f32[2,8,10,256]{3,2,0,1:T(8,128)S(1)} fusion(f32[8,768,256]{2,1,0:T(8,128)} %get-tuple-element.5, f32[2,8,10,768]{3,1,2,0:T(8,128)S(1)} %reshape.293), kind=kOutput, calls=%fused_computation.41 | convolution fusion | flops 377487360 | bytes 6946816 | tf_op jit(solution)/shard_map/pcjq,cqn->pcjn/dot_general | solution.py:58
  174.7 4.5 %psum.110 = f32[1280]{0:T(1024)S(1)} all-reduce(f32[1280]{0:T(1024)S(1)} %bitcast.146), channel_id=1, replica_groups=mesh['z'=4,'x'=8,'yh'=2,'ylo'=4,'core'=2] {'core'}, use_global_device_ids=true, to_apply=%region_26.27 | all-reduce | flops 1280 | bytes 10240 | tf_op jit(solution)/shard_map/psum | solution.py:84
  179.2 6.8 %psum.111 = f32[1280]{0:T(1024)S(1)} all-reduce(f32[1280]{0:T(1024)S(1)} %psum.110), channel_id=1, replica_groups=mesh['z'=4,'x'=8,'yh'=2,'ylo'=4,'core'=2] {'ylo'}, use_global_device_ids=true, to_apply=%region_27.28 | all-reduce | flops 1280 | bytes 10240 | tf_op jit(solution)/shard_map/psum | solution.py:84
  186.4 5.4 %fusion.46 = f32[2,2,8,8,128]{4,3,1,0,2:T(8,128)S(1)} fusion(f32[2,8,8,768]{3,2,0,1:T(8,128)S(1)} %bitcast.133, f32[8,768,256]{2,1,0:T(8,128)} %get-tuple-element.5), kind=kOutput, calls=%fused_computation.42 | convolution fusion | flops 301989888 | bytes 6815744 | tf_op jit(solution)/shard_map/pcjq,cqn->pcjn/dot_general | solution.py:58
  (69 shorter events, 7.2 us)
Async XLA Ops:
  0.6 22.8 %copy-start.2 = (s32[8]{0:T(128)S(1)}, s32[8]{0:T(128)}, u32[]{:S(2)}) copy-start(s32[8]{0:T(128)} %param.5) | copy-start | bytes 100
  2.3 38.8 %collective-permute-start = (f32[2,2,8,768]{3,2,1,0:T(8,128)S(1)}, f32[2,2,8,768]{3,2,1,0:T(8,128)S(1)}, u32[]{:S(2)}, u32[]{:S(2)}) collective-permute-start(f32[2,2,8,768]{3,2,1,0:T(8,128)S(1)} %pad_maximum_fusion.2), channel_id=1, source_target_pairs={{0,8},{8,16},{16,24},{24,32},{32,40},{40,48},{48,56},{56,64},{64,7... | collective-permute-start | bytes 294920 | tf_op jit(solution)/shard_map/ppermute | solution.py:117
  10.6 30.5 %collective-permute-start.1 = (f32[2,2,8,768]{3,2,1,0:T(8,128)S(1)}, f32[2,2,8,768]{3,2,1,0:T(8,128)S(1)}, u32[]{:S(2)}, u32[]{:S(2)}) collective-permute-start(f32[2,2,8,768]{3,2,1,0:T(8,128)S(1)} %pad_maximum_fusion.3), channel_id=1, source_target_pairs={{8,0},{16,8},{24,16},{32,24},{40,32},{48,40},{56,48},{64,56},{72,6... | collective-permute-start | bytes 294920 | tf_op jit(solution)/shard_map/ppermute | solution.py:118
  36.0 5.2 %copy-start = (f32[2,2,8,1024]{3,2,1,0:T(8,128)S(1)}, f32[2,2,8,1024]{3,2,1,0:T(8,128)}, u32[]{:S(2)}) copy-start(f32[2,2,8,1024]{3,2,1,0:T(8,128)} %param.3) | copy-start | bytes 393220
  67.0 44.1 %copy-start.1 = (f32[1,2,2,8,1024]{4,3,2,1,0:T(8,128)S(1)}, f32[1,2,2,8,1024]{4,3,2,1,0:T(8,128)}, u32[]{:S(2)}) copy-start(f32[1,2,2,8,1024]{4,3,2,1,0:T(8,128)} %param.4) | copy-start | bytes 393220

commit v2 on v1

--- a/solution.py
+++ b/solution.py
@@ -102,10 +102,6 @@
         total = psum_chan(jnp.sum(own, axis=0))
         return rotate(ext, sign, own, total)
 
-    def channel_power(current):
-        summed = psum_tm(jnp.sum(jnp.square(current), axis=(0, 1, 3)))
-        return summed / total_len
-
     last_noise = noise[FIBER_SECTIONS - 1]
     count, length = lax.axis_size(TM), field.shape[3]
     up = [(i, (i + 1) % count) for i in range(count)]
@@ -123,10 +119,20 @@
         current = disperse(current, forward, reach) * ATT
         current = nonlinear(current, 1.0)
     centre = slice(noise_width, noise_width + length)
-    gain = lax.rsqrt(channel_power(current[..., centre]) + EPS)
+    signal, added = current[..., centre], last_noise
+    sums = psum_tm(
+        jnp.stack(
+            [
+                jnp.sum(jnp.square(signal), axis=(0, 1, 3)),
+                jnp.sum(signal * added, axis=(0, 1, 3)),
+                jnp.sum(jnp.square(added), axis=(0, 1, 3)),
+            ]
+        )
+    )
+    gain = lax.rsqrt(sums[0] / total_len + EPS)
+    arrival = (gain * gain * sums[0] + 2.0 * gain * sums[1] + sums[2]) / total_len
     current = current * gain[None, None, :, None] + noise_ext
     received = current[..., centre]
-    arrival = channel_power(received)
     rescale = jnp.sqrt(ATT ** (2 * STEPS) / (arrival + EPS))
     current = current * rescale[None, None, :, None]
     for step in range(STEPS):

time: 194 us -> 158 us (0.81)
  blocking collectives: 121 us -> 85.1 us
    psum x6 -> x3, blocking collectives: 60.3 us -> 31.4 us  [psum_tm(): value = lax.psum(value, axis)]
    psum x8, blocking collectives: 60.4 us -> 53.7 us  [psum_chan(): value = lax.psum(value, axis)]
  transfers between devices with their start and end apart: 2 -> 2, of which waited for: 0 -> 0; matrix products, arithmetic and copies ran while one was open for 9% -> 11% of each run, Pallas kernels for 0% -> 0%
where the time goes in v2:
time: 158 us; the launch traced here: 157 us
  blocking collectives  85.1 us (54%)
  matrix products  23.6 us (15%)
  starting transfers between devices  20.9 us (13%)
  other arithmetic  20.7 us (13%)
  local copies, waits for them, and re-layouts  5.48 us (3%)
    psum x8, blocking collectives, psum_chan(): value = lax.psum(value, axis)  53.7 us
    psum x3, blocking collectives, psum_tm(): value = lax.psum(value, axis)  31.4 us
    dot_general x4, matrix products, disperse(): jnp.einsum('pcjq,cqn->pcjn', stacked, table, precision=lax.Precision.HIGH...  23.6 us
    ppermute x1, starting transfers between devices, on_device(): after = lax.ppermute(leading, TM, down)  12.6 us
    div x1, other arithmetic, tap_tables(): mat_im = sign * interior_part * symbol_profile * jnp.sin(turn) / scale  12.3 us
    ppermute x1, starting transfers between devices, on_device(): before = lax.ppermute(trailing, TM, up)  8.27 us
    concatenate x1, other arithmetic, merged_table(): return jnp.concatenate([top, bottom], axis=1)  5.14 us
  transfers between devices with their start and end apart: 2, of which 0 were waited for; matrix products, arithmetic and copies ran while one was open for 11% of the time, Pallas kernels for 0%

profile of v2, /device:TPU:1, one launch (start us, length us, event | category | flops | bytes accessed | tf_op | source)
XLA Modules:
  0.0 156.9 jit_solution(16434985247068703220)
XLA Ops:
  0.6 0.8 fusion.85
  1.4 0.9 fusion.84
  2.3 8.3 %collective-permute-start = (f32[2,2,8,768]{3,2,1,0:T(8,128)S(1)}, f32[2,2,8,768]{3,2,1,0:T(8,128)S(1)}, u32[]{:S(2)}, u32[]{:S(2)}) collective-permute-start(f32[2,2,8,768]{3,2,1,0:T(8,128)S(1)} %pad_maximum_fusion.2), channel_id=1, source_target_pairs={{0,8},{8,16},{16,24},{24,32},{32,40},{40,48},{48,56},{56,64},{64,7... | collective-permute-start | bytes 294920 | tf_op jit(solution)/shard_map/ppermute | solution.py:113
  10.6 12.6 %collective-permute-start.1 = (f32[2,2,8,768]{3,2,1,0:T(8,128)S(1)}, f32[2,2,8,768]{3,2,1,0:T(8,128)S(1)}, u32[]{:S(2)}, u32[]{:S(2)}) collective-permute-start(f32[2,2,8,768]{3,2,1,0:T(8,128)S(1)} %pad_maximum_fusion.3), channel_id=1, source_target_pairs={{8,0},{16,8},{24,16},{32,24},{40,32},{48,40},{56,48},{64,56},{72,6... | collective-permute-start | bytes 294920 | tf_op jit(solution)/shard_map/ppermute | solution.py:114
  23.6 12.3 %fusion.27 = (f32[8,384,128]{2,1,0:T(8,128)S(1)}, f32[8,384,128]{2,1,0:T(8,128)S(1)}, f32[8,384,128]{2,1,0:T(8,128)S(1)}, f32[8,384,128]{2,1,0:T(8,128)S(1)}, f3...) fusion(f32[384,128]{1,0:T(8,128)S(1)} %fusion.62, f32[384,128]{1,0:T(8,128)S(1)} %broadcast_multiply_fusion.1, ...), kind=kLoop, calls=%fused_computation.33 | loop fusion | flops 9830400 | bytes 10223680 | tf_op jit(solution)/shard_map/div | solution.py:39
  36.0 5.1 %maximum_maximum_fusion = (f32[8,768,256]{2,1,0:T(8,128)}, f32[8,768,256]{2,1,0:T(8,128)}) fusion(f32[8,384,128]{2,1,0:T(8,128)S(1)} %get-tuple-element.39, f32[8,384,128]{2,1,0:T(8,128)S(1)} %get-tuple-element.40, f32[8,384,128]{2,1,0:T(8,128)S(1)} %get-tuple-element.41, f32[8,384,128]{2,1,0:T(8,128)S(1)} %get-tuple-element.38, ...), kind=kLoop, calls=%fused_computation | loop fusion | flops 9437184 | bytes 22020096 | tf_op jit(solution)/shard_map/concatenate | solution.py:46
  41.9 0.6 reshape.320
  42.5 6.1 %multiply_reduce_fusion.3 = (f32[14,256]{1,0:T(8,128)S(1)}, f32[8,14,256]{2,1,0:T(8,128)S(1)}, f32[2,8,14,256]{3,2,0,1:T(8,128)S(1)}) fusion(f32[2,8,14,768]{3,1,2,0:T(8,128)S(1)} %reshape.320, f32[8,768,256]{2,1,0:T(8,128)} %get-tuple-element.4), kind=kOutput, calls=%fused_computation.56 | convolution fusion | flops 528679424 | bytes 7337984 | tf_op jit(solution)/shard_map/pcjq,cqn->pcjn/dot_general | solution.py:58
  48.7 3.1 %psum.77 = f32[1792]{0:T(1024)S(1)} all-reduce(f32[1792]{0:T(1024)S(1)} %bitcast.178), channel_id=1, replica_groups=mesh['z'=4,'x'=8,'yh'=2,'ylo'=4,'core'=2] {'core'}, use_global_device_ids=true, to_apply=%region_3.0 | all-reduce | flops 1792 | bytes 14336 | tf_op jit(solution)/shard_map/psum | solution.py:84
  51.8 7.6 %psum.78 = f32[1792]{0:T(1024)S(1)} all-reduce(f32[1792]{0:T(1024)S(1)} %psum.77), channel_id=1, replica_groups=mesh['z'=4,'x'=8,'yh'=2,'ylo'=4,'core'=2] {'ylo'}, use_global_device_ids=true, to_apply=%region_4.0 | all-reduce | flops 1792 | bytes 14336 | tf_op jit(solution)/shard_map/psum | solution.py:84
  60.9 6.1 %multiply_reduce_fusion.1 = (f32[12,256]{1,0:T(8,128)S(1)}, f32[8,12,256]{2,1,0:T(8,128)S(1)}, f32[2,8,12,256]{3,2,0,1:T(8,128)S(1)}) fusion(f32[2,8,12,768]{3,1,2,0:T(8,128)S(1)} %reshape.321, f32[8,768,256]{2,1,0:T(8,128)} %get-tuple-element.4), kind=kOutput, calls=%fused_computation.54 | convolution fusion | flops 453153792 | bytes 7188480 | tf_op jit(solution)/shard_map/pcjq,cqn->pcjn/dot_general | solution.py:58
  67.1 4.5 %psum.79 = f32[1536]{0:T(1024)S(1)} all-reduce(f32[1536]{0:T(1024)S(1)} %bitcast.179), channel_id=1, replica_groups=mesh['z'=4,'x'=8,'yh'=2,'ylo'=4,'core'=2] {'core'}, use_global_device_ids=true, to_apply=%region_9.0 | all-reduce | flops 1536 | bytes 12288 | tf_op jit(solution)/shard_map/psum | solution.py:84
  71.6 7.6 %psum.80 = f32[1536]{0:T(1024)S(1)} all-reduce(f32[1536]{0:T(1024)S(1)} %psum.79), channel_id=1, replica_groups=mesh['z'=4,'x'=8,'yh'=2,'ylo'=4,'core'=2] {'ylo'}, use_global_device_ids=true, to_apply=%region_10.0 | all-reduce | flops 1536 | bytes 12288 | tf_op jit(solution)/shard_map/psum | solution.py:84
  79.8 7.7 %psum.81 = f32[3,8]{1,0:T(4,128)S(1)} all-reduce(f32[3,8]{1,0:T(4,128)S(1)} %pad_maximum_fusion.4), channel_id=1, replica_groups=mesh['z'=4,'x'=8,'yh'=2,'ylo'=4,'core'=2] {'yh'}, use_global_device_ids=true, to_apply=%region_16.0 | all-reduce | flops 24 | bytes 192 | tf_op jit(solution)/shard_map/psum | solution.py:78
  87.5 12.5 %psum.82 = f32[3,8]{1,0:T(4,128)S(1)} all-reduce(f32[3,8]{1,0:T(4,128)S(1)} %psum.81), channel_id=1, replica_groups=mesh['z'=4,'x'=8,'yh'=2,'ylo'=4,'core'=2] {'x'}, use_global_device_ids=true, to_apply=%region_17.0 | all-reduce | flops 24 | bytes 192 | tf_op jit(solution)/shard_map/psum | solution.py:78
  100.0 11.2 %psum.83 = f32[3,8]{1,0:T(4,128)S(1)} all-reduce(f32[3,8]{1,0:T(4,128)S(1)} %psum.82), channel_id=1, replica_groups=mesh['z'=4,'x'=8,'yh'=2,'ylo'=4,'core'=2] {'z'}, use_global_device_ids=true, to_apply=%region_18.0 | all-reduce | flops 24 | bytes 192 | tf_op jit(solution)/shard_map/psum | solution.py:78
  111.3 11.2 %psum.84 = f32[1536]{0:T(1024)S(1)} all-reduce(f32[1536]{0:T(1024)S(1)} %get-tuple-element.10), channel_id=1, replica_groups=mesh['z'=4,'x'=8,'yh'=2,'ylo'=4,'core'=2] {'core'}, use_global_device_ids=true, to_apply=%region_20.0 | all-reduce | flops 1536 | bytes 12288 | tf_op jit(solution)/shard_map/psum | solution.py:84
  122.6 8.5 %psum.85 = f32[1536]{0:T(1024)S(1)} all-reduce(f32[1536]{0:T(1024)S(1)} %psum.84), channel_id=1, replica_groups=mesh['z'=4,'x'=8,'yh'=2,'ylo'=4,'core'=2] {'ylo'}, use_global_device_ids=true, to_apply=%region_21.0 | all-reduce | flops 1536 | bytes 12288 | tf_op jit(solution)/shard_map/psum | solution.py:84
  132.2 6.0 %fusion.43 = f32[2,8,10,256]{3,2,0,1:T(8,128)S(1)} fusion(f32[8,768,256]{2,1,0:T(8,128)} %get-tuple-element.5, f32[2,8,10,768]{3,1,2,0:T(8,128)S(1)} %reshape.322), kind=kOutput, calls=%fused_computation.41 | convolution fusion | flops 377487360 | bytes 6946816 | tf_op jit(solution)/shard_map/pcjq,cqn->pcjn/dot_general | solution.py:58
  138.4 4.5 %psum.86 = f32[1280]{0:T(1024)S(1)} all-reduce(f32[1280]{0:T(1024)S(1)} %bitcast.180), channel_id=1, replica_groups=mesh['z'=4,'x'=8,'yh'=2,'ylo'=4,'core'=2] {'core'}, use_global_device_ids=true, to_apply=%region_24.25 | all-reduce | flops 1280 | bytes 10240 | tf_op jit(solution)/shard_map/psum | solution.py:84
  142.9 6.8 %psum.87 = f32[1280]{0:T(1024)S(1)} all-reduce(f32[1280]{0:T(1024)S(1)} %psum.86), channel_id=1, replica_groups=mesh['z'=4,'x'=8,'yh'=2,'ylo'=4,'core'=2] {'ylo'}, use_global_device_ids=true, to_apply=%region_25.26 | all-reduce | flops 1280 | bytes 10240 | tf_op jit(solution)/shard_map/psum | solution.py:84
  150.1 5.4 %fusion.46 = f32[2,2,8,8,128]{4,3,1,0,2:T(8,128)S(1)} fusion(f32[2,8,8,768]{3,2,0,1:T(8,128)S(1)} %bitcast.167, f32[8,768,256]{2,1,0:T(8,128)} %get-tuple-element.5), kind=kOutput, calls=%fused_computation.42 | convolution fusion | flops 301989888 | bytes 6815744 | tf_op jit(solution)/shard_map/pcjq,cqn->pcjn/dot_general | solution.py:58
  155.5 0.7 copy.115
  156.2 0.7 slice.152
  (65 shorter events, 5.1 us)
Async XLA Ops:
  0.6 22.8 %copy-start.2 = (s32[8]{0:T(128)S(1)}, s32[8]{0:T(128)}, u32[]{:S(2)}) copy-start(s32[8]{0:T(128)} %param.5) | copy-start | bytes 100
  2.3 38.8 %collective-permute-start = (f32[2,2,8,768]{3,2,1,0:T(8,128)S(1)}, f32[2,2,8,768]{3,2,1,0:T(8,128)S(1)}, u32[]{:S(2)}, u32[]{:S(2)}) collective-permute-start(f32[2,2,8,768]{3,2,1,0:T(8,128)S(1)} %pad_maximum_fusion.2), channel_id=1, source_target_pairs={{0,8},{8,16},{16,24},{24,32},{32,40},{40,48},{48,56},{56,64},{64,7... | collective-permute-start | bytes 294920 | tf_op jit(solution)/shard_map/ppermute | solution.py:113
  10.6 30.5 %collective-permute-start.1 = (f32[2,2,8,768]{3,2,1,0:T(8,128)S(1)}, f32[2,2,8,768]{3,2,1,0:T(8,128)S(1)}, u32[]{:S(2)}, u32[]{:S(2)}) collective-permute-start(f32[2,2,8,768]{3,2,1,0:T(8,128)S(1)} %pad_maximum_fusion.3), channel_id=1, source_target_pairs={{8,0},{16,8},{24,16},{32,24},{40,32},{48,40},{56,48},{64,56},{72,6... | collective-permute-start | bytes 294920 | tf_op jit(solution)/shard_map/ppermute | solution.py:114
  36.0 5.2 %copy-start.1 = (f32[2,2,8,1024]{3,2,1,0:T(8,128)S(1)}, f32[2,2,8,1024]{3,2,1,0:T(8,128)}, u32[]{:S(2)}) copy-start(f32[2,2,8,1024]{3,2,1,0:T(8,128)} %param.3) | copy-start | bytes 393220
  60.9 18.7 %copy-start = (f32[1,2,2,8,1024]{4,3,2,1,0:T(8,128)S(1)}, f32[1,2,2,8,1024]{4,3,2,1,0:T(8,128)}, u32[]{:S(2)}) copy-start(f32[1,2,2,8,1024]{4,3,2,1,0:T(8,128)} %param.4) | copy-start | bytes 393220

commit v3 on v2

--- a/solution.py
+++ b/solution.py
@@ -1,6 +1,8 @@
 import jax
 import jax.numpy as jnp
 from jax import lax
+from jax.experimental import pallas as pl
+from jax.experimental.pallas import tpu as pltpu
 from jax.sharding import Mesh, PartitionSpec as P
 
 OPTICAL_CHANNELS = 64
@@ -17,33 +19,56 @@
 EPS = 1e-06
 
 
-def tap_tables(channel_ids, sign, reach, channels):
-    rows = jnp.arange(3 * reach, dtype=jnp.int32)[:, None]
-    cols = jnp.arange(reach, dtype=jnp.int32)[None, :]
-    lag = cols - rows + reach
-    interior_part = (jnp.abs(lag) <= reach).astype(jnp.float32)
-    centre = (
-        WALK * reach * (2.0 * channel_ids.astype(jnp.float32) - (channels - 1)) / (channels - 1)
-    )
-    centre = centre[:, None, None]
+def tap_rows(channel_ids, sign, reach, channels):
+    lag = jnp.arange(-reach, reach + 1, dtype=jnp.int32).astype(jnp.float32)[None, :]
+    centre = WALK * reach * (2.0 * channel_ids.astype(jnp.float32) - (channels - 1)) / (channels - 1)
+    centre = centre[:, None]
     width = SPREAD * reach
-    offset = sign * lag.astype(jnp.float32)[None] - centre
+    offset = sign * lag - centre
     symbol_profile = jnp.exp(-jnp.square(offset / width))
     turn = jnp.square(offset) / (2.0 * CHIRP * reach)
-    taps = jnp.arange(-reach, reach + 1, dtype=jnp.int32).astype(jnp.float32)
-    scale = jnp.sqrt(
-        jnp.sum(jnp.exp(-2.0 * jnp.square((taps[None, :] - centre[:, :, 0]) / width)), axis=1)
-    )
-    scale = scale[:, None, None]
-    mat_re = interior_part * symbol_profile * jnp.cos(turn) / scale
-    mat_im = sign * interior_part * symbol_profile * jnp.sin(turn) / scale
-    return (mat_re, mat_im)
+    scale = jnp.sqrt(jnp.sum(jnp.exp(-2.0 * jnp.square((lag - centre) / width)), axis=1))[:, None]
+    tap_re = symbol_profile * jnp.cos(turn) / scale
+    tap_im = sign * symbol_profile * jnp.sin(turn) / scale
+    return jnp.stack([tap_re, tap_im], axis=1)
 
 
-def merged_table(mat_re, mat_im):
-    top = jnp.concatenate([mat_re, mat_im], axis=2)
-    bottom = jnp.concatenate([-mat_im, mat_re], axis=2)
-    return jnp.concatenate([top, bottom], axis=1)
+def toeplitz_kernel(taps_ref, forward_ref, backward_ref):
+    for sign, out_ref in enumerate((forward_ref, backward_ref)):
+        toeplitz_fill(taps_ref.at[sign], out_ref)
+
+
+def toeplitz_fill(taps_ref, out_ref):
+    reach = out_ref.shape[1] // 2
+    for block in range(3):
+        start = reach * (2 - block)
+        parts = []
+        for part in range(2):
+            row = taps_ref[part : part + 1, start : start + 2 * reach]
+            rolled = pltpu.roll(jnp.broadcast_to(row, (reach, 2 * reach)), 0, 1, stride=1, stride_axis=0)
+            parts.append(rolled[:, reach:])
+        real, imag = parts
+        rows = slice(block * reach, (block + 1) * reach)
+        low = slice(3 * reach + block * reach, 3 * reach + (block + 1) * reach)
+        out_ref[rows, :reach] = real
+        out_ref[rows, reach:] = imag
+        out_ref[low, :reach] = -imag
+        out_ref[low, reach:] = real
+
+
+def merged_tables(channel_ids, reach, channels):
+    taps = jnp.stack([tap_rows(channel_ids, 1.0, reach, channels), tap_rows(channel_ids, -1.0, reach, channels)], axis=1)
+    padded = jnp.pad(taps, ((0, 0), (0, 0), (0, 0), (reach, reach - 1)))
+    count = taps.shape[0]
+    table = jax.ShapeDtypeStruct((count, 6 * reach, 2 * reach), jnp.float32)
+    block = pl.BlockSpec((None, 6 * reach, 2 * reach), lambda s: (s, 0, 0))
+    return pl.pallas_call(
+        toeplitz_kernel,
+        grid=(count,),
+        in_specs=[pl.BlockSpec((None, 2, 2, 4 * reach), lambda s: (s, 0, 0, 0))],
+        out_specs=(block, block),
+        out_shape=(table, table),
+    )(padded)
 
 
 def disperse(ext, table, reach):
@@ -86,12 +111,7 @@
 
 
 def on_device(field, noise, assign):
-    forward, backward = lax.optimization_barrier(
-        (
-            merged_table(*tap_tables(assign, 1.0, FILTER_HALF_TAPS, OPTICAL_CHANNELS)),
-            merged_table(*tap_tables(assign, -1.0, FILTER_HALF_TAPS, OPTICAL_CHANNELS)),
-        )
-    )
+    forward, backward = merged_tables(assign, FILTER_HALF_TAPS, OPTICAL_CHANNELS)
     total_len = lax.axis_size(TM) * field.shape[3]
     reach = FILTER_HALF_TAPS
     field_width = 2 * STEPS * reach

time: 158 us -> 153 us (0.968)
  other arithmetic: 20.7 us -> 6.2 us
  Pallas kernels: 0 us -> 7.64 us
  waiting for transfers between devices: 0.01 us -> 2.45 us
    div x2, other arithmetic: 12.3 us -> 1.5 us  [the longest x1 0.84 us: tap_rows(): tap_re = symbol_profile * jnp.cos(turn) / scale]
    pallas_call x0 -> x1, Pallas kernels: none -> 7.64 us  [merged_tables(): pl.pallas_call(toeplitz_kernel, grid=(count,), in_specs=[pl.BlockSpec((No...]
    ppermute x1, starting transfers between devices: 12.6 us -> 18.9 us  [on_device(): after = lax.ppermute(leading, TM, down)]
    ppermute x1, starting transfers between devices: 8.27 us -> 1.92 us  [on_device(): before = lax.ppermute(trailing, TM, up)]
    concatenate x1 -> x0, other arithmetic: 5.14 us -> none  [merged_table(): return jnp.concatenate([top, bottom], axis=1)]
    ppermute x1, waiting for transfers between devices: 0.01 us -> 2.45 us  [on_device(): before = lax.ppermute(trailing, TM, up)]
    psum x3, blocking collectives: 31.4 us -> 29.7 us  [psum_tm(): value = lax.psum(value, axis)]
  transfers between devices with their start and end apart: 2 -> 2, of which waited for: 0 -> 1; matrix products, arithmetic and copies ran while one was open for 11% -> 2% of each run, Pallas kernels for 0% -> 5%
where the time goes in v3:
time: 153 us; the launch traced here: 151 us
  blocking collectives  84 us (55%)
  matrix products  23.6 us (15%)
  starting transfers between devices  20.9 us (14%)
  Pallas kernels  7.64 us (5%)
  other arithmetic  6.2 us (4%)
  local copies, waits for them, and re-layouts  5.47 us (4%)
  waiting for transfers between devices  2.45 us (2%)
    psum x8, blocking collectives, psum_chan(): value = lax.psum(value, axis)  54.3 us
    psum x3, blocking collectives, psum_tm(): value = lax.psum(value, axis)  29.7 us
    dot_general x4, matrix products, disperse(): jnp.einsum('pcjq,cqn->pcjn', stacked, table, precision=lax.Precision.HIGH...  23.6 us
    ppermute x1, starting transfers between devices, on_device(): after = lax.ppermute(leading, TM, down)  18.9 us
    pallas_call x1, Pallas kernels, merged_tables(): pl.pallas_call(toeplitz_kernel, grid=(count,), in_specs=[pl.BlockSpec((No...  7.64 us
  transfers between devices with their start and end apart: 2, of which 1 were waited for; matrix products, arithmetic and copies ran while one was open for 2% of the time, Pallas kernels for 5%

profile of v3, /device:TPU:1, one launch (start us, length us, event | category | flops | bytes accessed | tf_op | source)
XLA Modules:
  0.0 151.3 jit_solution(2737183085421627250)
XLA Ops:
  0.6 0.8 fusion.65
  1.4 0.9 fusion.64
  2.3 18.9 %collective-permute-start.1 = (f32[2,2,8,768]{3,2,1,0:T(8,128)S(1)}, f32[2,2,8,768]{3,2,1,0:T(8,128)S(1)}, u32[]{:S(2)}, u32[]{:S(2)}) collective-permute-start(f32[2,2,8,768]{3,2,1,0:T(8,128)S(1)} %pad_maximum_fusion.3), channel_id=1, source_target_pairs={{8,0},{16,8},{24,16},{32,24},{40,32},{48,40},{56,48},{64,56},{72,6... | collective-permute-start | bytes 294920 | tf_op jit(solution)/shard_map/ppermute | solution.py:134
  21.3 1.9 %collective-permute-start = (f32[2,2,8,768]{3,2,1,0:T(8,128)S(1)}, f32[2,2,8,768]{3,2,1,0:T(8,128)S(1)}, u32[]{:S(2)}, u32[]{:S(2)}) collective-permute-start(f32[2,2,8,768]{3,2,1,0:T(8,128)S(1)} %pad_maximum_fusion.2), channel_id=1, source_target_pairs={{0,8},{8,16},{16,24},{24,32},{32,40},{40,48},{48,56},{56,64},{64,7... | collective-permute-start | bytes 294920 | tf_op jit(solution)/shard_map/ppermute | solution.py:133
  24.1 0.8 multiply_divide_fusion.3
  25.7 7.6 %shard_map.50 = (f32[8,768,256]{2,1,0:T(8,128)}, f32[8,768,256]{2,1,0:T(8,128)}) custom-call(f32[8,2,2,512]{3,2,1,0:T(2,128)} %select_maximum_fusion.taps_ref), custom_call_target="tpu_custom_call" | custom-call | tf_op jit(solution)/shard_map/pallas_call | solution.py:65
  33.3 2.5 %collective-permute-done = f32[2,2,8,768]{3,2,1,0:T(8,128)S(1)} collective-permute-done((f32[2,2,8,768]{3,2,1,0:T(8,128)S(1)}, f32[2,2,8,768]{3,2,1,0:T(8,128)S(1)}, u32[]{:S(2)}, u32[]{:S(2)}) %collective-permute-start) | collective-permute-done | bytes 98336 | tf_op jit(solution)/shard_map/ppermute | solution.py:133
  35.8 0.9 maximum_bitcast_fusion.3
  38.0 6.1 %multiply_reduce_fusion.3 = (f32[14,256]{1,0:T(8,128)S(1)}, f32[8,14,256]{2,1,0:T(8,128)S(1)}, f32[2,8,14,256]{3,2,0,1:T(8,128)S(1)}) fusion(f32[2,8,14,768]{3,1,2,0:T(8,128)S(1)} %reshape.566, f32[8,768,256]{2,1,0:T(8,128)} %get-tuple-element.4), kind=kOutput, calls=%fused_computation.27 | convolution fusion | flops 528679424 | bytes 7337984 | tf_op jit(solution)/shard_map/pcjq,cqn->pcjn/dot_general | solution.py:83
  44.1 3.4 %psum.77 = f32[1792]{0:T(1024)S(1)} all-reduce(f32[1792]{0:T(1024)S(1)} %bitcast.184), channel_id=1, replica_groups=mesh['z'=4,'x'=8,'yh'=2,'ylo'=4,'core'=2] {'core'}, use_global_device_ids=true, to_apply=%region_3.4 | all-reduce | flops 1792 | bytes 14336 | tf_op jit(solution)/shard_map/psum | solution.py:109
  47.6 8.7 %psum.78 = f32[1792]{0:T(1024)S(1)} all-reduce(f32[1792]{0:T(1024)S(1)} %psum.77), channel_id=1, replica_groups=mesh['z'=4,'x'=8,'yh'=2,'ylo'=4,'core'=2] {'ylo'}, use_global_device_ids=true, to_apply=%region_4.5 | all-reduce | flops 1792 | bytes 14336 | tf_op jit(solution)/shard_map/psum | solution.py:109
  57.9 6.1 %multiply_reduce_fusion.1 = (f32[12,256]{1,0:T(8,128)S(1)}, f32[8,12,256]{2,1,0:T(8,128)S(1)}, f32[2,8,12,256]{3,2,0,1:T(8,128)S(1)}) fusion(f32[2,8,12,768]{3,1,2,0:T(8,128)S(1)} %reshape.567, f32[8,768,256]{2,1,0:T(8,128)} %get-tuple-element.4), kind=kOutput, calls=%fused_computation.25 | convolution fusion | flops 453153792 | bytes 7188480 | tf_op jit(solution)/shard_map/pcjq,cqn->pcjn/dot_general | solution.py:83
  64.0 4.5 %psum.79 = f32[1536]{0:T(1024)S(1)} all-reduce(f32[1536]{0:T(1024)S(1)} %bitcast.185), channel_id=1, replica_groups=mesh['z'=4,'x'=8,'yh'=2,'ylo'=4,'core'=2] {'core'}, use_global_device_ids=true, to_apply=%region_9.10 | all-reduce | flops 1536 | bytes 12288 | tf_op jit(solution)/shard_map/psum | solution.py:109
  68.5 6.8 %psum.80 = f32[1536]{0:T(1024)S(1)} all-reduce(f32[1536]{0:T(1024)S(1)} %psum.79), channel_id=1, replica_groups=mesh['z'=4,'x'=8,'yh'=2,'ylo'=4,'core'=2] {'ylo'}, use_global_device_ids=true, to_apply=%region_10.11 | all-reduce | flops 1536 | bytes 12288 | tf_op jit(solution)/shard_map/psum | solution.py:109
  75.9 7.7 %psum.81 = f32[3,8]{1,0:T(4,128)S(1)} all-reduce(f32[3,8]{1,0:T(4,128)S(1)} %pad_maximum_fusion.4), channel_id=1, replica_groups=mesh['z'=4,'x'=8,'yh'=2,'ylo'=4,'core'=2] {'yh'}, use_global_device_ids=true, to_apply=%region_16.17 | all-reduce | flops 24 | bytes 192 | tf_op jit(solution)/shard_map/psum | solution.py:103
  83.6 12.5 %psum.82 = f32[3,8]{1,0:T(4,128)S(1)} all-reduce(f32[3,8]{1,0:T(4,128)S(1)} %psum.81), channel_id=1, replica_groups=mesh['z'=4,'x'=8,'yh'=2,'ylo'=4,'core'=2] {'x'}, use_global_device_ids=true, to_apply=%region_17.18 | all-reduce | flops 24 | bytes 192 | tf_op jit(solution)/shard_map/psum | solution.py:103
  96.1 9.5 %psum.83 = f32[3,8]{1,0:T(4,128)S(1)} all-reduce(f32[3,8]{1,0:T(4,128)S(1)} %psum.82), channel_id=1, replica_groups=mesh['z'=4,'x'=8,'yh'=2,'ylo'=4,'core'=2] {'z'}, use_global_device_ids=true, to_apply=%region_18.19 | all-reduce | flops 24 | bytes 192 | tf_op jit(solution)/shard_map/psum | solution.py:103
  105.8 11.2 %psum.84 = f32[1536]{0:T(1024)S(1)} all-reduce(f32[1536]{0:T(1024)S(1)} %get-tuple-element.10), channel_id=1, replica_groups=mesh['z'=4,'x'=8,'yh'=2,'ylo'=4,'core'=2] {'core'}, use_global_device_ids=true, to_apply=%region_20.21 | all-reduce | flops 1536 | bytes 12288 | tf_op jit(solution)/shard_map/psum | solution.py:109
  117.0 7.5 %psum.85 = f32[1536]{0:T(1024)S(1)} all-reduce(f32[1536]{0:T(1024)S(1)} %psum.84), channel_id=1, replica_groups=mesh['z'=4,'x'=8,'yh'=2,'ylo'=4,'core'=2] {'ylo'}, use_global_device_ids=true, to_apply=%region_21.22 | all-reduce | flops 1536 | bytes 12288 | tf_op jit(solution)/shard_map/psum | solution.py:109
  126.4 6.0 %fusion.20 = f32[2,8,10,256]{3,2,0,1:T(8,128)S(1)} fusion(f32[8,768,256]{2,1,0:T(8,128)} %get-tuple-element.5, f32[2,8,10,768]{3,1,2,0:T(8,128)S(1)} %reshape.568), kind=kOutput, calls=%fused_computation.12 | convolution fusion | flops 377487360 | bytes 6946816 | tf_op jit(solution)/shard_map/pcjq,cqn->pcjn/dot_general | solution.py:83
  132.6 4.5 %psum.86 = f32[1280]{0:T(1024)S(1)} all-reduce(f32[1280]{0:T(1024)S(1)} %bitcast.186), channel_id=1, replica_groups=mesh['z'=4,'x'=8,'yh'=2,'ylo'=4,'core'=2] {'core'}, use_global_device_ids=true, to_apply=%region_24.25 | all-reduce | flops 1280 | bytes 10240 | tf_op jit(solution)/shard_map/psum | solution.py:109
  137.1 7.6 %psum.87 = f32[1280]{0:T(1024)S(1)} all-reduce(f32[1280]{0:T(1024)S(1)} %psum.86), channel_id=1, replica_groups=mesh['z'=4,'x'=8,'yh'=2,'ylo'=4,'core'=2] {'ylo'}, use_global_device_ids=true, to_apply=%region_25.26 | all-reduce | flops 1280 | bytes 10240 | tf_op jit(solution)/shard_map/psum | solution.py:109
  145.1 5.4 %fusion.23 = f32[2,2,8,8,128]{4,3,1,0,2:T(8,128)S(1)} fusion(f32[2,8,8,768]{3,2,0,1:T(8,128)S(1)} %bitcast.173, f32[8,768,256]{2,1,0:T(8,128)} %get-tuple-element.5), kind=kOutput, calls=%fused_computation.13 | convolution fusion | flops 301989888 | bytes 6815744 | tf_op jit(solution)/shard_map/pcjq,cqn->pcjn/dot_general | solution.py:83
  150.5 0.7 copy.144
  (60 shorter events, 7.5 us)
Async XLA Ops:
  2.3 31.0 %collective-permute-start.1 = (f32[2,2,8,768]{3,2,1,0:T(8,128)S(1)}, f32[2,2,8,768]{3,2,1,0:T(8,128)S(1)}, u32[]{:S(2)}, u32[]{:S(2)}) collective-permute-start(f32[2,2,8,768]{3,2,1,0:T(8,128)S(1)} %pad_maximum_fusion.3), channel_id=1, source_target_pairs={{8,0},{16,8},{24,16},{32,24},{40,32},{48,40},{56,48},{64,56},{72,6... | collective-permute-start | bytes 294920 | tf_op jit(solution)/shard_map/ppermute | solution.py:134
  21.3 14.5 %collective-permute-start = (f32[2,2,8,768]{3,2,1,0:T(8,128)S(1)}, f32[2,2,8,768]{3,2,1,0:T(8,128)S(1)}, u32[]{:S(2)}, u32[]{:S(2)}) collective-permute-start(f32[2,2,8,768]{3,2,1,0:T(8,128)S(1)} %pad_maximum_fusion.2), channel_id=1, source_target_pairs={{0,8},{8,16},{16,24},{24,32},{32,40},{40,48},{48,56},{56,64},{64,7... | collective-permute-start | bytes 294920 | tf_op jit(solution)/shard_map/ppermute | solution.py:133
  56.5 19.2 %copy-start = (f32[1,2,2,8,1024]{4,3,2,1,0:T(8,128)S(1)}, f32[1,2,2,8,1024]{4,3,2,1,0:T(8,128)}, u32[]{:S(2)}) copy-start(f32[1,2,2,8,1024]{4,3,2,1,0:T(8,128)} %param.4) | copy-start | bytes 393220

commit v4 on v3

--- a/solution.py
+++ b/solution.py
@@ -94,12 +94,12 @@
     return jnp.stack([real * cosine - imag * sine, real * sine + imag * cosine], axis=1)
 
 
-TM = ("z", "x", "yh")
+TM = ("z", "xh", "xl", "yh")
 CHAN = ("ylo", "core")
 
 
 def psum_tm(value):
-    for axis in ("yh", "x", "z"):
+    for axis in ("yh", "xl", "xh", "z"):
         value = lax.psum(value, axis)
     return value
 
@@ -163,7 +163,7 @@
 
 def solution(mesh):
     tm, chan = mesh.shape["tm"], mesh.shape["chan"]
-    fine = Mesh(mesh.devices.reshape(tm // 16, 8, 2, chan // 2, 2), TM + CHAN)
+    fine = Mesh(mesh.devices.reshape(tm // 16, 2, 4, 2, chan // 2, 2), TM + CHAN)
     placed = (P(None, None, CHAN, TM), P(None, None, None, CHAN, TM), P(CHAN))
     return jax.shard_map(
         on_device,

time: 153 us -> 148 us (0.967)
  blocking collectives: 84 us -> 79.2 us
    psum x3 -> x4, blocking collectives: 29.7 us -> 25.9 us  [psum_tm(): value = lax.psum(value, axis)]
where the time goes in v4:
time: 148 us; the launch traced here: 146 us
  blocking collectives  79.2 us (54%)
  matrix products  23.6 us (16%)
  starting transfers between devices  20.9 us (14%)
  Pallas kernels  7.64 us (5%)
  other arithmetic  6.2 us (4%)
  local copies, waits for them, and re-layouts  5.47 us (4%)
  waiting for transfers between devices  2.45 us (2%)
    psum x8, blocking collectives, psum_chan(): value = lax.psum(value, axis)  53.3 us
    psum x4, blocking collectives, psum_tm(): value = lax.psum(value, axis)  25.9 us
    dot_general x4, matrix products, disperse(): jnp.einsum('pcjq,cqn->pcjn', stacked, table, precision=lax.Precision.HIGH...  23.6 us
    ppermute x1, starting transfers between devices, on_device(): after = lax.ppermute(leading, TM, down)  18.9 us
    pallas_call x1, Pallas kernels, merged_tables(): pl.pallas_call(toeplitz_kernel, grid=(count,), in_specs=[pl.BlockSpec((No...  7.64 us
  transfers between devices with their start and end apart: 2, of which 1 were waited for; matrix products, arithmetic and copies ran while one was open for 2% of the time, Pallas kernels for 5%

profile of v4, /device:TPU:1, one launch (start us, length us, event | category | flops | bytes accessed | tf_op | source)
XLA Modules:
  0.0 146.5 jit_solution(5225540348116240802)
XLA Ops:
  0.6 0.8 fusion.65
  1.4 0.9 fusion.64
  2.3 18.9 %collective-permute-start.1 = (f32[2,2,8,768]{3,2,1,0:T(8,128)S(1)}, f32[2,2,8,768]{3,2,1,0:T(8,128)S(1)}, u32[]{:S(2)}, u32[]{:S(2)}) collective-permute-start(f32[2,2,8,768]{3,2,1,0:T(8,128)S(1)} %pad_maximum_fusion.3), channel_id=1, source_target_pairs={{8,0},{16,8},{24,16},{32,24},{40,32},{48,40},{56,48},{64,56},{72,6... | collective-permute-start | bytes 294920 | tf_op jit(solution)/shard_map/ppermute | solution.py:134
  21.3 1.9 %collective-permute-start = (f32[2,2,8,768]{3,2,1,0:T(8,128)S(1)}, f32[2,2,8,768]{3,2,1,0:T(8,128)S(1)}, u32[]{:S(2)}, u32[]{:S(2)}) collective-permute-start(f32[2,2,8,768]{3,2,1,0:T(8,128)S(1)} %pad_maximum_fusion.2), channel_id=1, source_target_pairs={{0,8},{8,16},{16,24},{24,32},{32,40},{40,48},{48,56},{56,64},{64,7... | collective-permute-start | bytes 294920 | tf_op jit(solution)/shard_map/ppermute | solution.py:133
  24.1 0.8 multiply_divide_fusion.3
  25.7 7.6 %shard_map.50 = (f32[8,768,256]{2,1,0:T(8,128)}, f32[8,768,256]{2,1,0:T(8,128)}) custom-call(f32[8,2,2,512]{3,2,1,0:T(2,128)} %select_maximum_fusion.taps_ref), custom_call_target="tpu_custom_call" | custom-call | tf_op jit(solution)/shard_map/pallas_call | solution.py:65
  33.3 2.5 %collective-permute-done = f32[2,2,8,768]{3,2,1,0:T(8,128)S(1)} collective-permute-done((f32[2,2,8,768]{3,2,1,0:T(8,128)S(1)}, f32[2,2,8,768]{3,2,1,0:T(8,128)S(1)}, u32[]{:S(2)}, u32[]{:S(2)}) %collective-permute-start) | collective-permute-done | bytes 98336 | tf_op jit(solution)/shard_map/ppermute | solution.py:133
  35.8 0.9 maximum_bitcast_fusion.3
  38.0 6.1 %multiply_reduce_fusion.3 = (f32[14,256]{1,0:T(8,128)S(1)}, f32[8,14,256]{2,1,0:T(8,128)S(1)}, f32[2,8,14,256]{3,2,0,1:T(8,128)S(1)}) fusion(f32[2,8,14,768]{3,1,2,0:T(8,128)S(1)} %reshape.566, f32[8,768,256]{2,1,0:T(8,128)} %get-tuple-element.4), kind=kOutput, calls=%fused_computation.27 | convolution fusion | flops 528679424 | bytes 7337984 | tf_op jit(solution)/shard_map/pcjq,cqn->pcjn/dot_general | solution.py:83
  44.1 3.4 %psum.84 = f32[1792]{0:T(1024)S(1)} all-reduce(f32[1792]{0:T(1024)S(1)} %bitcast.184), channel_id=1, replica_groups=mesh['z'=4,'xh'=2,'xl'=4,'yh'=2,'ylo'=4,'core'=2] {'core'}, use_global_device_ids=true, to_apply=%region_3.4 | all-reduce | flops 1792 | bytes 14336 | tf_op jit(solution)/shard_map/psum | solution.py:109
  47.6 8.7 %psum.85 = f32[1792]{0:T(1024)S(1)} all-reduce(f32[1792]{0:T(1024)S(1)} %psum.84), channel_id=1, replica_groups=mesh['z'=4,'xh'=2,'xl'=4,'yh'=2,'ylo'=4,'core'=2] {'ylo'}, use_global_device_ids=true, to_apply=%region_4.5 | all-reduce | flops 1792 | bytes 14336 | tf_op jit(solution)/shard_map/psum | solution.py:109
  57.9 6.1 %multiply_reduce_fusion.1 = (f32[12,256]{1,0:T(8,128)S(1)}, f32[8,12,256]{2,1,0:T(8,128)S(1)}, f32[2,8,12,256]{3,2,0,1:T(8,128)S(1)}) fusion(f32[2,8,12,768]{3,1,2,0:T(8,128)S(1)} %reshape.567, f32[8,768,256]{2,1,0:T(8,128)} %get-tuple-element.4), kind=kOutput, calls=%fused_computation.25 | convolution fusion | flops 453153792 | bytes 7188480 | tf_op jit(solution)/shard_map/pcjq,cqn->pcjn/dot_general | solution.py:83
  64.0 4.5 %psum.86 = f32[1536]{0:T(1024)S(1)} all-reduce(f32[1536]{0:T(1024)S(1)} %bitcast.185), channel_id=1, replica_groups=mesh['z'=4,'xh'=2,'xl'=4,'yh'=2,'ylo'=4,'core'=2] {'core'}, use_global_device_ids=true, to_apply=%region_9.10 | all-reduce | flops 1536 | bytes 12288 | tf_op jit(solution)/shard_map/psum | solution.py:109
  68.5 6.8 %psum.87 = f32[1536]{0:T(1024)S(1)} all-reduce(f32[1536]{0:T(1024)S(1)} %psum.86), channel_id=1, replica_groups=mesh['z'=4,'xh'=2,'xl'=4,'yh'=2,'ylo'=4,'core'=2] {'ylo'}, use_global_device_ids=true, to_apply=%region_10.11 | all-reduce | flops 1536 | bytes 12288 | tf_op jit(solution)/shard_map/psum | solution.py:109
  75.9 7.7 %psum.88 = f32[3,8]{1,0:T(4,128)S(1)} all-reduce(f32[3,8]{1,0:T(4,128)S(1)} %pad_maximum_fusion.4), channel_id=1, replica_groups=mesh['z'=4,'xh'=2,'xl'=4,'yh'=2,'ylo'=4,'core'=2] {'yh'}, use_global_device_ids=true, to_apply=%region_16.17 | all-reduce | flops 24 | bytes 192 | tf_op jit(solution)/shard_map/psum | solution.py:103
  83.6 6.0 %psum.89 = f32[3,8]{1,0:T(4,128)S(1)} all-reduce(f32[3,8]{1,0:T(4,128)S(1)} %psum.88), channel_id=1, replica_groups=mesh['z'=4,'xh'=2,'xl'=4,'yh'=2,'ylo'=4,'core'=2] {'xl'}, use_global_device_ids=true, to_apply=%region_17.18 | all-reduce | flops 24 | bytes 192 | tf_op jit(solution)/shard_map/psum | solution.py:103
  89.6 3.8 %psum.90 = f32[3,8]{1,0:T(4,128)S(1)} all-reduce(f32[3,8]{1,0:T(4,128)S(1)} %psum.89), channel_id=1, replica_groups=mesh['z'=4,'xh'=2,'xl'=4,'yh'=2,'ylo'=4,'core'=2] {'xh'}, use_global_device_ids=true, to_apply=%region_18.19 | all-reduce | flops 24 | bytes 192 | tf_op jit(solution)/shard_map/psum | solution.py:103
  93.4 8.5 %psum.91 = f32[3,8]{1,0:T(4,128)S(1)} all-reduce(f32[3,8]{1,0:T(4,128)S(1)} %psum.90), channel_id=1, replica_groups=mesh['z'=4,'xh'=2,'xl'=4,'yh'=2,'ylo'=4,'core'=2] {'z'}, use_global_device_ids=true, to_apply=%region_19.20 | all-reduce | flops 24 | bytes 192 | tf_op jit(solution)/shard_map/psum | solution.py:103
  102.0 10.2 %psum.92 = f32[1536]{0:T(1024)S(1)} all-reduce(f32[1536]{0:T(1024)S(1)} %get-tuple-element.10), channel_id=1, replica_groups=mesh['z'=4,'xh'=2,'xl'=4,'yh'=2,'ylo'=4,'core'=2] {'core'}, use_global_device_ids=true, to_apply=%region_21.22 | all-reduce | flops 1536 | bytes 12288 | tf_op jit(solution)/shard_map/psum | solution.py:109
  112.2 7.5 %psum.93 = f32[1536]{0:T(1024)S(1)} all-reduce(f32[1536]{0:T(1024)S(1)} %psum.92), channel_id=1, replica_groups=mesh['z'=4,'xh'=2,'xl'=4,'yh'=2,'ylo'=4,'core'=2] {'ylo'}, use_global_device_ids=true, to_apply=%region_22.23 | all-reduce | flops 1536 | bytes 12288 | tf_op jit(solution)/shard_map/psum | solution.py:109
  121.6 6.0 %fusion.20 = f32[2,8,10,256]{3,2,0,1:T(8,128)S(1)} fusion(f32[8,768,256]{2,1,0:T(8,128)} %get-tuple-element.5, f32[2,8,10,768]{3,1,2,0:T(8,128)S(1)} %reshape.568), kind=kOutput, calls=%fused_computation.12 | convolution fusion | flops 377487360 | bytes 6946816 | tf_op jit(solution)/shard_map/pcjq,cqn->pcjn/dot_general | solution.py:83
  127.8 4.5 %psum.94 = f32[1280]{0:T(1024)S(1)} all-reduce(f32[1280]{0:T(1024)S(1)} %bitcast.186), channel_id=1, replica_groups=mesh['z'=4,'xh'=2,'xl'=4,'yh'=2,'ylo'=4,'core'=2] {'core'}, use_global_device_ids=true, to_apply=%region_25.26 | all-reduce | flops 1280 | bytes 10240 | tf_op jit(solution)/shard_map/psum | solution.py:109
  132.3 7.6 %psum.95 = f32[1280]{0:T(1024)S(1)} all-reduce(f32[1280]{0:T(1024)S(1)} %psum.94), channel_id=1, replica_groups=mesh['z'=4,'xh'=2,'xl'=4,'yh'=2,'ylo'=4,'core'=2] {'ylo'}, use_global_device_ids=true, to_apply=%region_26.27 | all-reduce | flops 1280 | bytes 10240 | tf_op jit(solution)/shard_map/psum | solution.py:109
  140.3 5.4 %fusion.23 = f32[2,2,8,8,128]{4,3,1,0,2:T(8,128)S(1)} fusion(f32[2,8,8,768]{3,2,0,1:T(8,128)S(1)} %bitcast.173, f32[8,768,256]{2,1,0:T(8,128)} %get-tuple-element.5), kind=kOutput, calls=%fused_computation.13 | convolution fusion | flops 301989888 | bytes 6815744 | tf_op jit(solution)/shard_map/pcjq,cqn->pcjn/dot_general | solution.py:83
  (61 shorter events, 8.2 us)
Async XLA Ops:
  2.3 31.0 %collective-permute-start.1 = (f32[2,2,8,768]{3,2,1,0:T(8,128)S(1)}, f32[2,2,8,768]{3,2,1,0:T(8,128)S(1)}, u32[]{:S(2)}, u32[]{:S(2)}) collective-permute-start(f32[2,2,8,768]{3,2,1,0:T(8,128)S(1)} %pad_maximum_fusion.3), channel_id=1, source_target_pairs={{8,0},{16,8},{24,16},{32,24},{40,32},{48,40},{56,48},{64,56},{72,6... | collective-permute-start | bytes 294920 | tf_op jit(solution)/shard_map/ppermute | solution.py:134
  21.3 14.5 %collective-permute-start = (f32[2,2,8,768]{3,2,1,0:T(8,128)S(1)}, f32[2,2,8,768]{3,2,1,0:T(8,128)S(1)}, u32[]{:S(2)}, u32[]{:S(2)}) collective-permute-start(f32[2,2,8,768]{3,2,1,0:T(8,128)S(1)} %pad_maximum_fusion.2), channel_id=1, source_target_pairs={{0,8},{8,16},{16,24},{24,32},{32,40},{40,48},{48,56},{56,64},{64,7... | collective-permute-start | bytes 294920 | tf_op jit(solution)/shard_map/ppermute | solution.py:133
  56.5 19.2 %copy-start = (f32[1,2,2,8,1024]{4,3,2,1,0:T(8,128)S(1)}, f32[1,2,2,8,1024]{4,3,2,1,0:T(8,128)}, u32[]{:S(2)}) copy-start(f32[1,2,2,8,1024]{4,3,2,1,0:T(8,128)} %param.4) | copy-start | bytes 393220

commit v5 on v4

--- a/solution.py
+++ b/solution.py
@@ -130,6 +130,7 @@
         [field[..., length - field_width :], last_noise[..., length - noise_width :]], axis=3
     )
     leading = jnp.concatenate([field[..., :field_width], last_noise[..., :noise_width]], axis=3)
+    forward, backward, trailing, leading = lax.optimization_barrier((forward, backward, trailing, leading))
     before = lax.ppermute(trailing, TM, up)
     after = lax.ppermute(leading, TM, down)
     current = jnp.concatenate([before[..., :field_width], field, after[..., :field_width]], axis=3)

time: 148 us -> 155 us (1.047)
  blocking collectives: 79.2 us -> 87.1 us
    psum x4, blocking collectives: 25.9 us -> 32.5 us  [psum_tm(): value = lax.psum(value, axis)]
    ppermute x1, starting transfers between devices: 18.9 us -> 12.6 us  [on_device(): after = lax.ppermute(leading, TM, down)]
    ppermute x1, starting transfers between devices: 1.92 us -> 8.27 us  [on_device(): before = lax.ppermute(trailing, TM, up)]
    ppermute x1, waiting for transfers between devices: 2.45 us -> 0.55 us  [on_device(): before = lax.ppermute(trailing, TM, up)]
  transfers between devices with their start and end apart: 2 -> 2, of which waited for: 1 -> 2; matrix products, arithmetic and copies ran while one was open for 2% -> 0% of each run, Pallas kernels for 5% -> 0%
where the time goes in v5:
time: 155 us; the launch traced here: 154 us
  blocking collectives  87.1 us (56%)
  matrix products  23.6 us (15%)
  starting transfers between devices  20.9 us (13%)
  Pallas kernels  7.64 us (5%)
  other arithmetic  6.19 us (4%)
  local copies, waits for them, and re-layouts  5.47 us (4%)
  waiting for transfers between devices  1.61 us (1%)
    psum x8, blocking collectives, psum_chan(): value = lax.psum(value, axis)  54.6 us
    psum x4, blocking collectives, psum_tm(): value = lax.psum(value, axis)  32.5 us
    dot_general x4, matrix products, disperse(): jnp.einsum('pcjq,cqn->pcjn', stacked, table, precision=lax.Precision.HIGH...  23.6 us
    ppermute x1, starting transfers between devices, on_device(): after = lax.ppermute(leading, TM, down)  12.6 us
    ppermute x1, starting transfers between devices, on_device(): before = lax.ppermute(trailing, TM, up)  8.27 us
    pallas_call x1, Pallas kernels, merged_tables(): pl.pallas_call(toeplitz_kernel, grid=(count,), in_specs=[pl.BlockSpec((No...  7.64 us
  transfers between devices with their start and end apart: 2, of which 2 were waited for; matrix products, arithmetic and copies ran while one was open for 0% of the time, Pallas kernels for 0%

profile of v5, /device:TPU:1, one launch (start us, length us, event | category | flops | bytes accessed | tf_op | source)
XLA Modules:
  0.0 153.5 jit_solution(431086576756804396)
XLA Ops:
  1.5 0.8 fusion.65
  2.3 0.9 fusion.64
  3.2 0.8 multiply_divide_fusion.3
  4.7 7.6 %shard_map.50 = (f32[8,768,256]{2,1,0:T(8,128)}, f32[8,768,256]{2,1,0:T(8,128)}) custom-call(f32[8,2,2,512]{3,2,1,0:T(2,128)} %select_maximum_fusion.taps_ref), custom_call_target="tpu_custom_call" | custom-call | tf_op jit(solution)/shard_map/pallas_call | solution.py:65
  12.4 8.3 %collective-permute-start = (f32[2,2,8,768]{3,2,1,0:T(8,128)S(1)}, f32[2,2,8,768]{3,2,1,0:T(8,128)S(1)}, u32[]{:S(2)}, u32[]{:S(2)}) collective-permute-start(f32[2,2,8,768]{3,2,1,0:T(8,128)S(1)} %get-tuple-element.11), channel_id=1, source_target_pairs={{0,8},{8,16},{16,24},{24,32},{32,40},{40,48},{48,56},{56,64},{64,7... | collective-permute-start | bytes 294920 | tf_op jit(solution)/shard_map/ppermute | solution.py:134
  20.7 12.6 %collective-permute-start.1 = (f32[2,2,8,768]{3,2,1,0:T(8,128)S(1)}, f32[2,2,8,768]{3,2,1,0:T(8,128)S(1)}, u32[]{:S(2)}, u32[]{:S(2)}) collective-permute-start(f32[2,2,8,768]{3,2,1,0:T(8,128)S(1)} %get-tuple-element.12), channel_id=1, source_target_pairs={{8,0},{16,8},{24,16},{32,24},{40,32},{48,40},{56,48},{64,56},{72,6... | collective-permute-start | bytes 294920 | tf_op jit(solution)/shard_map/ppermute | solution.py:135
  33.8 1.1 collective-permute-done.1
  34.9 0.9 maximum_bitcast_fusion.3
  37.1 6.1 %multiply_reduce_fusion.3 = (f32[14,256]{1,0:T(8,128)S(1)}, f32[8,14,256]{2,1,0:T(8,128)S(1)}, f32[2,8,14,256]{3,2,0,1:T(8,128)S(1)}) fusion(f32[2,8,14,768]{3,1,2,0:T(8,128)S(1)} %reshape.566, f32[8,768,256]{2,1,0:T(8,128)} %get-tuple-element.10), kind=kOutput, calls=%fused_computation.27 | convolution fusion | flops 528679424 | bytes 7337984 | tf_op jit(solution)/shard_map/pcjq,cqn->pcjn/dot_general | solution.py:83
  43.3 3.7 %psum.84 = f32[1792]{0:T(1024)S(1)} all-reduce(f32[1792]{0:T(1024)S(1)} %bitcast.184), channel_id=1, replica_groups=mesh['z'=4,'xh'=2,'xl'=4,'yh'=2,'ylo'=4,'core'=2] {'core'}, use_global_device_ids=true, to_apply=%region_3.4 | all-reduce | flops 1792 | bytes 14336 | tf_op jit(solution)/shard_map/psum | solution.py:109
  47.0 9.1 %psum.85 = f32[1792]{0:T(1024)S(1)} all-reduce(f32[1792]{0:T(1024)S(1)} %psum.84), channel_id=1, replica_groups=mesh['z'=4,'xh'=2,'xl'=4,'yh'=2,'ylo'=4,'core'=2] {'ylo'}, use_global_device_ids=true, to_apply=%region_4.5 | all-reduce | flops 1792 | bytes 14336 | tf_op jit(solution)/shard_map/psum | solution.py:109
  57.6 6.1 %multiply_reduce_fusion.1 = (f32[12,256]{1,0:T(8,128)S(1)}, f32[8,12,256]{2,1,0:T(8,128)S(1)}, f32[2,8,12,256]{3,2,0,1:T(8,128)S(1)}) fusion(f32[2,8,12,768]{3,1,2,0:T(8,128)S(1)} %reshape.567, f32[8,768,256]{2,1,0:T(8,128)} %get-tuple-element.10), kind=kOutput, calls=%fused_computation.25 | convolution fusion | flops 453153792 | bytes 7188480 | tf_op jit(solution)/shard_map/pcjq,cqn->pcjn/dot_general | solution.py:83
  63.8 4.5 %psum.86 = f32[1536]{0:T(1024)S(1)} all-reduce(f32[1536]{0:T(1024)S(1)} %bitcast.185), channel_id=1, replica_groups=mesh['z'=4,'xh'=2,'xl'=4,'yh'=2,'ylo'=4,'core'=2] {'core'}, use_global_device_ids=true, to_apply=%region_9.10 | all-reduce | flops 1536 | bytes 12288 | tf_op jit(solution)/shard_map/psum | solution.py:109
  68.3 6.8 %psum.87 = f32[1536]{0:T(1024)S(1)} all-reduce(f32[1536]{0:T(1024)S(1)} %psum.86), channel_id=1, replica_groups=mesh['z'=4,'xh'=2,'xl'=4,'yh'=2,'ylo'=4,'core'=2] {'ylo'}, use_global_device_ids=true, to_apply=%region_10.11 | all-reduce | flops 1536 | bytes 12288 | tf_op jit(solution)/shard_map/psum | solution.py:109
  75.7 7.7 %psum.88 = f32[3,8]{1,0:T(4,128)S(1)} all-reduce(f32[3,8]{1,0:T(4,128)S(1)} %pad_maximum_fusion.4), channel_id=1, replica_groups=mesh['z'=4,'xh'=2,'xl'=4,'yh'=2,'ylo'=4,'core'=2] {'yh'}, use_global_device_ids=true, to_apply=%region_16.17 | all-reduce | flops 24 | bytes 192 | tf_op jit(solution)/shard_map/psum | solution.py:103
  83.4 6.0 %psum.89 = f32[3,8]{1,0:T(4,128)S(1)} all-reduce(f32[3,8]{1,0:T(4,128)S(1)} %psum.88), channel_id=1, replica_groups=mesh['z'=4,'xh'=2,'xl'=4,'yh'=2,'ylo'=4,'core'=2] {'xl'}, use_global_device_ids=true, to_apply=%region_17.18 | all-reduce | flops 24 | bytes 192 | tf_op jit(solution)/shard_map/psum | solution.py:103
  89.4 4.4 %psum.90 = f32[3,8]{1,0:T(4,128)S(1)} all-reduce(f32[3,8]{1,0:T(4,128)S(1)} %psum.89), channel_id=1, replica_groups=mesh['z'=4,'xh'=2,'xl'=4,'yh'=2,'ylo'=4,'core'=2] {'xh'}, use_global_device_ids=true, to_apply=%region_18.19 | all-reduce | flops 24 | bytes 192 | tf_op jit(solution)/shard_map/psum | solution.py:103
  93.8 14.4 %psum.91 = f32[3,8]{1,0:T(4,128)S(1)} all-reduce(f32[3,8]{1,0:T(4,128)S(1)} %psum.90), channel_id=1, replica_groups=mesh['z'=4,'xh'=2,'xl'=4,'yh'=2,'ylo'=4,'core'=2] {'z'}, use_global_device_ids=true, to_apply=%region_19.20 | all-reduce | flops 24 | bytes 192 | tf_op jit(solution)/shard_map/psum | solution.py:103
  108.4 10.8 %psum.92 = f32[1536]{0:T(1024)S(1)} all-reduce(f32[1536]{0:T(1024)S(1)} %get-tuple-element.18), channel_id=1, replica_groups=mesh['z'=4,'xh'=2,'xl'=4,'yh'=2,'ylo'=4,'core'=2] {'core'}, use_global_device_ids=true, to_apply=%region_21.22 | all-reduce | flops 1536 | bytes 12288 | tf_op jit(solution)/shard_map/psum | solution.py:109
  119.2 8.2 %psum.93 = f32[1536]{0:T(1024)S(1)} all-reduce(f32[1536]{0:T(1024)S(1)} %psum.92), channel_id=1, replica_groups=mesh['z'=4,'xh'=2,'xl'=4,'yh'=2,'ylo'=4,'core'=2] {'ylo'}, use_global_device_ids=true, to_apply=%region_22.23 | all-reduce | flops 1536 | bytes 12288 | tf_op jit(solution)/shard_map/psum | solution.py:109
  129.3 6.0 %fusion.20 = f32[2,8,10,256]{3,2,0,1:T(8,128)S(1)} fusion(f32[8,768,256]{2,1,0:T(8,128)} %get-tuple-element.13, f32[2,8,10,768]{3,1,2,0:T(8,128)S(1)} %reshape.568), kind=kOutput, calls=%fused_computation.12 | convolution fusion | flops 377487360 | bytes 6946816 | tf_op jit(solution)/shard_map/pcjq,cqn->pcjn/dot_general | solution.py:83
  135.4 4.5 %psum.94 = f32[1280]{0:T(1024)S(1)} all-reduce(f32[1280]{0:T(1024)S(1)} %bitcast.186), channel_id=1, replica_groups=mesh['z'=4,'xh'=2,'xl'=4,'yh'=2,'ylo'=4,'core'=2] {'core'}, use_global_device_ids=true, to_apply=%region_25.26 | all-reduce | flops 1280 | bytes 10240 | tf_op jit(solution)/shard_map/psum | solution.py:109
  139.9 7.0 %psum.95 = f32[1280]{0:T(1024)S(1)} all-reduce(f32[1280]{0:T(1024)S(1)} %psum.94), channel_id=1, replica_groups=mesh['z'=4,'xh'=2,'xl'=4,'yh'=2,'ylo'=4,'core'=2] {'ylo'}, use_global_device_ids=true, to_apply=%region_26.27 | all-reduce | flops 1280 | bytes 10240 | tf_op jit(solution)/shard_map/psum | solution.py:109
  147.4 5.4 %fusion.23 = f32[2,2,8,8,128]{4,3,1,0,2:T(8,128)S(1)} fusion(f32[2,8,8,768]{3,2,0,1:T(8,128)S(1)} %bitcast.173, f32[8,768,256]{2,1,0:T(8,128)} %get-tuple-element.13), kind=kOutput, calls=%fused_computation.13 | convolution fusion | flops 301989888 | bytes 6815744 | tf_op jit(solution)/shard_map/pcjq,cqn->pcjn/dot_general | solution.py:83
  (60 shorter events, 8.8 us)
Async XLA Ops:
  12.4 21.4 %collective-permute-start = (f32[2,2,8,768]{3,2,1,0:T(8,128)S(1)}, f32[2,2,8,768]{3,2,1,0:T(8,128)S(1)}, u32[]{:S(2)}, u32[]{:S(2)}) collective-permute-start(f32[2,2,8,768]{3,2,1,0:T(8,128)S(1)} %get-tuple-element.11), channel_id=1, source_target_pairs={{0,8},{8,16},{16,24},{24,32},{32,40},{40,48},{48,56},{56,64},{64,7... | collective-permute-start | bytes 294920 | tf_op jit(solution)/shard_map/ppermute | solution.py:134
  20.7 14.2 %collective-permute-start.1 = (f32[2,2,8,768]{3,2,1,0:T(8,128)S(1)}, f32[2,2,8,768]{3,2,1,0:T(8,128)S(1)}, u32[]{:S(2)}, u32[]{:S(2)}) collective-permute-start(f32[2,2,8,768]{3,2,1,0:T(8,128)S(1)} %get-tuple-element.12), channel_id=1, source_target_pairs={{8,0},{16,8},{24,16},{32,24},{40,32},{48,40},{56,48},{64,56},{72,6... | collective-permute-start | bytes 294920 | tf_op jit(solution)/shard_map/ppermute | solution.py:135
  56.3 19.2 %copy-start = (f32[1,2,2,8,1024]{4,3,2,1,0:T(8,128)S(1)}, f32[1,2,2,8,1024]{4,3,2,1,0:T(8,128)}, u32[]{:S(2)}) copy-start(f32[1,2,2,8,1024]{4,3,2,1,0:T(8,128)} %param.4) | copy-start | bytes 393220

commit v6 on v4

--- a/solution.py
+++ b/solution.py
@@ -75,11 +75,10 @@
     pols, parts, chans, segment_length = ext.shape
     blocks = segment_length // reach - 2
     rows = ext.reshape(pols, parts, chans, blocks + 2, reach)
-    window = jnp.concatenate(
-        [rows[:, :, :, 0:blocks], rows[:, :, :, 1 : blocks + 1], rows[:, :, :, 2 : blocks + 2]],
-        axis=4,
+    stacked = jnp.concatenate(
+        [rows[:, part, :, shift : shift + blocks] for part in range(parts) for shift in range(3)],
+        axis=3,
     )
-    stacked = jnp.moveaxis(window, 1, 3).reshape(pols, chans, blocks, parts * 3 * reach)
     out = jnp.einsum("pcjq,cqn->pcjn", stacked, table, precision=lax.Precision.HIGHEST)
     out = jnp.moveaxis(out.reshape(pols, chans, blocks, parts, reach), 3, 1)
     return out.reshape(pols, parts, chans, blocks * reach)

time: 148 us -> 144 us (0.973)
  waiting for transfers between devices: 2.45 us -> 0.01 us
  local copies, waits for them, and re-layouts: 5.47 us -> 3.95 us
  blocking collectives: 79.2 us -> 80.7 us
    ppermute x1, starting transfers between devices: 1.92 us -> 8.27 us  [on_device(): before = lax.ppermute(trailing, TM, up)]
    ppermute x1, starting transfers between devices: 18.9 us -> 12.6 us  [on_device(): after = lax.ppermute(leading, TM, down)]
    ppermute x1, waiting for transfers between devices: 2.45 us -> 0.01 us  [on_device(): before = lax.ppermute(trailing, TM, up)]
    psum x4, blocking collectives: 25.9 us -> 27.7 us  [psum_tm(): value = lax.psum(value, axis)]
  transfers between devices with their start and end apart: 2 -> 2, of which waited for: 1 -> 0; matrix products, arithmetic and copies ran while one was open for 2% -> 2% of each run, Pallas kernels for 5% -> 5%
where the time goes in v6:
time: 144 us; the launch traced here: 143 us
  blocking collectives  80.7 us (56%)
  matrix products  23.4 us (16%)
  starting transfers between devices  20.9 us (15%)
  Pallas kernels  7.64 us (5%)
  other arithmetic  4.93 us (3%)
  local copies, waits for them, and re-layouts  3.95 us (3%)
    psum x8, blocking collectives, psum_chan(): value = lax.psum(value, axis)  53 us
    psum x4, blocking collectives, psum_tm(): value = lax.psum(value, axis)  27.7 us
    dot_general x4, matrix products, disperse(): jnp.einsum('pcjq,cqn->pcjn', stacked, table, precision=lax.Precision.HIGH...  23.4 us
    ppermute x1, starting transfers between devices, on_device(): after = lax.ppermute(leading, TM, down)  12.6 us
    ppermute x1, starting transfers between devices, on_device(): before = lax.ppermute(trailing, TM, up)  8.27 us
    pallas_call x1, Pallas kernels, merged_tables(): pl.pallas_call(toeplitz_kernel, grid=(count,), in_specs=[pl.BlockSpec((No...  7.64 us
  transfers between devices with their start and end apart: 2, of which 0 were waited for; matrix products, arithmetic and copies ran while one was open for 2% of the time, Pallas kernels for 5%

profile of v6, /device:TPU:1, one launch (start us, length us, event | category | flops | bytes accessed | tf_op | source)
XLA Modules:
  0.0 142.7 jit_solution(3565723228757812840)
XLA Ops:
  0.6 0.8 fusion.80
  1.4 0.9 fusion.79
  2.3 8.3 %collective-permute-start = (f32[2,2,8,768]{3,2,1,0:T(8,128)S(1)}, f32[2,2,8,768]{3,2,1,0:T(8,128)S(1)}, u32[]{:S(2)}, u32[]{:S(2)}) collective-permute-start(f32[2,2,8,768]{3,2,1,0:T(8,128)S(1)} %pad_maximum_fusion.2), channel_id=1, source_target_pairs={{0,8},{8,16},{16,24},{24,32},{32,40},{40,48},{48,56},{56,64},{64,7... | collective-permute-start | bytes 294920 | tf_op jit(solution)/shard_map/ppermute | solution.py:132
  10.6 12.6 %collective-permute-start.1 = (f32[2,2,8,768]{3,2,1,0:T(8,128)S(1)}, f32[2,2,8,768]{3,2,1,0:T(8,128)S(1)}, u32[]{:S(2)}, u32[]{:S(2)}) collective-permute-start(f32[2,2,8,768]{3,2,1,0:T(8,128)S(1)} %pad_maximum_fusion.3), channel_id=1, source_target_pairs={{8,0},{16,8},{24,16},{32,24},{40,32},{48,40},{56,48},{64,56},{72,6... | collective-permute-start | bytes 294920 | tf_op jit(solution)/shard_map/ppermute | solution.py:133
  24.1 0.8 multiply_divide_fusion.3
  25.7 7.6 %shard_map.50 = (f32[8,768,256]{2,1,0:T(8,128)}, f32[8,768,256]{2,1,0:T(8,128)}) custom-call(f32[8,2,2,512]{3,2,1,0:T(2,128)} %select_maximum_fusion.taps_ref), custom_call_target="tpu_custom_call" | custom-call | tf_op jit(solution)/shard_map/pallas_call | solution.py:65
  33.3 0.9 pad_maximum_fusion
  34.5 6.0 %multiply_reduce_fusion.3 = (f32[14,256]{1,0:T(8,128)S(1)}, f32[8,14,256]{2,1,0:T(8,128)S(1)}, f32[2,8,14,256]{3,2,0,1:T(8,128)S(1)}) fusion(f32[2,8,14,768]{3,2,0,1:T(8,128)S(1)} %fusion.41, f32[8,768,256]{2,1,0:T(8,128)} %get-tuple-element.4), kind=kOutput, calls=%fused_computation.20 | convolution fusion | flops 528679424 | bytes 7337984 | tf_op jit(solution)/shard_map/pcjq,cqn->pcjn/dot_general | solution.py:82
  40.6 3.1 %psum.84 = f32[1792]{0:T(1024)S(1)} all-reduce(f32[1792]{0:T(1024)S(1)} %bitcast.262), channel_id=1, replica_groups=mesh['z'=4,'xh'=2,'xl'=4,'yh'=2,'ylo'=4,'core'=2] {'core'}, use_global_device_ids=true, to_apply=%region_3.4 | all-reduce | flops 1792 | bytes 14336 | tf_op jit(solution)/shard_map/psum | solution.py:108
  43.8 7.4 %psum.85 = f32[1792]{0:T(1024)S(1)} all-reduce(f32[1792]{0:T(1024)S(1)} %psum.84), channel_id=1, replica_groups=mesh['z'=4,'xh'=2,'xl'=4,'yh'=2,'ylo'=4,'core'=2] {'ylo'}, use_global_device_ids=true, to_apply=%region_4.5 | all-reduce | flops 1792 | bytes 14336 | tf_op jit(solution)/shard_map/psum | solution.py:108
  51.8 6.0 %multiply_reduce_fusion.1 = (f32[12,256]{1,0:T(8,128)S(1)}, f32[8,12,256]{2,1,0:T(8,128)S(1)}, f32[2,8,12,256]{3,2,0,1:T(8,128)S(1)}) fusion(f32[2,8,12,768]{3,2,0,1:T(8,128)S(1)} %fusion.35, f32[8,768,256]{2,1,0:T(8,128)} %get-tuple-element.4), kind=kOutput, calls=%fused_computation.18 | convolution fusion | flops 453153792 | bytes 7188480 | tf_op jit(solution)/shard_map/pcjq,cqn->pcjn/dot_general | solution.py:82
  57.9 4.5 %psum.86 = f32[1536]{0:T(1024)S(1)} all-reduce(f32[1536]{0:T(1024)S(1)} %bitcast.263), channel_id=1, replica_groups=mesh['z'=4,'xh'=2,'xl'=4,'yh'=2,'ylo'=4,'core'=2] {'core'}, use_global_device_ids=true, to_apply=%region_9.10 | all-reduce | flops 1536 | bytes 12288 | tf_op jit(solution)/shard_map/psum | solution.py:108
  62.5 7.6 %psum.87 = f32[1536]{0:T(1024)S(1)} all-reduce(f32[1536]{0:T(1024)S(1)} %psum.86), channel_id=1, replica_groups=mesh['z'=4,'xh'=2,'xl'=4,'yh'=2,'ylo'=4,'core'=2] {'ylo'}, use_global_device_ids=true, to_apply=%region_10.11 | all-reduce | flops 1536 | bytes 12288 | tf_op jit(solution)/shard_map/psum | solution.py:108
  70.6 7.7 %psum.88 = f32[3,8]{1,0:T(4,128)S(1)} all-reduce(f32[3,8]{1,0:T(4,128)S(1)} %pad_maximum_fusion.4), channel_id=1, replica_groups=mesh['z'=4,'xh'=2,'xl'=4,'yh'=2,'ylo'=4,'core'=2] {'yh'}, use_global_device_ids=true, to_apply=%region_16.17 | all-reduce | flops 24 | bytes 192 | tf_op jit(solution)/shard_map/psum | solution.py:102
  78.3 6.0 %psum.89 = f32[3,8]{1,0:T(4,128)S(1)} all-reduce(f32[3,8]{1,0:T(4,128)S(1)} %psum.88), channel_id=1, replica_groups=mesh['z'=4,'xh'=2,'xl'=4,'yh'=2,'ylo'=4,'core'=2] {'xl'}, use_global_device_ids=true, to_apply=%region_17.18 | all-reduce | flops 24 | bytes 192 | tf_op jit(solution)/shard_map/psum | solution.py:102
  84.3 3.8 %psum.90 = f32[3,8]{1,0:T(4,128)S(1)} all-reduce(f32[3,8]{1,0:T(4,128)S(1)} %psum.89), channel_id=1, replica_groups=mesh['z'=4,'xh'=2,'xl'=4,'yh'=2,'ylo'=4,'core'=2] {'xh'}, use_global_device_ids=true, to_apply=%region_18.19 | all-reduce | flops 24 | bytes 192 | tf_op jit(solution)/shard_map/psum | solution.py:102
  88.0 10.3 %psum.91 = f32[3,8]{1,0:T(4,128)S(1)} all-reduce(f32[3,8]{1,0:T(4,128)S(1)} %psum.90), channel_id=1, replica_groups=mesh['z'=4,'xh'=2,'xl'=4,'yh'=2,'ylo'=4,'core'=2] {'z'}, use_global_device_ids=true, to_apply=%region_19.20 | all-reduce | flops 24 | bytes 192 | tf_op jit(solution)/shard_map/psum | solution.py:102
  98.5 10.6 %psum.92 = f32[1536]{0:T(1024)S(1)} all-reduce(f32[1536]{0:T(1024)S(1)} %get-tuple-element.12), channel_id=1, replica_groups=mesh['z'=4,'xh'=2,'xl'=4,'yh'=2,'ylo'=4,'core'=2] {'core'}, use_global_device_ids=true, to_apply=%region_21.22 | all-reduce | flops 1536 | bytes 12288 | tf_op jit(solution)/shard_map/psum | solution.py:108
  109.1 8.5 %psum.93 = f32[1536]{0:T(1024)S(1)} all-reduce(f32[1536]{0:T(1024)S(1)} %psum.92), channel_id=1, replica_groups=mesh['z'=4,'xh'=2,'xl'=4,'yh'=2,'ylo'=4,'core'=2] {'ylo'}, use_global_device_ids=true, to_apply=%region_22.23 | all-reduce | flops 1536 | bytes 12288 | tf_op jit(solution)/shard_map/psum | solution.py:108
  118.1 5.9 %fusion.20 = f32[2,8,10,256]{3,2,0,1:T(8,128)S(1)} fusion(f32[2,8,10,768]{3,2,0,1:T(8,128)S(1)} %fusion.29, f32[8,768,256]{2,1,0:T(8,128)} %get-tuple-element.5), kind=kOutput, calls=%fused_computation.12 | convolution fusion | flops 377487360 | bytes 6946816 | tf_op jit(solution)/shard_map/pcjq,cqn->pcjn/dot_general | solution.py:82
  124.1 4.5 %psum.94 = f32[1280]{0:T(1024)S(1)} all-reduce(f32[1280]{0:T(1024)S(1)} %bitcast.264), channel_id=1, replica_groups=mesh['z'=4,'xh'=2,'xl'=4,'yh'=2,'ylo'=4,'core'=2] {'core'}, use_global_device_ids=true, to_apply=%region_25.26 | all-reduce | flops 1280 | bytes 10240 | tf_op jit(solution)/shard_map/psum | solution.py:108
  128.7 6.8 %psum.95 = f32[1280]{0:T(1024)S(1)} all-reduce(f32[1280]{0:T(1024)S(1)} %psum.94), channel_id=1, replica_groups=mesh['z'=4,'xh'=2,'xl'=4,'yh'=2,'ylo'=4,'core'=2] {'ylo'}, use_global_device_ids=true, to_apply=%region_26.27 | all-reduce | flops 1280 | bytes 10240 | tf_op jit(solution)/shard_map/psum | solution.py:108
  135.9 5.4 %fusion.23 = f32[2,2,8,8,128]{4,3,1,0,2:T(8,128)S(1)} fusion(f32[2,8,8,768]{3,2,0,1:T(8,128)S(1)} %fusion.47, f32[8,768,256]{2,1,0:T(8,128)} %get-tuple-element.5), kind=kOutput, calls=%fused_computation.13 | convolution fusion | flops 301989888 | bytes 6815744 | tf_op jit(solution)/shard_map/pcjq,cqn->pcjn/dot_general | solution.py:82
  141.3 0.7 copy.185
  (78 shorter events, 4.7 us)
Async XLA Ops:
  2.3 31.0 %collective-permute-start = (f32[2,2,8,768]{3,2,1,0:T(8,128)S(1)}, f32[2,2,8,768]{3,2,1,0:T(8,128)S(1)}, u32[]{:S(2)}, u32[]{:S(2)}) collective-permute-start(f32[2,2,8,768]{3,2,1,0:T(8,128)S(1)} %pad_maximum_fusion.2), channel_id=1, source_target_pairs={{0,8},{8,16},{16,24},{24,32},{32,40},{40,48},{48,56},{56,64},{64,7... | collective-permute-start | bytes 294920 | tf_op jit(solution)/shard_map/ppermute | solution.py:132
  10.6 22.7 %collective-permute-start.1 = (f32[2,2,8,768]{3,2,1,0:T(8,128)S(1)}, f32[2,2,8,768]{3,2,1,0:T(8,128)S(1)}, u32[]{:S(2)}, u32[]{:S(2)}) collective-permute-start(f32[2,2,8,768]{3,2,1,0:T(8,128)S(1)} %pad_maximum_fusion.3), channel_id=1, source_target_pairs={{8,0},{16,8},{24,16},{32,24},{40,32},{48,40},{56,48},{64,56},{72,6... | collective-permute-start | bytes 294920 | tf_op jit(solution)/shard_map/ppermute | solution.py:133
  51.2 19.2 %copy-start = (f32[1,2,2,8,1024]{4,3,2,1,0:T(8,128)S(1)}, f32[1,2,2,8,1024]{4,3,2,1,0:T(8,128)}, u32[]{:S(2)}) copy-start(f32[1,2,2,8,1024]{4,3,2,1,0:T(8,128)} %param.4) | copy-start | bytes 393220

commit v7 on v6

--- a/solution.py
+++ b/solution.py
@@ -34,12 +34,13 @@
 
 
 def toeplitz_kernel(taps_ref, forward_ref, backward_ref):
-    for sign, out_ref in enumerate((forward_ref, backward_ref)):
-        toeplitz_fill(taps_ref.at[sign], out_ref)
+    for slot in range(taps_ref.shape[0]):
+        for sign, out_ref in enumerate((forward_ref, backward_ref)):
+            toeplitz_fill(taps_ref.at[slot, sign], out_ref.at[slot])
 
 
 def toeplitz_fill(taps_ref, out_ref):
-    reach = out_ref.shape[1] // 2
+    reach = out_ref.shape[-1] // 2
     for block in range(3):
         start = reach * (2 - block)
         parts = []
@@ -61,11 +62,12 @@
     padded = jnp.pad(taps, ((0, 0), (0, 0), (0, 0), (reach, reach - 1)))
     count = taps.shape[0]
     table = jax.ShapeDtypeStruct((count, 6 * reach, 2 * reach), jnp.float32)
-    block = pl.BlockSpec((None, 6 * reach, 2 * reach), lambda s: (s, 0, 0))
+    per = 2
+    block = pl.BlockSpec((per, 6 * reach, 2 * reach), lambda s: (s, 0, 0))
     return pl.pallas_call(
         toeplitz_kernel,
-        grid=(count,),
-        in_specs=[pl.BlockSpec((None, 2, 2, 4 * reach), lambda s: (s, 0, 0, 0))],
+        grid=(count // per,),
+        in_specs=[pl.BlockSpec((per, 2, 2, 4 * reach), lambda s: (s, 0, 0, 0))],
         out_specs=(block, block),
         out_shape=(table, table),
     )(padded)

time: 144 us -> 143 us (level)
  no operation moved by 1% of the time
where the time goes in v7:
time: 143 us; the launch traced here: 142 us
  blocking collectives  80.7 us (56%)
  matrix products  23.4 us (16%)
  starting transfers between devices  20.9 us (15%)
  Pallas kernels  6.63 us (5%)
  other arithmetic  4.93 us (3%)
  local copies, waits for them, and re-layouts  3.95 us (3%)
    psum x8, blocking collectives, psum_chan(): value = lax.psum(value, axis)  53 us
    psum x4, blocking collectives, psum_tm(): value = lax.psum(value, axis)  27.8 us
    dot_general x4, matrix products, disperse(): jnp.einsum('pcjq,cqn->pcjn', stacked, table, precision=lax.Precision.HIGH...  23.4 us
    ppermute x1, starting transfers between devices, on_device(): after = lax.ppermute(leading, TM, down)  12.6 us
    ppermute x1, starting transfers between devices, on_device(): before = lax.ppermute(trailing, TM, up)  8.27 us
    pallas_call x1, Pallas kernels, merged_tables(): pl.pallas_call(toeplitz_kernel, grid=(count // per,), in_specs=[pl.BlockS...  6.63 us
  transfers between devices with their start and end apart: 2, of which 0 were waited for; matrix products, arithmetic and copies ran while one was open for 2% of the time, Pallas kernels for 5%

profile of v7, /device:TPU:1, one launch (start us, length us, event | category | flops | bytes accessed | tf_op | source)
XLA Modules:
  0.0 141.7 jit_solution(10611744150855034407)
XLA Ops:
  0.6 0.8 fusion.80
  1.4 0.9 fusion.79
  2.3 8.3 %collective-permute-start = (f32[2,2,8,768]{3,2,1,0:T(8,128)S(1)}, f32[2,2,8,768]{3,2,1,0:T(8,128)S(1)}, u32[]{:S(2)}, u32[]{:S(2)}) collective-permute-start(f32[2,2,8,768]{3,2,1,0:T(8,128)S(1)} %pad_maximum_fusion.2), channel_id=1, source_target_pairs={{0,8},{8,16},{16,24},{24,32},{32,40},{40,48},{48,56},{56,64},{64,7... | collective-permute-start | bytes 294920 | tf_op jit(solution)/shard_map/ppermute | solution.py:134
  10.6 12.6 %collective-permute-start.1 = (f32[2,2,8,768]{3,2,1,0:T(8,128)S(1)}, f32[2,2,8,768]{3,2,1,0:T(8,128)S(1)}, u32[]{:S(2)}, u32[]{:S(2)}) collective-permute-start(f32[2,2,8,768]{3,2,1,0:T(8,128)S(1)} %pad_maximum_fusion.3), channel_id=1, source_target_pairs={{8,0},{16,8},{24,16},{32,24},{40,32},{48,40},{56,48},{64,56},{72,6... | collective-permute-start | bytes 294920 | tf_op jit(solution)/shard_map/ppermute | solution.py:135
  24.1 0.8 multiply_divide_fusion.3
  25.7 6.6 %shard_map.50 = (f32[8,768,256]{2,1,0:T(8,128)}, f32[8,768,256]{2,1,0:T(8,128)}) custom-call(f32[8,2,2,512]{3,2,1,0:T(2,128)} %select_maximum_fusion.taps_ref), custom_call_target="tpu_custom_call" | custom-call | tf_op jit(solution)/shard_map/pallas_call | solution.py:67
  32.3 0.9 pad_maximum_fusion
  33.5 6.0 %multiply_reduce_fusion.3 = (f32[14,256]{1,0:T(8,128)S(1)}, f32[8,14,256]{2,1,0:T(8,128)S(1)}, f32[2,8,14,256]{3,2,0,1:T(8,128)S(1)}) fusion(f32[2,8,14,768]{3,2,0,1:T(8,128)S(1)} %fusion.41, f32[8,768,256]{2,1,0:T(8,128)} %get-tuple-element.4), kind=kOutput, calls=%fused_computation.20 | convolution fusion | flops 528679424 | bytes 7337984 | tf_op jit(solution)/shard_map/pcjq,cqn->pcjn/dot_general | solution.py:84
  39.6 3.1 %psum.84 = f32[1792]{0:T(1024)S(1)} all-reduce(f32[1792]{0:T(1024)S(1)} %bitcast.262), channel_id=1, replica_groups=mesh['z'=4,'xh'=2,'xl'=4,'yh'=2,'ylo'=4,'core'=2] {'core'}, use_global_device_ids=true, to_apply=%region_3.4 | all-reduce | flops 1792 | bytes 14336 | tf_op jit(solution)/shard_map/psum | solution.py:110
  42.7 7.4 %psum.85 = f32[1792]{0:T(1024)S(1)} all-reduce(f32[1792]{0:T(1024)S(1)} %psum.84), channel_id=1, replica_groups=mesh['z'=4,'xh'=2,'xl'=4,'yh'=2,'ylo'=4,'core'=2] {'ylo'}, use_global_device_ids=true, to_apply=%region_4.5 | all-reduce | flops 1792 | bytes 14336 | tf_op jit(solution)/shard_map/psum | solution.py:110
  50.8 6.0 %multiply_reduce_fusion.1 = (f32[12,256]{1,0:T(8,128)S(1)}, f32[8,12,256]{2,1,0:T(8,128)S(1)}, f32[2,8,12,256]{3,2,0,1:T(8,128)S(1)}) fusion(f32[2,8,12,768]{3,2,0,1:T(8,128)S(1)} %fusion.35, f32[8,768,256]{2,1,0:T(8,128)} %get-tuple-element.4), kind=kOutput, calls=%fused_computation.18 | convolution fusion | flops 453153792 | bytes 7188480 | tf_op jit(solution)/shard_map/pcjq,cqn->pcjn/dot_general | solution.py:84
  56.9 4.5 %psum.86 = f32[1536]{0:T(1024)S(1)} all-reduce(f32[1536]{0:T(1024)S(1)} %bitcast.263), channel_id=1, replica_groups=mesh['z'=4,'xh'=2,'xl'=4,'yh'=2,'ylo'=4,'core'=2] {'core'}, use_global_device_ids=true, to_apply=%region_9.10 | all-reduce | flops 1536 | bytes 12288 | tf_op jit(solution)/shard_map/psum | solution.py:110
  61.4 7.6 %psum.87 = f32[1536]{0:T(1024)S(1)} all-reduce(f32[1536]{0:T(1024)S(1)} %psum.86), channel_id=1, replica_groups=mesh['z'=4,'xh'=2,'xl'=4,'yh'=2,'ylo'=4,'core'=2] {'ylo'}, use_global_device_ids=true, to_apply=%region_10.11 | all-reduce | flops 1536 | bytes 12288 | tf_op jit(solution)/shard_map/psum | solution.py:110
  69.6 7.7 %psum.88 = f32[3,8]{1,0:T(4,128)S(1)} all-reduce(f32[3,8]{1,0:T(4,128)S(1)} %pad_maximum_fusion.4), channel_id=1, replica_groups=mesh['z'=4,'xh'=2,'xl'=4,'yh'=2,'ylo'=4,'core'=2] {'yh'}, use_global_device_ids=true, to_apply=%region_16.17 | all-reduce | flops 24 | bytes 192 | tf_op jit(solution)/shard_map/psum | solution.py:104
  77.3 6.0 %psum.89 = f32[3,8]{1,0:T(4,128)S(1)} all-reduce(f32[3,8]{1,0:T(4,128)S(1)} %psum.88), channel_id=1, replica_groups=mesh['z'=4,'xh'=2,'xl'=4,'yh'=2,'ylo'=4,'core'=2] {'xl'}, use_global_device_ids=true, to_apply=%region_17.18 | all-reduce | flops 24 | bytes 192 | tf_op jit(solution)/shard_map/psum | solution.py:104
  83.3 3.8 %psum.90 = f32[3,8]{1,0:T(4,128)S(1)} all-reduce(f32[3,8]{1,0:T(4,128)S(1)} %psum.89), channel_id=1, replica_groups=mesh['z'=4,'xh'=2,'xl'=4,'yh'=2,'ylo'=4,'core'=2] {'xh'}, use_global_device_ids=true, to_apply=%region_18.19 | all-reduce | flops 24 | bytes 192 | tf_op jit(solution)/shard_map/psum | solution.py:104
  87.0 10.3 %psum.91 = f32[3,8]{1,0:T(4,128)S(1)} all-reduce(f32[3,8]{1,0:T(4,128)S(1)} %psum.90), channel_id=1, replica_groups=mesh['z'=4,'xh'=2,'xl'=4,'yh'=2,'ylo'=4,'core'=2] {'z'}, use_global_device_ids=true, to_apply=%region_19.20 | all-reduce | flops 24 | bytes 192 | tf_op jit(solution)/shard_map/psum | solution.py:104
  97.5 10.6 %psum.92 = f32[1536]{0:T(1024)S(1)} all-reduce(f32[1536]{0:T(1024)S(1)} %get-tuple-element.12), channel_id=1, replica_groups=mesh['z'=4,'xh'=2,'xl'=4,'yh'=2,'ylo'=4,'core'=2] {'core'}, use_global_device_ids=true, to_apply=%region_21.22 | all-reduce | flops 1536 | bytes 12288 | tf_op jit(solution)/shard_map/psum | solution.py:110
  108.2 8.5 %psum.93 = f32[1536]{0:T(1024)S(1)} all-reduce(f32[1536]{0:T(1024)S(1)} %psum.92), channel_id=1, replica_groups=mesh['z'=4,'xh'=2,'xl'=4,'yh'=2,'ylo'=4,'core'=2] {'ylo'}, use_global_device_ids=true, to_apply=%region_22.23 | all-reduce | flops 1536 | bytes 12288 | tf_op jit(solution)/shard_map/psum | solution.py:110
  117.1 5.9 %fusion.20 = f32[2,8,10,256]{3,2,0,1:T(8,128)S(1)} fusion(f32[2,8,10,768]{3,2,0,1:T(8,128)S(1)} %fusion.29, f32[8,768,256]{2,1,0:T(8,128)} %get-tuple-element.5), kind=kOutput, calls=%fused_computation.12 | convolution fusion | flops 377487360 | bytes 6946816 | tf_op jit(solution)/shard_map/pcjq,cqn->pcjn/dot_general | solution.py:84
  123.2 4.5 %psum.94 = f32[1280]{0:T(1024)S(1)} all-reduce(f32[1280]{0:T(1024)S(1)} %bitcast.264), channel_id=1, replica_groups=mesh['z'=4,'xh'=2,'xl'=4,'yh'=2,'ylo'=4,'core'=2] {'core'}, use_global_device_ids=true, to_apply=%region_25.26 | all-reduce | flops 1280 | bytes 10240 | tf_op jit(solution)/shard_map/psum | solution.py:110
  127.7 6.8 %psum.95 = f32[1280]{0:T(1024)S(1)} all-reduce(f32[1280]{0:T(1024)S(1)} %psum.94), channel_id=1, replica_groups=mesh['z'=4,'xh'=2,'xl'=4,'yh'=2,'ylo'=4,'core'=2] {'ylo'}, use_global_device_ids=true, to_apply=%region_26.27 | all-reduce | flops 1280 | bytes 10240 | tf_op jit(solution)/shard_map/psum | solution.py:110
  134.9 5.4 %fusion.23 = f32[2,2,8,8,128]{4,3,1,0,2:T(8,128)S(1)} fusion(f32[2,8,8,768]{3,2,0,1:T(8,128)S(1)} %fusion.47, f32[8,768,256]{2,1,0:T(8,128)} %get-tuple-element.5), kind=kOutput, calls=%fused_computation.13 | convolution fusion | flops 301989888 | bytes 6815744 | tf_op jit(solution)/shard_map/pcjq,cqn->pcjn/dot_general | solution.py:84
  140.3 0.7 copy.185
  (78 shorter events, 4.7 us)
Async XLA Ops:
  2.3 30.0 %collective-permute-start = (f32[2,2,8,768]{3,2,1,0:T(8,128)S(1)}, f32[2,2,8,768]{3,2,1,0:T(8,128)S(1)}, u32[]{:S(2)}, u32[]{:S(2)}) collective-permute-start(f32[2,2,8,768]{3,2,1,0:T(8,128)S(1)} %pad_maximum_fusion.2), channel_id=1, source_target_pairs={{0,8},{8,16},{16,24},{24,32},{32,40},{40,48},{48,56},{56,64},{64,7... | collective-permute-start | bytes 294920 | tf_op jit(solution)/shard_map/ppermute | solution.py:134
  10.6 21.7 %collective-permute-start.1 = (f32[2,2,8,768]{3,2,1,0:T(8,128)S(1)}, f32[2,2,8,768]{3,2,1,0:T(8,128)S(1)}, u32[]{:S(2)}, u32[]{:S(2)}) collective-permute-start(f32[2,2,8,768]{3,2,1,0:T(8,128)S(1)} %pad_maximum_fusion.3), channel_id=1, source_target_pairs={{8,0},{16,8},{24,16},{32,24},{40,32},{48,40},{56,48},{64,56},{72,6... | collective-permute-start | bytes 294920 | tf_op jit(solution)/shard_map/ppermute | solution.py:135
  50.2 19.3 %copy-start = (f32[1,2,2,8,1024]{4,3,2,1,0:T(8,128)S(1)}, f32[1,2,2,8,1024]{4,3,2,1,0:T(8,128)}, u32[]{:S(2)}) copy-start(f32[1,2,2,8,1024]{4,3,2,1,0:T(8,128)} %param.4) | copy-start | bytes 393220

commit v8 on v7

--- a/solution.py
+++ b/solution.py
@@ -50,20 +50,17 @@
             parts.append(rolled[:, reach:])
         real, imag = parts
         rows = slice(block * reach, (block + 1) * reach)
-        low = slice(3 * reach + block * reach, 3 * reach + (block + 1) * reach)
         out_ref[rows, :reach] = real
         out_ref[rows, reach:] = imag
-        out_ref[low, :reach] = -imag
-        out_ref[low, reach:] = real
 
 
 def merged_tables(channel_ids, reach, channels):
     taps = jnp.stack([tap_rows(channel_ids, 1.0, reach, channels), tap_rows(channel_ids, -1.0, reach, channels)], axis=1)
     padded = jnp.pad(taps, ((0, 0), (0, 0), (0, 0), (reach, reach - 1)))
     count = taps.shape[0]
-    table = jax.ShapeDtypeStruct((count, 6 * reach, 2 * reach), jnp.float32)
+    table = jax.ShapeDtypeStruct((count, 3 * reach, 2 * reach), jnp.float32)
     per = 2
-    block = pl.BlockSpec((per, 6 * reach, 2 * reach), lambda s: (s, 0, 0))
+    block = pl.BlockSpec((per, 3 * reach, 2 * reach), lambda s: (s, 0, 0))
     return pl.pallas_call(
         toeplitz_kernel,
         grid=(count // per,),
@@ -77,13 +74,12 @@
     pols, parts, chans, segment_length = ext.shape
     blocks = segment_length // reach - 2
     rows = ext.reshape(pols, parts, chans, blocks + 2, reach)
-    stacked = jnp.concatenate(
-        [rows[:, part, :, shift : shift + blocks] for part in range(parts) for shift in range(3)],
-        axis=3,
-    )
-    out = jnp.einsum("pcjq,cqn->pcjn", stacked, table, precision=lax.Precision.HIGHEST)
-    out = jnp.moveaxis(out.reshape(pols, chans, blocks, parts, reach), 3, 1)
-    return out.reshape(pols, parts, chans, blocks * reach)
+    stacked = jnp.concatenate([rows[:, :, :, shift : shift + blocks] for shift in range(3)], axis=4)
+    out = jnp.einsum("pacjq,cqn->pacjn", stacked, table, precision=lax.Precision.HIGHEST)
+    from_re, from_im = out[:, 0], out[:, 1]
+    real = from_re[..., :reach] - from_im[..., reach:]
+    imag = from_re[..., reach:] + from_im[..., :reach]
+    return jnp.stack([real, imag], axis=1).reshape(pols, parts, chans, blocks * reach)
 
 
 def rotate(ext, sign, own, total):

time: 143 us -> 139 us (0.972)
  matrix products: 23.4 us -> 10.1 us
  other arithmetic: 4.93 us -> 11.8 us
  waiting for transfers between devices: 0.01 us -> 4.55 us
  blocking collectives: 80.7 us -> 77.8 us
    dot_general x4, matrix products: 23.4 us -> 10.1 us  [disperse(): jnp.einsum('pacjq,cqn->pacjn', stacked, table, precision=lax.Precision.HI...]
    ppermute x1, starting transfers between devices: 8.27 us -> 1.92 us  [on_device(): before = lax.ppermute(trailing, TM, up)]
    ppermute x1, starting transfers between devices: 12.6 us -> 18.9 us  [on_device(): after = lax.ppermute(leading, TM, down)]
    ppermute x1, waiting for transfers between devices: 0.01 us -> 4.55 us  [on_device(): before = lax.ppermute(trailing, TM, up)]
    psum x4, blocking collectives: 27.8 us -> 24.3 us  [psum_tm(): value = lax.psum(value, axis)]
    reduce_sum x4, other arithmetic: 0.28 us -> 2.83 us  [nonlinear(): total = psum_chan(jnp.sum(own, axis=0))]
  transfers between devices with their start and end apart: 2 -> 2, of which waited for: 0 -> 1; matrix products, arithmetic and copies ran while one was open for 2% -> 2% of each run, Pallas kernels for 5% -> 4%
where the time goes in v8:
time: 139 us; the launch traced here: 137 us
  blocking collectives  77.8 us (56%)
  starting transfers between devices  20.9 us (15%)
  other arithmetic  11.8 us (8%)
  matrix products  10.1 us (7%)
  Pallas kernels  5.55 us (4%)
  local copies, waits for them, and re-layouts  5.21 us (4%)
  waiting for transfers between devices  4.55 us (3%)
    psum x8, blocking collectives, psum_chan(): value = lax.psum(value, axis)  53.5 us
    psum x4, blocking collectives, psum_tm(): value = lax.psum(value, axis)  24.3 us
    ppermute x1, starting transfers between devices, on_device(): after = lax.ppermute(leading, TM, down)  18.9 us
    dot_general x4, matrix products, disperse(): jnp.einsum('pacjq,cqn->pacjn', stacked, table, precision=lax.Precision.HI...  10.1 us
    pallas_call x1, Pallas kernels, merged_tables(): pl.pallas_call(toeplitz_kernel, grid=(count // per,), in_specs=[pl.BlockS...  5.55 us
    ppermute x1, waiting for transfers between devices, on_device(): before = lax.ppermute(trailing, TM, up)  4.55 us
    reduce_sum x4, other arithmetic, nonlinear(): total = psum_chan(jnp.sum(own, axis=0))  2.83 us
  transfers between devices with their start and end apart: 2, of which 1 were waited for; matrix products, arithmetic and copies ran while one was open for 2% of the time, Pallas kernels for 4%

profile of v8, /device:TPU:1, one launch (start us, length us, event | category | flops | bytes accessed | tf_op | source)
XLA Modules:
  0.0 137.0 jit_solution(16878143940031047966)
XLA Ops:
  2.5 18.9 %collective-permute-start.1 = (f32[2,2,8,768]{3,2,0,1:T(8,128)S(1)}, f32[2,2,8,768]{3,2,0,1:T(8,128)S(1)}, u32[]{:S(2)}, u32[]{:S(2)}) collective-permute-start(f32[2,2,8,768]{3,2,0,1:T(8,128)S(1)} %pad_maximum_fusion.6), channel_id=1, source_target_pairs={{8,0},{16,8},{24,16},{32,24},{40,32},{48,40},{56,48},{64,56},{72,6... | collective-permute-start | bytes 294920 | tf_op jit(solution)/shard_map/ppermute | solution.py:131
  21.4 1.9 %collective-permute-start = (f32[2,2,8,768]{3,2,0,1:T(8,128)S(1)}, f32[2,2,8,768]{3,2,0,1:T(8,128)S(1)}, u32[]{:S(2)}, u32[]{:S(2)}) collective-permute-start(f32[2,2,8,768]{3,2,0,1:T(8,128)S(1)} %pad_maximum_fusion.5), channel_id=1, source_target_pairs={{0,8},{8,16},{16,24},{24,32},{32,40},{40,48},{48,56},{56,64},{64,7... | collective-permute-start | bytes 294920 | tf_op jit(solution)/shard_map/ppermute | solution.py:130
  25.8 5.5 %shard_map.50 = (f32[8,384,256]{2,1,0:T(8,128)}, f32[8,384,256]{2,1,0:T(8,128)}) custom-call(f32[8,2,2,512]{3,2,1,0:T(2,128)} %select_maximum_fusion.taps_ref), custom_call_target="tpu_custom_call" | custom-call | tf_op jit(solution)/shard_map/pallas_call | solution.py:64
  31.4 4.5 %collective-permute-done = f32[2,2,8,768]{3,2,0,1:T(8,128)S(1)} collective-permute-done((f32[2,2,8,768]{3,2,0,1:T(8,128)S(1)}, f32[2,2,8,768]{3,2,0,1:T(8,128)S(1)}, u32[]{:S(2)}, u32[]{:S(2)}) %collective-permute-start) | collective-permute-done | bytes 98336 | tf_op jit(solution)/shard_map/ppermute | solution.py:130
  37.0 3.9 %fusion.8 = f32[2,2,8,14,256]{4,3,1,0,2:T(8,128)S(1)} fusion(f32[8,384,256]{2,1,0:T(8,128)} %get-tuple-element.4, f32[2,2,8,14,128]{4,3,2,1,0:T(8,128)S(1)} %get-tuple-element.60, f32[2,2,8,14,128]{4,3,2,1,0:T(8,128)S(1)} %get-tuple-element.59, f32[2,2,8,14,128]{4,3,2,1,0:T(8,128)S(1)} %get-tuple-element.58), kind=kOutput, calls=%fused_computation.8 | convolution fusion | flops 528826368 | bytes 4292608 | tf_op jit(solution)/shard_map/pacjq,cqn->pacjn/dot_general | solution.py:78
  41.9 3.5 %psum.84 = f32[1792]{0:T(1024)S(1)} all-reduce(f32[1792]{0:T(1024)S(1)} %get-tuple-element.12), channel_id=1, replica_groups=mesh['z'=4,'xh'=2,'xl'=4,'yh'=2,'ylo'=4,'core'=2] {'core'}, use_global_device_ids=true, to_apply=%region_2.3 | all-reduce | flops 1792 | bytes 14336 | tf_op jit(solution)/shard_map/psum | solution.py:106
  45.4 8.7 %psum.85 = f32[1792]{0:T(1024)S(1)} all-reduce(f32[1792]{0:T(1024)S(1)} %psum.84), channel_id=1, replica_groups=mesh['z'=4,'xh'=2,'xl'=4,'yh'=2,'ylo'=4,'core'=2] {'ylo'}, use_global_device_ids=true, to_apply=%region_3.4 | all-reduce | flops 1792 | bytes 14336 | tf_op jit(solution)/shard_map/psum | solution.py:106
  54.1 1.0 fusion.38
  55.4 2.1 %fusion.11 = f32[2,2,8,12,256]{4,3,1,0,2:T(8,128)S(1)} fusion(f32[8,384,256]{2,1,0:T(8,128)S(1)} %copy-done, f32[2,2,8,12,128]{4,3,1,0,2:T(8,128)S(1)} %get-tuple-element.56, f32[2,2,8,12,128]{4,3,1,0,2:T(8,128)S(1)} %get-tuple-element.57, f32[2,2,8,12,128]{4,3,1,0,2:T(8,128)S(1)} %get-tuple-element.55), kind=kOutput, calls=%fused_computation.9 | convolution fusion | flops 453279744 | bytes 4128768 | tf_op jit(solution)/shard_map/pacjq,cqn->pacjn/dot_general | solution.py:78
  58.4 4.6 %psum.86 = f32[1536]{0:T(1024)S(1)} all-reduce(f32[1536]{0:T(1024)S(1)} %get-tuple-element.18), channel_id=1, replica_groups=mesh['z'=4,'xh'=2,'xl'=4,'yh'=2,'ylo'=4,'core'=2] {'core'}, use_global_device_ids=true, to_apply=%region_6.7 | all-reduce | flops 1536 | bytes 12288 | tf_op jit(solution)/shard_map/psum | solution.py:106
  63.0 6.8 %psum.87 = f32[1536]{0:T(1024)S(1)} all-reduce(f32[1536]{0:T(1024)S(1)} %psum.86), channel_id=1, replica_groups=mesh['z'=4,'xh'=2,'xl'=4,'yh'=2,'ylo'=4,'core'=2] {'ylo'}, use_global_device_ids=true, to_apply=%region_7.8 | all-reduce | flops 1536 | bytes 12288 | tf_op jit(solution)/shard_map/psum | solution.py:106
  70.0 1.0 multiply_subtract_fusion
  71.0 1.1 multiply_reduce_fusion.8
  72.1 7.7 %psum.88 = f32[3,8]{1,0:T(4,128)S(1)} all-reduce(f32[3,8]{1,0:T(4,128)S(1)} %pad_maximum_fusion.7), channel_id=1, replica_groups=mesh['z'=4,'xh'=2,'xl'=4,'yh'=2,'ylo'=4,'core'=2] {'yh'}, use_global_device_ids=true, to_apply=%region_12.13 | all-reduce | flops 24 | bytes 192 | tf_op jit(solution)/shard_map/psum | solution.py:100
  79.8 6.0 %psum.89 = f32[3,8]{1,0:T(4,128)S(1)} all-reduce(f32[3,8]{1,0:T(4,128)S(1)} %psum.88), channel_id=1, replica_groups=mesh['z'=4,'xh'=2,'xl'=4,'yh'=2,'ylo'=4,'core'=2] {'xl'}, use_global_device_ids=true, to_apply=%region_13.14 | all-reduce | flops 24 | bytes 192 | tf_op jit(solution)/shard_map/psum | solution.py:100
  85.7 3.8 %psum.90 = f32[3,8]{1,0:T(4,128)S(1)} all-reduce(f32[3,8]{1,0:T(4,128)S(1)} %psum.89), channel_id=1, replica_groups=mesh['z'=4,'xh'=2,'xl'=4,'yh'=2,'ylo'=4,'core'=2] {'xh'}, use_global_device_ids=true, to_apply=%region_14.15 | all-reduce | flops 24 | bytes 192 | tf_op jit(solution)/shard_map/psum | solution.py:100
  89.5 6.9 %psum.91 = f32[3,8]{1,0:T(4,128)S(1)} all-reduce(f32[3,8]{1,0:T(4,128)S(1)} %psum.90), channel_id=1, replica_groups=mesh['z'=4,'xh'=2,'xl'=4,'yh'=2,'ylo'=4,'core'=2] {'z'}, use_global_device_ids=true, to_apply=%region_15.16 | all-reduce | flops 24 | bytes 192 | tf_op jit(solution)/shard_map/psum | solution.py:100
  97.2 1.5 %multiply_reduce_fusion.3 = (f32[1536]{0:T(1024)}, f32[8,1536]{1,0:T(8,128)S(1)}, f32[2,2,8,1536]{3,2,0,1:T(8,128)}, f32[2,2,8,1536]{3,2,0,1:T(8,128)}) fusion(f32[8]{0:T(128)S(1)} %get-tuple-element.80, f32[2,2,8,256]{3,2,0,1:T(8,128)S(1)} %slice-done, f32[2,2,8,1024]{3,2,0,1:T(8,128)S(1)} %bitcast.155, f32[2,2,8,256]{3,2,0,1:T(8,128)S(1)} %slice.251, ...), kind=kLoop, calls=%fused_computation.45 | loop fusion | flops 428544 | bytes 841792 | tf_op jit(solution)/shard_map/reduce_sum | solution.py:119
  98.6 10.2 %psum.92 = f32[1536]{0:T(1024)S(1)} all-reduce(f32[1536]{0:T(1024)} %get-tuple-element.14), channel_id=1, replica_groups=mesh['z'=4,'xh'=2,'xl'=4,'yh'=2,'ylo'=4,'core'=2] {'core'}, use_global_device_ids=true, to_apply=%region_17.18 | all-reduce | flops 1536 | bytes 12288 | tf_op jit(solution)/shard_map/psum | solution.py:106
  108.9 8.4 %psum.93 = f32[1536]{0:T(1024)S(1)} all-reduce(f32[1536]{0:T(1024)S(1)} %psum.92), channel_id=1, replica_groups=mesh['z'=4,'xh'=2,'xl'=4,'yh'=2,'ylo'=4,'core'=2] {'ylo'}, use_global_device_ids=true, to_apply=%region_18.19 | all-reduce | flops 1536 | bytes 12288 | tf_op jit(solution)/shard_map/psum | solution.py:106
  120.2 2.1 %fusion.14 = f32[2,2,8,10,256]{4,3,1,0,2:T(8,128)S(1)} fusion(f32[8,384,256]{2,1,0:T(8,128)S(1)} %copy-done.1, f32[2,2,8,10,128]{4,3,1,0,2:T(8,128)S(1)} %get-tuple-element.53, f32[2,2,8,10,128]{4,3,1,0,2:T(8,128)S(1)} %get-tuple-element.54, f32[2,2,8,10,128]{4,3,1,0,2:T(8,128)S(1)} %get-tuple-element.52), kind=kOutput, calls=%fused_computation.10 | convolution fusion | flops 377733120 | bytes 3964928 | tf_op jit(solution)/shard_map/pacjq,cqn->pacjn/dot_general | solution.py:78
  122.5 4.5 %psum.94 = f32[1280]{0:T(1024)S(1)} all-reduce(f32[1280]{0:T(1024)S(1)} %get-tuple-element.20), channel_id=1, replica_groups=mesh['z'=4,'xh'=2,'xl'=4,'yh'=2,'ylo'=4,'core'=2] {'core'}, use_global_device_ids=true, to_apply=%region_21.22 | all-reduce | flops 1280 | bytes 10240 | tf_op jit(solution)/shard_map/psum | solution.py:106
  127.0 6.8 %psum.95 = f32[1280]{0:T(1024)S(1)} all-reduce(f32[1280]{0:T(1024)S(1)} %psum.94), channel_id=1, replica_groups=mesh['z'=4,'xh'=2,'xl'=4,'yh'=2,'ylo'=4,'core'=2] {'ylo'}, use_global_device_ids=true, to_apply=%region_22.23 | all-reduce | flops 1280 | bytes 10240 | tf_op jit(solution)/shard_map/psum | solution.py:106
  134.1 2.0 %fusion.17 = f32[2,2,8,8,256]{4,3,1,0,2:T(8,128)S(1)} fusion(f32[8,384,256]{2,1,0:T(8,128)S(1)} %copy-done.1, f32[2,2,8,8,128]{4,3,0,2,1:T(8,128)S(1)} %get-tuple-element.50, f32[2,2,8,8,128]{4,3,0,2,1:T(8,128)S(1)} %get-tuple-element.51, f32[2,2,8,8,128]{4,3,0,2,1:T(8,128)S(1)} %get-tuple-element.49), kind=kOutput, calls=%fused_computation.11 | convolution fusion | flops 302186496 | bytes 3801088 | tf_op jit(solution)/shard_map/pacjq,cqn->pacjn/dot_general | solution.py:78
  (75 shorter events, 12.4 us)
Async XLA Ops:
  2.5 28.9 %collective-permute-start.1 = (f32[2,2,8,768]{3,2,0,1:T(8,128)S(1)}, f32[2,2,8,768]{3,2,0,1:T(8,128)S(1)}, u32[]{:S(2)}, u32[]{:S(2)}) collective-permute-start(f32[2,2,8,768]{3,2,0,1:T(8,128)S(1)} %pad_maximum_fusion.6), channel_id=1, source_target_pairs={{8,0},{16,8},{24,16},{32,24},{40,32},{48,40},{56,48},{64,56},{72,6... | collective-permute-start | bytes 294920 | tf_op jit(solution)/shard_map/ppermute | solution.py:131
  21.4 14.5 %collective-permute-start = (f32[2,2,8,768]{3,2,0,1:T(8,128)S(1)}, f32[2,2,8,768]{3,2,0,1:T(8,128)S(1)}, u32[]{:S(2)}, u32[]{:S(2)}) collective-permute-start(f32[2,2,8,768]{3,2,0,1:T(8,128)S(1)} %pad_maximum_fusion.5), channel_id=1, source_target_pairs={{0,8},{8,16},{16,24},{24,32},{32,40},{40,48},{48,56},{56,64},{64,7... | collective-permute-start | bytes 294920 | tf_op jit(solution)/shard_map/ppermute | solution.py:130
  31.4 5.6 %copy-start.2 = (f32[2,2,8,768]{3,2,0,1:T(8,128)}, f32[2,2,8,768]{3,2,0,1:T(8,128)S(1)}, u32[]{:S(2)}) copy-start(f32[2,2,8,768]{3,2,0,1:T(8,128)S(1)} %collective-permute-done.1) | copy-start | bytes 294916
  35.9 1.1 copy-start.3
  41.0 14.4 %copy-start = (f32[8,384,256]{2,1,0:T(8,128)S(1)}, f32[8,384,256]{2,1,0:T(8,128)}, u32[]{:S(2)}) copy-start(f32[8,384,256]{2,1,0:T(8,128)} %get-tuple-element.4) | copy-start | bytes 9437188
  55.4 41.8 %slice-start = ((f32[2,2,8,768]{3,2,0,1:T(8,128)}), f32[2,2,8,256]{3,2,0,1:T(8,128)S(1)}, s32[]{:S(2)}) async-start(f32[2,2,8,768]{3,2,0,1:T(8,128)} %copy-done.2), calls=%async_computation | async-start | bytes 65536 | tf_op jit(solution)/shard_map/slice | solution.py:133
  57.7 62.5 %copy-start.1 = (f32[8,384,256]{2,1,0:T(8,128)S(1)}, f32[8,384,256]{2,1,0:T(8,128)}, u32[]{:S(2)}) copy-start(f32[8,384,256]{2,1,0:T(8,128)} %get-tuple-element.5) | copy-start | bytes 9437188

commit v9 on v8

--- a/solution.py
+++ b/solution.py
@@ -148,8 +148,8 @@
     )
     gain = lax.rsqrt(sums[0] / total_len + EPS)
     arrival = (gain * gain * sums[0] + 2.0 * gain * sums[1] + sums[2]) / total_len
+    received = signal * gain[None, None, :, None] + added
     current = current * gain[None, None, :, None] + noise_ext
-    received = current[..., centre]
     rescale = jnp.sqrt(ATT ** (2 * STEPS) / (arrival + EPS))
     current = current * rescale[None, None, :, None]
     for step in range(STEPS):

time: 139 us -> 136 us (0.978)
  other arithmetic: 11.8 us -> 9.79 us
where the time goes in v9:
time: 136 us; the launch traced here: 134 us
  blocking collectives  77.7 us (57%)
  starting transfers between devices  20.9 us (15%)
  matrix products  10.1 us (7%)
  other arithmetic  9.79 us (7%)
  Pallas kernels  5.55 us (4%)
  waiting for transfers between devices  4.55 us (3%)
  local copies, waits for them, and re-layouts  4.17 us (3%)
    psum x8, blocking collectives, psum_chan(): value = lax.psum(value, axis)  53.4 us
    psum x4, blocking collectives, psum_tm(): value = lax.psum(value, axis)  24.3 us
    ppermute x1, starting transfers between devices, on_device(): after = lax.ppermute(leading, TM, down)  18.9 us
    dot_general x4, matrix products, disperse(): jnp.einsum('pacjq,cqn->pacjn', stacked, table, precision=lax.Precision.HI...  10.1 us
    pallas_call x1, Pallas kernels, merged_tables(): pl.pallas_call(toeplitz_kernel, grid=(count // per,), in_specs=[pl.BlockS...  5.55 us
    ppermute x1, waiting for transfers between devices, on_device(): before = lax.ppermute(trailing, TM, up)  4.55 us
  transfers between devices with their start and end apart: 2, of which 1 were waited for; matrix products, arithmetic and copies ran while one was open for 2% of the time, Pallas kernels for 4%

profile of v9, /device:TPU:1, one launch (start us, length us, event | category | flops | bytes accessed | tf_op | source)
XLA Modules:
  0.0 133.9 jit_solution(17069678893347649634)
XLA Ops:
  3.1 18.9 %collective-permute-start.1 = (f32[2,2,8,768]{3,2,0,1:T(8,128)S(1)}, f32[2,2,8,768]{3,2,0,1:T(8,128)S(1)}, u32[]{:S(2)}, u32[]{:S(2)}) collective-permute-start(f32[2,2,8,768]{3,2,0,1:T(8,128)S(1)} %pad_maximum_fusion.6), channel_id=1, source_target_pairs={{8,0},{16,8},{24,16},{32,24},{40,32},{48,40},{56,48},{64,56},{72,6... | collective-permute-start | bytes 294920 | tf_op jit(solution)/shard_map/ppermute | solution.py:131
  22.1 1.9 %collective-permute-start = (f32[2,2,8,768]{3,2,0,1:T(8,128)S(1)}, f32[2,2,8,768]{3,2,0,1:T(8,128)S(1)}, u32[]{:S(2)}, u32[]{:S(2)}) collective-permute-start(f32[2,2,8,768]{3,2,0,1:T(8,128)S(1)} %pad_maximum_fusion.5), channel_id=1, source_target_pairs={{0,8},{8,16},{16,24},{24,32},{32,40},{40,48},{48,56},{56,64},{64,7... | collective-permute-start | bytes 294920 | tf_op jit(solution)/shard_map/ppermute | solution.py:130
  26.5 5.5 %shard_map.50 = (f32[8,384,256]{2,1,0:T(8,128)}, f32[8,384,256]{2,1,0:T(8,128)}) custom-call(f32[8,2,2,512]{3,2,1,0:T(2,128)} %select_maximum_fusion.taps_ref), custom_call_target="tpu_custom_call" | custom-call | tf_op jit(solution)/shard_map/pallas_call | solution.py:64
  32.0 4.5 %collective-permute-done = f32[2,2,8,768]{3,2,0,1:T(8,128)S(1)} collective-permute-done((f32[2,2,8,768]{3,2,0,1:T(8,128)S(1)}, f32[2,2,8,768]{3,2,0,1:T(8,128)S(1)}, u32[]{:S(2)}, u32[]{:S(2)}) %collective-permute-start) | collective-permute-done | bytes 98336 | tf_op jit(solution)/shard_map/ppermute | solution.py:130
  36.6 1.0 pad_maximum_fusion.2
  37.7 3.9 %fusion.8 = f32[2,2,8,14,256]{4,3,1,0,2:T(8,128)S(1)} fusion(f32[8,384,256]{2,1,0:T(8,128)} %get-tuple-element.4, f32[2,2,8,14,128]{4,3,2,1,0:T(8,128)S(1)} %get-tuple-element.59, f32[2,2,8,14,128]{4,3,2,1,0:T(8,128)S(1)} %get-tuple-element.58, f32[2,2,8,14,128]{4,3,2,1,0:T(8,128)S(1)} %get-tuple-element.57), kind=kOutput, calls=%fused_computation.8 | convolution fusion | flops 528826368 | bytes 4292608 | tf_op jit(solution)/shard_map/pacjq,cqn->pacjn/dot_general | solution.py:78
  41.9 3.6 %psum.84 = f32[1792]{0:T(1024)S(1)} all-reduce(f32[1792]{0:T(1024)S(1)} %get-tuple-element.12), channel_id=1, replica_groups=mesh['z'=4,'xh'=2,'xl'=4,'yh'=2,'ylo'=4,'core'=2] {'core'}, use_global_device_ids=true, to_apply=%region_2.3 | all-reduce | flops 1792 | bytes 14336 | tf_op jit(solution)/shard_map/psum | solution.py:106
  45.5 8.7 %psum.85 = f32[1792]{0:T(1024)S(1)} all-reduce(f32[1792]{0:T(1024)S(1)} %psum.84), channel_id=1, replica_groups=mesh['z'=4,'xh'=2,'xl'=4,'yh'=2,'ylo'=4,'core'=2] {'ylo'}, use_global_device_ids=true, to_apply=%region_3.4 | all-reduce | flops 1792 | bytes 14336 | tf_op jit(solution)/shard_map/psum | solution.py:106
  54.7 2.1 %fusion.11 = f32[2,2,8,12,256]{4,3,1,0,2:T(8,128)S(1)} fusion(f32[8,384,256]{2,1,0:T(8,128)S(1)} %copy-done, f32[2,2,8,12,128]{4,3,1,0,2:T(8,128)S(1)} %get-tuple-element.55, f32[2,2,8,12,128]{4,3,1,0,2:T(8,128)S(1)} %get-tuple-element.56, f32[2,2,8,12,128]{4,3,1,0,2:T(8,128)S(1)} %get-tuple-element.54), kind=kOutput, calls=%fused_computation.9 | convolution fusion | flops 453279744 | bytes 4128768 | tf_op jit(solution)/shard_map/pacjq,cqn->pacjn/dot_general | solution.py:78
  57.7 4.6 %psum.86 = f32[1536]{0:T(1024)S(1)} all-reduce(f32[1536]{0:T(1024)S(1)} %get-tuple-element.18), channel_id=1, replica_groups=mesh['z'=4,'xh'=2,'xl'=4,'yh'=2,'ylo'=4,'core'=2] {'core'}, use_global_device_ids=true, to_apply=%region_6.7 | all-reduce | flops 1536 | bytes 12288 | tf_op jit(solution)/shard_map/psum | solution.py:106
  62.3 6.8 %psum.87 = f32[1536]{0:T(1024)S(1)} all-reduce(f32[1536]{0:T(1024)S(1)} %psum.86), channel_id=1, replica_groups=mesh['z'=4,'xh'=2,'xl'=4,'yh'=2,'ylo'=4,'core'=2] {'ylo'}, use_global_device_ids=true, to_apply=%region_7.8 | all-reduce | flops 1536 | bytes 12288 | tf_op jit(solution)/shard_map/psum | solution.py:106
  69.3 1.0 multiply_subtract_fusion
  70.5 7.7 %psum.88 = f32[3,8]{1,0:T(4,128)S(1)} all-reduce(f32[3,8]{1,0:T(4,128)S(1)} %pad_maximum_fusion.7), channel_id=1, replica_groups=mesh['z'=4,'xh'=2,'xl'=4,'yh'=2,'ylo'=4,'core'=2] {'yh'}, use_global_device_ids=true, to_apply=%region_12.13 | all-reduce | flops 24 | bytes 192 | tf_op jit(solution)/shard_map/psum | solution.py:100
  78.2 6.0 %psum.89 = f32[3,8]{1,0:T(4,128)S(1)} all-reduce(f32[3,8]{1,0:T(4,128)S(1)} %psum.88), channel_id=1, replica_groups=mesh['z'=4,'xh'=2,'xl'=4,'yh'=2,'ylo'=4,'core'=2] {'xl'}, use_global_device_ids=true, to_apply=%region_13.14 | all-reduce | flops 24 | bytes 192 | tf_op jit(solution)/shard_map/psum | solution.py:100
  84.1 3.8 %psum.90 = f32[3,8]{1,0:T(4,128)S(1)} all-reduce(f32[3,8]{1,0:T(4,128)S(1)} %psum.89), channel_id=1, replica_groups=mesh['z'=4,'xh'=2,'xl'=4,'yh'=2,'ylo'=4,'core'=2] {'xh'}, use_global_device_ids=true, to_apply=%region_14.15 | all-reduce | flops 24 | bytes 192 | tf_op jit(solution)/shard_map/psum | solution.py:100
  87.9 6.9 %psum.91 = f32[3,8]{1,0:T(4,128)S(1)} all-reduce(f32[3,8]{1,0:T(4,128)S(1)} %psum.90), channel_id=1, replica_groups=mesh['z'=4,'xh'=2,'xl'=4,'yh'=2,'ylo'=4,'core'=2] {'z'}, use_global_device_ids=true, to_apply=%region_15.16 | all-reduce | flops 24 | bytes 192 | tf_op jit(solution)/shard_map/psum | solution.py:100
  95.6 1.7 %multiply_reduce_fusion.3 = (f32[1536]{0:T(1024)S(1)}, f32[8,1536]{1,0:T(8,128)S(1)}, f32[2,2,8,1536]{3,2,0,1:T(8,128)}) fusion(f32[8]{0:T(128)S(1)} %get-tuple-element.78, f32[2,2,8,256]{3,2,0,1:T(8,128)S(1)} %slice-done, f32[2,2,8,1024]{3,2,0,1:T(8,128)} %bitcast.157, f32[2,2,8,256]{3,2,0,1:T(8,128)S(1)} %slice-done.1, f32[8]{0:T(128)S(1)} %get-tuple-element.79, ...), kind=kLoop, calls=%fused_computation.46 | loop fusion | flops 428544 | bytes 645184 | tf_op jit(solution)/shard_map/reduce_sum | solution.py:119
  97.3 10.1 %psum.92 = f32[1536]{0:T(1024)S(1)} all-reduce(f32[1536]{0:T(1024)S(1)} %get-tuple-element.14), channel_id=1, replica_groups=mesh['z'=4,'xh'=2,'xl'=4,'yh'=2,'ylo'=4,'core'=2] {'core'}, use_global_device_ids=true, to_apply=%region_17.18 | all-reduce | flops 1536 | bytes 12288 | tf_op jit(solution)/shard_map/psum | solution.py:106
  107.4 8.4 %psum.93 = f32[1536]{0:T(1024)S(1)} all-reduce(f32[1536]{0:T(1024)S(1)} %psum.92), channel_id=1, replica_groups=mesh['z'=4,'xh'=2,'xl'=4,'yh'=2,'ylo'=4,'core'=2] {'ylo'}, use_global_device_ids=true, to_apply=%region_18.19 | all-reduce | flops 1536 | bytes 12288 | tf_op jit(solution)/shard_map/psum | solution.py:106
  116.0 1.0 subtract_bitcast_fusion.2
  117.1 2.1 %fusion.14 = f32[2,2,8,10,256]{4,3,1,0,2:T(8,128)S(1)} fusion(f32[8,384,256]{2,1,0:T(8,128)S(1)} %copy-done.1, f32[2,2,8,10,128]{4,3,1,0,2:T(8,128)S(1)} %get-tuple-element.52, f32[2,2,8,10,128]{4,3,1,0,2:T(8,128)S(1)} %get-tuple-element.53, f32[2,2,8,10,128]{4,3,1,0,2:T(8,128)S(1)} %get-tuple-element.51), kind=kOutput, calls=%fused_computation.10 | convolution fusion | flops 377733120 | bytes 3964928 | tf_op jit(solution)/shard_map/pacjq,cqn->pacjn/dot_general | solution.py:78
  119.4 4.5 %psum.94 = f32[1280]{0:T(1024)S(1)} all-reduce(f32[1280]{0:T(1024)S(1)} %get-tuple-element.20), channel_id=1, replica_groups=mesh['z'=4,'xh'=2,'xl'=4,'yh'=2,'ylo'=4,'core'=2] {'core'}, use_global_device_ids=true, to_apply=%region_21.22 | all-reduce | flops 1280 | bytes 10240 | tf_op jit(solution)/shard_map/psum | solution.py:106
  124.0 6.8 %psum.95 = f32[1280]{0:T(1024)S(1)} all-reduce(f32[1280]{0:T(1024)S(1)} %psum.94), channel_id=1, replica_groups=mesh['z'=4,'xh'=2,'xl'=4,'yh'=2,'ylo'=4,'core'=2] {'ylo'}, use_global_device_ids=true, to_apply=%region_22.23 | all-reduce | flops 1280 | bytes 10240 | tf_op jit(solution)/shard_map/psum | solution.py:106
  131.1 2.0 %fusion.17 = f32[2,2,8,8,256]{4,3,1,0,2:T(8,128)S(1)} fusion(f32[8,384,256]{2,1,0:T(8,128)S(1)} %copy-done.1, f32[2,2,8,8,128]{4,3,0,2,1:T(8,128)S(1)} %get-tuple-element.49, f32[2,2,8,8,128]{4,3,0,2,1:T(8,128)S(1)} %get-tuple-element.50, f32[2,2,8,8,128]{4,3,0,2,1:T(8,128)S(1)} %get-tuple-element.48), kind=kOutput, calls=%fused_computation.11 | convolution fusion | flops 302186496 | bytes 3801088 | tf_op jit(solution)/shard_map/pacjq,cqn->pacjn/dot_general | solution.py:78
  (80 shorter events, 9.4 us)
Async XLA Ops:
  1.5 0.7 copy-start.3
  3.1 28.9 %collective-permute-start.1 = (f32[2,2,8,768]{3,2,0,1:T(8,128)S(1)}, f32[2,2,8,768]{3,2,0,1:T(8,128)S(1)}, u32[]{:S(2)}, u32[]{:S(2)}) collective-permute-start(f32[2,2,8,768]{3,2,0,1:T(8,128)S(1)} %pad_maximum_fusion.6), channel_id=1, source_target_pairs={{8,0},{16,8},{24,16},{32,24},{40,32},{48,40},{56,48},{64,56},{72,6... | collective-permute-start | bytes 294920 | tf_op jit(solution)/shard_map/ppermute | solution.py:131
  22.1 14.5 %collective-permute-start = (f32[2,2,8,768]{3,2,0,1:T(8,128)S(1)}, f32[2,2,8,768]{3,2,0,1:T(8,128)S(1)}, u32[]{:S(2)}, u32[]{:S(2)}) collective-permute-start(f32[2,2,8,768]{3,2,0,1:T(8,128)S(1)} %pad_maximum_fusion.5), channel_id=1, source_target_pairs={{0,8},{8,16},{16,24},{24,32},{32,40},{40,48},{48,56},{56,64},{64,7... | collective-permute-start | bytes 294920 | tf_op jit(solution)/shard_map/ppermute | solution.py:130
  32.0 5.6 %copy-start.4 = (f32[2,2,8,768]{3,2,0,1:T(8,128)}, f32[2,2,8,768]{3,2,0,1:T(8,128)S(1)}, u32[]{:S(2)}) copy-start(f32[2,2,8,768]{3,2,0,1:T(8,128)S(1)} %collective-permute-done.1) | copy-start | bytes 294916
  36.6 1.1 copy-start.5
  41.6 13.0 %copy-start = (f32[8,384,256]{2,1,0:T(8,128)S(1)}, f32[8,384,256]{2,1,0:T(8,128)}, u32[]{:S(2)}) copy-start(f32[8,384,256]{2,1,0:T(8,128)} %get-tuple-element.4) | copy-start | bytes 9437188
  54.7 15.6 %copy-start.2 = (f32[1,2,2,8,1024]{4,3,2,1,0:T(8,128)S(1)}, f32[1,2,2,8,1024]{4,3,2,1,0:T(8,128)}, u32[]{:S(2)}) copy-start(f32[1,2,2,8,1024]{4,3,2,1,0:T(8,128)} %param.4) | copy-start | bytes 393220
  56.8 38.8 %slice-start = ((f32[2,2,8,768]{3,2,0,1:T(8,128)}), f32[2,2,8,256]{3,2,0,1:T(8,128)S(1)}, s32[]{:S(2)}) async-start(f32[2,2,8,768]{3,2,0,1:T(8,128)} %copy-done.4), calls=%async_computation | async-start | bytes 65536 | tf_op jit(solution)/shard_map/slice | solution.py:133
  56.8 38.8 %slice-start.1 = ((f32[2,2,8,768]{3,2,0,1:T(8,128)}), f32[2,2,8,256]{3,2,0,1:T(8,128)S(1)}, s32[]{:S(2)}) async-start(f32[2,2,8,768]{3,2,0,1:T(8,128)} %copy-done.5), calls=%async_computation.1 | async-start | bytes 65536 | tf_op jit(solution)/shard_map/slice | solution.py:133
  57.0 60.1 %copy-start.1 = (f32[8,384,256]{2,1,0:T(8,128)S(1)}, f32[8,384,256]{2,1,0:T(8,128)}, u32[]{:S(2)}) copy-start(f32[8,384,256]{2,1,0:T(8,128)} %get-tuple-element.5) | copy-start | bytes 9437188

commit v10 on v9

--- a/solution.py
+++ b/solution.py
@@ -129,12 +129,21 @@
     leading = jnp.concatenate([field[..., :field_width], last_noise[..., :noise_width]], axis=3)
     before = lax.ppermute(trailing, TM, up)
     after = lax.ppermute(leading, TM, down)
-    current = jnp.concatenate([before[..., :field_width], field, after[..., :field_width]], axis=3)
     noise_ext = jnp.concatenate([before[..., field_width:], last_noise, after[..., field_width:]], axis=3)
 
+    edge = 2 * reach
+    current = jnp.concatenate(
+        [
+            disperse(jnp.concatenate([before[..., :field_width], field[..., :edge]], axis=3), forward, reach),
+            disperse(field, forward, reach),
+            disperse(jnp.concatenate([field[..., length - edge :], after[..., :field_width]], axis=3), forward, reach),
+        ],
+        axis=3,
+    )
     for step in range(STEPS):
-        current = disperse(current, forward, reach) * ATT
-        current = nonlinear(current, 1.0)
+        if step:
+            current = disperse(current, forward, reach)
+        current = nonlinear(current * ATT, 1.0)
     centre = slice(noise_width, noise_width + length)
     signal, added = current[..., centre], last_noise
     sums = psum_tm(

time: 136 us -> 146 us (1.074)
  local copies, waits for them, and re-layouts: 4.17 us -> 9.46 us
  waiting for transfers between devices: 4.55 us -> 0.01 us
  matrix products: 10.1 us -> 14.1 us
  blocking collectives: 77.7 us -> 81.7 us
    psum x4, blocking collectives: 24.3 us -> 29.4 us  [psum_tm(): value = lax.psum(value, axis)]
    ppermute x1, waiting for transfers between devices: 4.55 us -> 0.01 us  [on_device(): before = lax.ppermute(trailing, TM, up)]
    dot_general x4 -> x6, matrix products: 10.1 us -> 14.1 us  [disperse(): jnp.einsum('pacjq,cqn->pacjn', stacked, table, precision=lax.Precision.HI...]
    another operation x4 -> x12, local copies, waits for them, and re-layouts: 0.12 us -> 2.09 us  [disperse(): jnp.stack([real, imag], axis=1).reshape(pols, parts, chans, blocks * reach)]
    slice x0 -> x3, local copies, waits for them, and re-layouts: none -> 1.7 us  [the longest x1 0.85 us: on_device(): after[..., :field_width]]
  transfers between devices with their start and end apart: 2 -> 2, of which waited for: 1 -> 0; matrix products, arithmetic and copies ran while one was open for 2% -> 7% of each run, Pallas kernels for 4% -> 4%
where the time goes in v10:
time: 146 us; the launch traced here: 144 us
  blocking collectives  81.7 us (56%)
  starting transfers between devices  20.8 us (14%)
  matrix products  14.1 us (10%)
  other arithmetic  10.7 us (7%)
  local copies, waits for them, and re-layouts  9.46 us (6%)
  Pallas kernels  5.55 us (4%)
    psum x8, blocking collectives, psum_chan(): value = lax.psum(value, axis)  52.3 us
    psum x4, blocking collectives, psum_tm(): value = lax.psum(value, axis)  29.4 us
    ppermute x1, starting transfers between devices, on_device(): after = lax.ppermute(leading, TM, down)  18.9 us
    dot_general x6, matrix products, disperse(): jnp.einsum('pacjq,cqn->pacjn', stacked, table, precision=lax.Precision.HI...  14.1 us
    pallas_call x1, Pallas kernels, merged_tables(): pl.pallas_call(toeplitz_kernel, grid=(count // per,), in_specs=[pl.BlockS...  5.55 us
  transfers between devices with their start and end apart: 2, of which 0 were waited for; matrix products, arithmetic and copies ran while one was open for 7% of the time, Pallas kernels for 4%

profile of v10, /device:TPU:1, one launch (start us, length us, event | category | flops | bytes accessed | tf_op | source)
XLA Modules:
  0.0 143.6 jit_solution(3613139502793404854)
XLA Ops:
  2.9 18.9 %collective-permute-start.1 = (f32[2,2,8,768]{3,2,1,0:T(8,128)}, f32[2,2,8,768]{3,2,1,0:T(8,128)}, u32[]{:S(2)}, u32[]{:S(2)}) collective-permute-start(f32[2,2,8,768]{3,2,1,0:T(8,128)} %pad_maximum_fusion.5), channel_id=1, source_target_pairs={{8,0},{16,8},{24,16},{32,24},{40,32},{48,40},{56,48},{64,56},{72,6... | collective-permute-start | bytes 294920 | tf_op jit(solution)/shard_map/ppermute | solution.py:131
  22.5 1.9 %collective-permute-start = (f32[2,2,8,768]{3,2,1,0:T(8,128)}, f32[2,2,8,768]{3,2,1,0:T(8,128)}, u32[]{:S(2)}, u32[]{:S(2)}) collective-permute-start(f32[2,2,8,768]{3,2,1,0:T(8,128)} %pad_maximum_fusion.4), channel_id=1, source_target_pairs={{0,8},{8,16},{16,24},{24,32},{32,40},{40,48},{48,56},{56,64},{64,7... | collective-permute-start | bytes 294920 | tf_op jit(solution)/shard_map/ppermute | solution.py:130
  25.3 0.9 copy.149
  28.5 5.5 %shard_map.50 = (f32[8,384,256]{2,1,0:T(8,128)}, f32[8,384,256]{2,1,0:T(8,128)}) custom-call(f32[8,2,2,512]{3,2,1,0:T(2,128)} %select_maximum_fusion.taps_ref), custom_call_target="tpu_custom_call" | custom-call | tf_op jit(solution)/shard_map/pallas_call | solution.py:64
  34.1 4.0 %fusion.18 = f32[2,2,8,6,256]{4,3,1,0,2:T(8,128)S(1)} fusion(f32[8,384,256]{2,1,0:T(8,128)} %get-tuple-element.4, f32[2,2,8,6,128]{4,3,2,1,0:T(8,128)} %get-tuple-element.65, f32[2,2,8,6,128]{4,3,2,1,0:T(8,128)S(1)} %get-tuple-element.64, f32[2,2,8,6,128]{4,3,2,1,0:T(8,128)S(1)} %get-tuple-element.63), kind=kOutput, calls=%fused_computation.14 | convolution fusion | flops 226639872 | bytes 3637248 | tf_op jit(solution)/shard_map/pacjq,cqn->pacjn/dot_general | solution.py:78
  40.1 2.0 %fusion.24 = f32[2,2,8,4,256]{4,3,1,0,2:T(4,128)S(1)} fusion(f32[8,384,256]{2,1,0:T(8,128)S(1)} %copy-done, f32[2,2,8,4,128]{4,3,1,0,2:T(4,128)S(1)} %copy.134, f32[2,2,8,4,128]{4,3,1,0,2:T(4,128)S(1)} %copy.133, f32[2,2,8,4,128]{4,3,1,0,2:T(4,128)S(1)} %copy.132), kind=kOutput, calls=%fused_computation.16 | convolution fusion | flops 151093248 | bytes 3473408 | tf_op jit(solution)/shard_map/pacjq,cqn->pacjn/dot_general | solution.py:78
  42.8 2.0 %fusion.27 = f32[2,2,8,4,256]{4,3,1,0,2:T(4,128)S(1)} fusion(f32[8,384,256]{2,1,0:T(8,128)S(1)} %copy-done, f32[2,2,8,4,128]{4,3,1,0,2:T(4,128)S(1)} %copy.142, f32[2,2,8,4,128]{4,3,1,0,2:T(4,128)S(1)} %copy.141, f32[2,2,8,4,128]{4,3,1,0,2:T(4,128)S(1)} %copy.140), kind=kOutput, calls=%fused_computation.17 | convolution fusion | flops 151093248 | bytes 3473408 | tf_op jit(solution)/shard_map/pacjq,cqn->pacjn/dot_general | solution.py:78
  47.1 3.1 %psum.84 = f32[1792]{0:T(1024)S(1)} all-reduce(f32[1792]{0:T(1024)S(1)} %get-tuple-element.6), channel_id=1, replica_groups=mesh['z'=4,'xh'=2,'xl'=4,'yh'=2,'ylo'=4,'core'=2] {'core'}, use_global_device_ids=true, to_apply=%region_2.3 | all-reduce | flops 1792 | bytes 14336 | tf_op jit(solution)/shard_map/psum | solution.py:106
  50.2 7.4 %psum.85 = f32[1792]{0:T(1024)S(1)} all-reduce(f32[1792]{0:T(1024)S(1)} %psum.84), channel_id=1, replica_groups=mesh['z'=4,'xh'=2,'xl'=4,'yh'=2,'ylo'=4,'core'=2] {'ylo'}, use_global_device_ids=true, to_apply=%region_3.4 | all-reduce | flops 1792 | bytes 14336 | tf_op jit(solution)/shard_map/psum | solution.py:106
  58.0 2.1 %fusion.12 = f32[2,2,8,12,256]{4,3,1,0,2:T(8,128)S(1)} fusion(f32[8,384,256]{2,1,0:T(8,128)S(1)} %copy-done, f32[2,2,8,12,128]{4,3,1,0,2:T(8,128)S(1)} %get-tuple-element.46, f32[2,2,8,12,128]{4,3,1,0,2:T(8,128)S(1)} %get-tuple-element.47, f32[2,2,8,12,128]{4,3,1,0,2:T(8,128)S(1)} %get-tuple-element.45), kind=kOutput, calls=%fused_computation.12 | convolution fusion | flops 453279744 | bytes 4128768 | tf_op jit(solution)/shard_map/pacjq,cqn->pacjn/dot_general | solution.py:78
  61.0 4.6 %psum.86 = f32[1536]{0:T(1024)S(1)} all-reduce(f32[1536]{0:T(1024)S(1)} %get-tuple-element.12), channel_id=1, replica_groups=mesh['z'=4,'xh'=2,'xl'=4,'yh'=2,'ylo'=4,'core'=2] {'core'}, use_global_device_ids=true, to_apply=%region_6.7 | all-reduce | flops 1536 | bytes 12288 | tf_op jit(solution)/shard_map/psum | solution.py:106
  65.6 7.6 %psum.87 = f32[1536]{0:T(1024)S(1)} all-reduce(f32[1536]{0:T(1024)S(1)} %psum.86), channel_id=1, replica_groups=mesh['z'=4,'xh'=2,'xl'=4,'yh'=2,'ylo'=4,'core'=2] {'ylo'}, use_global_device_ids=true, to_apply=%region_7.8 | all-reduce | flops 1536 | bytes 12288 | tf_op jit(solution)/shard_map/psum | solution.py:106
  73.4 1.0 multiply_subtract_fusion
  74.6 7.7 %psum.88 = f32[3,8]{1,0:T(4,128)S(1)} all-reduce(f32[3,8]{1,0:T(4,128)S(1)} %pad_maximum_fusion.6), channel_id=1, replica_groups=mesh['z'=4,'xh'=2,'xl'=4,'yh'=2,'ylo'=4,'core'=2] {'yh'}, use_global_device_ids=true, to_apply=%region_12.13 | all-reduce | flops 24 | bytes 192 | tf_op jit(solution)/shard_map/psum | solution.py:100
  82.3 6.0 %psum.89 = f32[3,8]{1,0:T(4,128)S(1)} all-reduce(f32[3,8]{1,0:T(4,128)S(1)} %psum.88), channel_id=1, replica_groups=mesh['z'=4,'xh'=2,'xl'=4,'yh'=2,'ylo'=4,'core'=2] {'xl'}, use_global_device_ids=true, to_apply=%region_13.14 | all-reduce | flops 24 | bytes 192 | tf_op jit(solution)/shard_map/psum | solution.py:100
  88.3 3.8 %psum.90 = f32[3,8]{1,0:T(4,128)S(1)} all-reduce(f32[3,8]{1,0:T(4,128)S(1)} %psum.89), channel_id=1, replica_groups=mesh['z'=4,'xh'=2,'xl'=4,'yh'=2,'ylo'=4,'core'=2] {'xh'}, use_global_device_ids=true, to_apply=%region_14.15 | all-reduce | flops 24 | bytes 192 | tf_op jit(solution)/shard_map/psum | solution.py:100
  92.0 12.0 %psum.91 = f32[3,8]{1,0:T(4,128)S(1)} all-reduce(f32[3,8]{1,0:T(4,128)S(1)} %psum.90), channel_id=1, replica_groups=mesh['z'=4,'xh'=2,'xl'=4,'yh'=2,'ylo'=4,'core'=2] {'z'}, use_global_device_ids=true, to_apply=%region_15.16 | all-reduce | flops 24 | bytes 192 | tf_op jit(solution)/shard_map/psum | solution.py:100
  107.1 10.1 %psum.92 = f32[1536]{0:T(1024)S(1)} all-reduce(f32[1536]{0:T(1024)S(1)} %get-tuple-element.8), channel_id=1, replica_groups=mesh['z'=4,'xh'=2,'xl'=4,'yh'=2,'ylo'=4,'core'=2] {'core'}, use_global_device_ids=true, to_apply=%region_17.18 | all-reduce | flops 1536 | bytes 12288 | tf_op jit(solution)/shard_map/psum | solution.py:106
  117.2 7.4 %psum.93 = f32[1536]{0:T(1024)S(1)} all-reduce(f32[1536]{0:T(1024)S(1)} %psum.92), channel_id=1, replica_groups=mesh['z'=4,'xh'=2,'xl'=4,'yh'=2,'ylo'=4,'core'=2] {'ylo'}, use_global_device_ids=true, to_apply=%region_18.19 | all-reduce | flops 1536 | bytes 12288 | tf_op jit(solution)/shard_map/psum | solution.py:106
  124.8 1.0 subtract_bitcast_fusion.2
  125.9 2.1 %fusion.15 = f32[2,2,8,10,256]{4,3,1,0,2:T(8,128)S(1)} fusion(f32[8,384,256]{2,1,0:T(8,128)S(1)} %copy-done.1, f32[2,2,8,10,128]{4,3,1,0,2:T(8,128)S(1)} %get-tuple-element.43, f32[2,2,8,10,128]{4,3,1,0,2:T(8,128)S(1)} %get-tuple-element.44, f32[2,2,8,10,128]{4,3,1,0,2:T(8,128)S(1)} %get-tuple-element.42), kind=kOutput, calls=%fused_computation.13 | convolution fusion | flops 377733120 | bytes 3964928 | tf_op jit(solution)/shard_map/pacjq,cqn->pacjn/dot_general | solution.py:78
  128.2 4.5 %psum.94 = f32[1280]{0:T(1024)S(1)} all-reduce(f32[1280]{0:T(1024)S(1)} %get-tuple-element.14), channel_id=1, replica_groups=mesh['z'=4,'xh'=2,'xl'=4,'yh'=2,'ylo'=4,'core'=2] {'core'}, use_global_device_ids=true, to_apply=%region_21.22 | all-reduce | flops 1280 | bytes 10240 | tf_op jit(solution)/shard_map/psum | solution.py:106
  132.8 7.6 %psum.95 = f32[1280]{0:T(1024)S(1)} all-reduce(f32[1280]{0:T(1024)S(1)} %psum.94), channel_id=1, replica_groups=mesh['z'=4,'xh'=2,'xl'=4,'yh'=2,'ylo'=4,'core'=2] {'ylo'}, use_global_device_ids=true, to_apply=%region_22.23 | all-reduce | flops 1280 | bytes 10240 | tf_op jit(solution)/shard_map/psum | solution.py:106
  140.7 2.0 %fusion.21 = f32[2,2,8,8,256]{4,3,1,0,2:T(8,128)S(1)} fusion(f32[8,384,256]{2,1,0:T(8,128)S(1)} %copy-done.1, f32[2,2,8,8,128]{4,3,0,2,1:T(8,128)S(1)} %get-tuple-element.40, f32[2,2,8,8,128]{4,3,0,2,1:T(8,128)S(1)} %get-tuple-element.41, f32[2,2,8,8,128]{4,3,0,2,1:T(8,128)S(1)} %get-tuple-element.39), kind=kOutput, calls=%fused_computation.15 | convolution fusion | flops 302186496 | bytes 3801088 | tf_op jit(solution)/shard_map/pacjq,cqn->pacjn/dot_general | solution.py:78
  (97 shorter events, 17.3 us)
Async XLA Ops:
  2.9 35.3 %collective-permute-start.1 = (f32[2,2,8,768]{3,2,1,0:T(8,128)}, f32[2,2,8,768]{3,2,1,0:T(8,128)}, u32[]{:S(2)}, u32[]{:S(2)}) collective-permute-start(f32[2,2,8,768]{3,2,1,0:T(8,128)} %pad_maximum_fusion.5), channel_id=1, source_target_pairs={{8,0},{16,8},{24,16},{32,24},{40,32},{48,40},{56,48},{64,56},{72,6... | collective-permute-start | bytes 294920 | tf_op jit(solution)/shard_map/ppermute | solution.py:131
  21.9 16.3 %copy-start.3 = (f32[2,2,8,1024]{3,2,1,0:T(8,128)S(1)}, f32[2,2,8,1024]{3,2,1,0:T(8,128)}, u32[]{:S(2)}) copy-start(f32[2,2,8,1024]{3,2,1,0:T(8,128)} %param.3) | copy-start | bytes 393220
  22.5 16.5 %collective-permute-start = (f32[2,2,8,768]{3,2,1,0:T(8,128)}, f32[2,2,8,768]{3,2,1,0:T(8,128)}, u32[]{:S(2)}, u32[]{:S(2)}) collective-permute-start(f32[2,2,8,768]{3,2,1,0:T(8,128)} %pad_maximum_fusion.4), channel_id=1, source_target_pairs={{0,8},{8,16},{16,24},{24,32},{32,40},{40,48},{48,56},{56,64},{64,7... | collective-permute-start | bytes 294920 | tf_op jit(solution)/shard_map/ppermute | solution.py:130
  34.1 6.1 %copy-start = (f32[8,384,256]{2,1,0:T(8,128)S(1)}, f32[8,384,256]{2,1,0:T(8,128)}, u32[]{:S(2)}) copy-start(f32[8,384,256]{2,1,0:T(8,128)} %get-tuple-element.4) | copy-start | bytes 9437188
  58.0 16.4 %copy-start.2 = (f32[1,2,2,8,1024]{4,3,2,1,0:T(8,128)S(1)}, f32[1,2,2,8,1024]{4,3,2,1,0:T(8,128)}, u32[]{:S(2)}) copy-start(f32[1,2,2,8,1024]{4,3,2,1,0:T(8,128)} %param.4) | copy-start | bytes 393220
  60.2 65.7 %copy-start.1 = (f32[8,384,256]{2,1,0:T(8,128)S(1)}, f32[8,384,256]{2,1,0:T(8,128)}, u32[]{:S(2)}) copy-start(f32[8,384,256]{2,1,0:T(8,128)} %get-tuple-element.5) | copy-start | bytes 9437188

commit v11 on v9

--- a/solution.py
+++ b/solution.py
@@ -123,10 +123,12 @@
     count, length = lax.axis_size(TM), field.shape[3]
     up = [(i, (i + 1) % count) for i in range(count)]
     down = [(j, i) for i, j in up]
+    halo_noise = last_noise
+    last_noise = lax.optimization_barrier(last_noise)
     trailing = jnp.concatenate(
-        [field[..., length - field_width :], last_noise[..., length - noise_width :]], axis=3
+        [field[..., length - field_width :], halo_noise[..., length - noise_width :]], axis=3
     )
-    leading = jnp.concatenate([field[..., :field_width], last_noise[..., :noise_width]], axis=3)
+    leading = jnp.concatenate([field[..., :field_width], halo_noise[..., :noise_width]], axis=3)
     before = lax.ppermute(trailing, TM, up)
     after = lax.ppermute(leading, TM, down)
     current = jnp.concatenate([before[..., :field_width], field, after[..., :field_width]], axis=3)

time: 136 us -> 139 us (1.022)
  other arithmetic: 9.79 us -> 11.6 us
where the time goes in v11:
time: 139 us; the launch traced here: 137 us
  blocking collectives  77.8 us (56%)
  starting transfers between devices  20.9 us (15%)
  other arithmetic  11.6 us (8%)
  matrix products  10.1 us (7%)
  Pallas kernels  5.55 us (4%)
  local copies, waits for them, and re-layouts  5.18 us (4%)
  waiting for transfers between devices  4.55 us (3%)
    psum x8, blocking collectives, psum_chan(): value = lax.psum(value, axis)  53.5 us
    psum x4, blocking collectives, psum_tm(): value = lax.psum(value, axis)  24.3 us
    ppermute x1, starting transfers between devices, on_device(): after = lax.ppermute(leading, TM, down)  18.9 us
    dot_general x4, matrix products, disperse(): jnp.einsum('pacjq,cqn->pacjn', stacked, table, precision=lax.Precision.HI...  10.1 us
    pallas_call x1, Pallas kernels, merged_tables(): pl.pallas_call(toeplitz_kernel, grid=(count // per,), in_specs=[pl.BlockS...  5.55 us
    ppermute x1, waiting for transfers between devices, on_device(): before = lax.ppermute(trailing, TM, up)  4.55 us
  transfers between devices with their start and end apart: 2, of which 1 were waited for; matrix products, arithmetic and copies ran while one was open for 2% of the time, Pallas kernels for 4%

profile of v11, /device:TPU:1, one launch (start us, length us, event | category | flops | bytes accessed | tf_op | source)
XLA Modules:
  0.0 136.8 jit_solution(9650563096480253693)
XLA Ops:
  2.5 18.9 %collective-permute-start.1 = (f32[2,2,8,768]{3,2,0,1:T(8,128)S(1)}, f32[2,2,8,768]{3,2,0,1:T(8,128)S(1)}, u32[]{:S(2)}, u32[]{:S(2)}) collective-permute-start(f32[2,2,8,768]{3,2,0,1:T(8,128)S(1)} %pad_maximum_fusion.6), channel_id=1, source_target_pairs={{8,0},{16,8},{24,16},{32,24},{40,32},{48,40},{56,48},{64,56},{72,6... | collective-permute-start | bytes 294920 | tf_op jit(solution)/shard_map/ppermute | solution.py:133
  21.4 1.9 %collective-permute-start = (f32[2,2,8,768]{3,2,0,1:T(8,128)S(1)}, f32[2,2,8,768]{3,2,0,1:T(8,128)S(1)}, u32[]{:S(2)}, u32[]{:S(2)}) collective-permute-start(f32[2,2,8,768]{3,2,0,1:T(8,128)S(1)} %pad_maximum_fusion.5), channel_id=1, source_target_pairs={{0,8},{8,16},{16,24},{24,32},{32,40},{40,48},{48,56},{56,64},{64,7... | collective-permute-start | bytes 294920 | tf_op jit(solution)/shard_map/ppermute | solution.py:132
  25.8 5.5 %shard_map.50 = (f32[8,384,256]{2,1,0:T(8,128)}, f32[8,384,256]{2,1,0:T(8,128)}) custom-call(f32[8,2,2,512]{3,2,1,0:T(2,128)} %select_maximum_fusion.taps_ref), custom_call_target="tpu_custom_call" | custom-call | tf_op jit(solution)/shard_map/pallas_call | solution.py:64
  31.4 4.5 %collective-permute-done = f32[2,2,8,768]{3,2,0,1:T(8,128)S(1)} collective-permute-done((f32[2,2,8,768]{3,2,0,1:T(8,128)S(1)}, f32[2,2,8,768]{3,2,0,1:T(8,128)S(1)}, u32[]{:S(2)}, u32[]{:S(2)}) %collective-permute-start) | collective-permute-done | bytes 98336 | tf_op jit(solution)/shard_map/ppermute | solution.py:132
  37.0 3.9 %fusion.8 = f32[2,2,8,14,256]{4,3,1,0,2:T(8,128)S(1)} fusion(f32[8,384,256]{2,1,0:T(8,128)} %get-tuple-element.4, f32[2,2,8,14,128]{4,3,2,1,0:T(8,128)S(1)} %get-tuple-element.59, f32[2,2,8,14,128]{4,3,2,1,0:T(8,128)S(1)} %get-tuple-element.58, f32[2,2,8,14,128]{4,3,2,1,0:T(8,128)S(1)} %get-tuple-element.57), kind=kOutput, calls=%fused_computation.8 | convolution fusion | flops 528826368 | bytes 4292608 | tf_op jit(solution)/shard_map/pacjq,cqn->pacjn/dot_general | solution.py:78
  41.9 3.5 %psum.84 = f32[1792]{0:T(1024)S(1)} all-reduce(f32[1792]{0:T(1024)S(1)} %get-tuple-element.12), channel_id=1, replica_groups=mesh['z'=4,'xh'=2,'xl'=4,'yh'=2,'ylo'=4,'core'=2] {'core'}, use_global_device_ids=true, to_apply=%region_2.3 | all-reduce | flops 1792 | bytes 14336 | tf_op jit(solution)/shard_map/psum | solution.py:106
  45.4 8.7 %psum.85 = f32[1792]{0:T(1024)S(1)} all-reduce(f32[1792]{0:T(1024)S(1)} %psum.84), channel_id=1, replica_groups=mesh['z'=4,'xh'=2,'xl'=4,'yh'=2,'ylo'=4,'core'=2] {'ylo'}, use_global_device_ids=true, to_apply=%region_3.4 | all-reduce | flops 1792 | bytes 14336 | tf_op jit(solution)/shard_map/psum | solution.py:106
  54.2 1.0 fusion.39
  55.4 2.1 %fusion.11 = f32[2,2,8,12,256]{4,3,1,0,2:T(8,128)S(1)} fusion(f32[8,384,256]{2,1,0:T(8,128)S(1)} %copy-done, f32[2,2,8,12,128]{4,3,1,0,2:T(8,128)S(1)} %get-tuple-element.55, f32[2,2,8,12,128]{4,3,1,0,2:T(8,128)S(1)} %get-tuple-element.56, f32[2,2,8,12,128]{4,3,1,0,2:T(8,128)S(1)} %get-tuple-element.54), kind=kOutput, calls=%fused_computation.9 | convolution fusion | flops 453279744 | bytes 4128768 | tf_op jit(solution)/shard_map/pacjq,cqn->pacjn/dot_general | solution.py:78
  58.4 4.6 %psum.86 = f32[1536]{0:T(1024)S(1)} all-reduce(f32[1536]{0:T(1024)S(1)} %get-tuple-element.18), channel_id=1, replica_groups=mesh['z'=4,'xh'=2,'xl'=4,'yh'=2,'ylo'=4,'core'=2] {'core'}, use_global_device_ids=true, to_apply=%region_6.7 | all-reduce | flops 1536 | bytes 12288 | tf_op jit(solution)/shard_map/psum | solution.py:106
  63.0 6.8 %psum.87 = f32[1536]{0:T(1024)S(1)} all-reduce(f32[1536]{0:T(1024)S(1)} %psum.86), channel_id=1, replica_groups=mesh['z'=4,'xh'=2,'xl'=4,'yh'=2,'ylo'=4,'core'=2] {'ylo'}, use_global_device_ids=true, to_apply=%region_7.8 | all-reduce | flops 1536 | bytes 12288 | tf_op jit(solution)/shard_map/psum | solution.py:106
  71.2 7.7 %psum.88 = f32[3,8]{1,0:T(4,128)S(1)} all-reduce(f32[3,8]{1,0:T(4,128)S(1)} %pad_maximum_fusion.7), channel_id=1, replica_groups=mesh['z'=4,'xh'=2,'xl'=4,'yh'=2,'ylo'=4,'core'=2] {'yh'}, use_global_device_ids=true, to_apply=%region_12.13 | all-reduce | flops 24 | bytes 192 | tf_op jit(solution)/shard_map/psum | solution.py:100
  78.9 6.0 %psum.89 = f32[3,8]{1,0:T(4,128)S(1)} all-reduce(f32[3,8]{1,0:T(4,128)S(1)} %psum.88), channel_id=1, replica_groups=mesh['z'=4,'xh'=2,'xl'=4,'yh'=2,'ylo'=4,'core'=2] {'xl'}, use_global_device_ids=true, to_apply=%region_13.14 | all-reduce | flops 24 | bytes 192 | tf_op jit(solution)/shard_map/psum | solution.py:100
  84.8 3.8 %psum.90 = f32[3,8]{1,0:T(4,128)S(1)} all-reduce(f32[3,8]{1,0:T(4,128)S(1)} %psum.89), channel_id=1, replica_groups=mesh['z'=4,'xh'=2,'xl'=4,'yh'=2,'ylo'=4,'core'=2] {'xh'}, use_global_device_ids=true, to_apply=%region_14.15 | all-reduce | flops 24 | bytes 192 | tf_op jit(solution)/shard_map/psum | solution.py:100
  88.6 6.9 %psum.91 = f32[3,8]{1,0:T(4,128)S(1)} all-reduce(f32[3,8]{1,0:T(4,128)S(1)} %psum.90), channel_id=1, replica_groups=mesh['z'=4,'xh'=2,'xl'=4,'yh'=2,'ylo'=4,'core'=2] {'z'}, use_global_device_ids=true, to_apply=%region_15.16 | all-reduce | flops 24 | bytes 192 | tf_op jit(solution)/shard_map/psum | solution.py:100
  97.0 1.4 %multiply_reduce_fusion.3 = (f32[1536]{0:T(1024)}, f32[8,1536]{1,0:T(8,128)S(1)}, f32[2,2,8,1536]{3,2,0,1:T(8,128)}) fusion(f32[8]{0:T(128)S(1)} %get-tuple-element.78, f32[2,2,8,256]{3,2,0,1:T(8,128)S(1)} %slice-done, f32[2,2,8,1024]{3,2,0,1:T(8,128)S(1)} %bitcast.152, f32[2,2,8,256]{3,2,0,1:T(8,128)S(1)} %slice.247, f32[8]{0:T(128)S(1)} %get-tuple-element.79, ...), kind=kLoop, calls=%fused_computation.46 | loop fusion | flops 428544 | bytes 645184 | tf_op jit(solution)/shard_map/reduce_sum | solution.py:119
  98.4 10.2 %psum.92 = f32[1536]{0:T(1024)S(1)} all-reduce(f32[1536]{0:T(1024)} %get-tuple-element.14), channel_id=1, replica_groups=mesh['z'=4,'xh'=2,'xl'=4,'yh'=2,'ylo'=4,'core'=2] {'core'}, use_global_device_ids=true, to_apply=%region_17.18 | all-reduce | flops 1536 | bytes 12288 | tf_op jit(solution)/shard_map/psum | solution.py:106
  108.6 8.4 %psum.93 = f32[1536]{0:T(1024)S(1)} all-reduce(f32[1536]{0:T(1024)S(1)} %psum.92), channel_id=1, replica_groups=mesh['z'=4,'xh'=2,'xl'=4,'yh'=2,'ylo'=4,'core'=2] {'ylo'}, use_global_device_ids=true, to_apply=%region_18.19 | all-reduce | flops 1536 | bytes 12288 | tf_op jit(solution)/shard_map/psum | solution.py:106
  117.0 1.6 %copy.100 = f32[2,2,8,1024]{3,2,1,0:T(8,128)} copy(f32[2,2,8,1024]{3,2,0,1:T(8,128)} %multiply_add_fusion) | data formatting | bytes 262144
  118.8 1.0 subtract_bitcast_fusion.2
  119.9 2.1 %fusion.14 = f32[2,2,8,10,256]{4,3,1,0,2:T(8,128)S(1)} fusion(f32[8,384,256]{2,1,0:T(8,128)S(1)} %copy-done.1, f32[2,2,8,10,128]{4,3,1,0,2:T(8,128)S(1)} %get-tuple-element.52, f32[2,2,8,10,128]{4,3,1,0,2:T(8,128)S(1)} %get-tuple-element.53, f32[2,2,8,10,128]{4,3,1,0,2:T(8,128)S(1)} %get-tuple-element.51), kind=kOutput, calls=%fused_computation.10 | convolution fusion | flops 377733120 | bytes 3964928 | tf_op jit(solution)/shard_map/pacjq,cqn->pacjn/dot_general | solution.py:78
  122.3 4.5 %psum.94 = f32[1280]{0:T(1024)S(1)} all-reduce(f32[1280]{0:T(1024)S(1)} %get-tuple-element.20), channel_id=1, replica_groups=mesh['z'=4,'xh'=2,'xl'=4,'yh'=2,'ylo'=4,'core'=2] {'core'}, use_global_device_ids=true, to_apply=%region_21.22 | all-reduce | flops 1280 | bytes 10240 | tf_op jit(solution)/shard_map/psum | solution.py:106
  126.8 6.8 %psum.95 = f32[1280]{0:T(1024)S(1)} all-reduce(f32[1280]{0:T(1024)S(1)} %psum.94), channel_id=1, replica_groups=mesh['z'=4,'xh'=2,'xl'=4,'yh'=2,'ylo'=4,'core'=2] {'ylo'}, use_global_device_ids=true, to_apply=%region_22.23 | all-reduce | flops 1280 | bytes 10240 | tf_op jit(solution)/shard_map/psum | solution.py:106
  133.9 2.0 %fusion.17 = f32[2,2,8,8,256]{4,3,1,0,2:T(8,128)S(1)} fusion(f32[8,384,256]{2,1,0:T(8,128)S(1)} %copy-done.1, f32[2,2,8,8,128]{4,3,0,2,1:T(8,128)S(1)} %get-tuple-element.49, f32[2,2,8,8,128]{4,3,0,2,1:T(8,128)S(1)} %get-tuple-element.50, f32[2,2,8,8,128]{4,3,0,2,1:T(8,128)S(1)} %get-tuple-element.48), kind=kOutput, calls=%fused_computation.11 | convolution fusion | flops 302186496 | bytes 3801088 | tf_op jit(solution)/shard_map/pacjq,cqn->pacjn/dot_general | solution.py:78
  (75 shorter events, 11.8 us)
Async XLA Ops:
  2.5 28.9 %collective-permute-start.1 = (f32[2,2,8,768]{3,2,0,1:T(8,128)S(1)}, f32[2,2,8,768]{3,2,0,1:T(8,128)S(1)}, u32[]{:S(2)}, u32[]{:S(2)}) collective-permute-start(f32[2,2,8,768]{3,2,0,1:T(8,128)S(1)} %pad_maximum_fusion.6), channel_id=1, source_target_pairs={{8,0},{16,8},{24,16},{32,24},{40,32},{48,40},{56,48},{64,56},{72,6... | collective-permute-start | bytes 294920 | tf_op jit(solution)/shard_map/ppermute | solution.py:133
  21.4 14.5 %collective-permute-start = (f32[2,2,8,768]{3,2,0,1:T(8,128)S(1)}, f32[2,2,8,768]{3,2,0,1:T(8,128)S(1)}, u32[]{:S(2)}, u32[]{:S(2)}) collective-permute-start(f32[2,2,8,768]{3,2,0,1:T(8,128)S(1)} %pad_maximum_fusion.5), channel_id=1, source_target_pairs={{0,8},{8,16},{16,24},{24,32},{32,40},{40,48},{48,56},{56,64},{64,7... | collective-permute-start | bytes 294920 | tf_op jit(solution)/shard_map/ppermute | solution.py:132
  31.4 5.6 %copy-start.2 = (f32[2,2,8,768]{3,2,0,1:T(8,128)}, f32[2,2,8,768]{3,2,0,1:T(8,128)S(1)}, u32[]{:S(2)}) copy-start(f32[2,2,8,768]{3,2,0,1:T(8,128)S(1)} %collective-permute-done.1) | copy-start | bytes 294916
  35.9 1.1 copy-start.3
  41.0 14.4 %copy-start = (f32[8,384,256]{2,1,0:T(8,128)S(1)}, f32[8,384,256]{2,1,0:T(8,128)}, u32[]{:S(2)}) copy-start(f32[8,384,256]{2,1,0:T(8,128)} %get-tuple-element.4) | copy-start | bytes 9437188
  57.5 39.5 %slice-start = ((f32[2,2,8,768]{3,2,0,1:T(8,128)}), f32[2,2,8,256]{3,2,0,1:T(8,128)S(1)}, s32[]{:S(2)}) async-start(f32[2,2,8,768]{3,2,0,1:T(8,128)} %copy-done.2), calls=%async_computation | async-start | bytes 65536 | tf_op jit(solution)/shard_map/slice | solution.py:135
  57.7 62.2 %copy-start.1 = (f32[8,384,256]{2,1,0:T(8,128)S(1)}, f32[8,384,256]{2,1,0:T(8,128)}, u32[]{:S(2)}) copy-start(f32[8,384,256]{2,1,0:T(8,128)} %get-tuple-element.5) | copy-start | bytes 9437188
